TPU v7x, 256 devices: a whole 4x4x8 slice. The times are simulated.
256 devices in a mesh: dp: 4 (over y), section: 16 (over z, x_lo), tensor: 4 (over x_hi, core).
Axes of the slice: x: 4 (x_hi: 2, x_lo: 2; x = x_hi * 2 + x_lo), y: 4, z: 8, core: 2. Of those that a mesh axis runs over, the one named last changes fastest.
Arguments:
- saved_input: bfloat16 [16, 2, 512, 8192], P('section', None, ('dp', 'tensor')), may hold values from -6 to 6
- kv_grad: bfloat16 [16, 2, 512, 2048], P('section', None, 'dp', 'tensor'), may hold values from -1.5 to 1.5
- kv_weight: bfloat16 [16, 8192, 2048], P('section', 'dp', 'tensor'), may hold values from -0.0625 to 0.0625
- norm_gain: bfloat16 [16, 8192], P('section'), may hold values from 0.5 to 1.5
- top_grad: bfloat16 [2, 512, 8192], P(None, ('dp', 'tensor')), may hold values from -1.5 to 1.5
- noise_salt: int32 [1], replicated, may hold values from 0 to 1073741823
- step_counter: int32 [1], replicated, may hold values from 0 to 999999
Outputs:
- input_grads: bfloat16 [16, 2, 512, 8192], P('section', None, ('dp', 'tensor'))
- weight_grads: float32 [16, 8192, 2048], P('section', 'dp', 'tensor')
All inputs are finite; a program needn't handle non-finite values.
Results may differ from a plain program's by a relative error of at most 0.012.
Values may be sent and summed in bfloat16 or wider, within the bound.
No kernel may reach another device: no remote copies, remote signals or barrier semaphores. Data moves between devices by JAX's collectives and lax.ppermute only.
A program may use at most 128 MiB of HBM per device.

v0:
```python
import jax
import jax.numpy as jnp
from jax import lax
from jax.sharding import PartitionSpec as P


def entering(shard, axis, join, neutral):
    count = lax.axis_size(axis)
    place = lax.axis_index(axis)
    ahead = count - 1 - place
    gathered = lax.all_gather(shard.astype(jnp.bfloat16), axis)
    state = jnp.zeros_like(shard) + jnp.asarray(neutral, shard.dtype)

    def one(lap, state):
        source = count - 1 - lap
        return join(state, lax.dynamic_index_in_dim(gathered, source, 0, False).astype(shard.dtype))

    return lax.fori_loop(0, ahead, one, state)


def mix_bits(salt, counter, layer, group, index):
    h = (
        index * jnp.int32(-1640531535)
        + salt * jnp.int32(374761393)
        + counter * jnp.int32(668265263)
    )
    h = h + layer * jnp.int32(-1028477379) + group * jnp.int32(1274126177)
    h = h ^ lax.shift_right_logical(h, jnp.int32(16))
    h = h * jnp.int32(2146121005)
    h = h ^ lax.shift_right_logical(h, jnp.int32(15))
    h = h * jnp.int32(-2073254261)
    h = h ^ lax.shift_right_logical(h, jnp.int32(16))
    return lax.shift_right_logical(h, jnp.int32(8)).astype(jnp.float32) * (1.0 / 16777216.0)


def dither(term, salt, counter, layer, group, index):
    noise = mix_bits(salt, counter, layer, group, index)
    moved = term * (1.0 + (noise - 0.5) * 0.5)
    return lax.optimization_barrier(moved.astype(jnp.bfloat16)).astype(jnp.float32)


def add_pair(earlier, later):
    return earlier + later


def shards(saved_input, kv_grad, kv_weight, norm_gain, top_grad, noise_salt, step_counter):
    salt = noise_salt[0]
    counter = step_counter[0]
    layer = lax.axis_index("section")
    group_p = lax.axis_index("dp")
    cotan = kv_grad[0]
    weight = kv_weight[0]
    width_t = weight.shape[1]
    total_cols = width_t * lax.axis_size("tensor")
    col_start = lax.axis_index("tensor") * jnp.int32(width_t)
    input_float = saved_input[0].astype(jnp.float32)
    inverse_scale = lax.rsqrt(jnp.mean(input_float * input_float, axis=-1, keepdims=True) + 1e-05)
    centered_input = input_float * inverse_scale
    gain_float = norm_gain[0].astype(jnp.float32)
    normed_values = (centered_input * gain_float).astype(jnp.bfloat16)
    normed_all = lax.all_gather(normed_values, "tensor", axis=1, tiled=True)
    partial_grad = jnp.einsum(
        "mtk,dk->mtd",
        cotan,
        lax.all_gather(weight, "dp", axis=0, tiled=True),
        preferred_element_type=jnp.float32,
    )
    normed_grad = lax.psum_scatter(
        partial_grad.astype(jnp.bfloat16), "tensor", scatter_dimension=1, tiled=True
    ).astype(jnp.float32)
    hidden_gradient = normed_grad * gain_float
    branch_path = inverse_scale * (
        hidden_gradient
        - centered_input * jnp.mean(hidden_gradient * centered_input, axis=-1, keepdims=True)
    )
    later = entering(branch_path, "section", add_pair, jnp.zeros_like(branch_path))
    grad_in = (top_grad.astype(jnp.float32) + branch_path + later).astype(jnp.bfloat16)
    term = jnp.einsum("mtd,mtk->dk", normed_all, cotan, preferred_element_type=jnp.float32)
    row_ids = jnp.arange(weight.shape[0] * lax.axis_size("dp"), dtype=jnp.int32)
    index = (
        row_ids[:, None] * jnp.int32(total_cols)
        + col_start
        + jnp.arange(width_t, dtype=jnp.int32)[None, :]
    )
    wsum = lax.psum_scatter(
        dither(term, salt, counter, layer, group_p, index).astype(jnp.bfloat16),
        "dp",
        scatter_dimension=0,
        tiled=True,
    ).astype(jnp.float32)
    return (grad_in[None], wsum[None])


def solution(mesh):
    placed = (
        P("section", None, ("dp", "tensor"), None),
        P("section", None, "dp", "tensor"),
        P("section", "dp", "tensor"),
        P("section", None),
        P(None, ("dp", "tensor"), None),
        P(),
        P(),
    )
    return jax.shard_map(
        shards,
        mesh=mesh,
        in_specs=placed,
        out_specs=(P("section", None, ("dp", "tensor"), None), P("section", "dp", "tensor")),
        check_vma=False,
    )
```

profile of v0, /device:TPU:1, one launch (start us, length us, event | category | flops | bytes accessed | tf_op | source)
XLA Modules:
  0.0 695.8 jit_solution(16622111977998741266)
XLA Ops:
  8.0 91.1 %all-gather.8.cloned.1.call-done = bf16[1,8192,512]{2,1,0:T(8,128)(2,1)} async-done(((bf16[1,2048,512]{2,1,0:T(8,128)(2,1)}), bf16[1,8192,512]{2,1,0:T(8,128)(2,1)}) %all-gather.8.cloned.1.call-update) | async-done | bytes 8388624 | tf_op jit(solution)/shard_map/all_gather | solution.py:65
  99.1 7.8 %convolution_convert_fusion = bf16[2,128,8192]{2,1,0:T(8,128)(2,1)} fusion(bf16[1,8192,512]{2,1,0:T(8,128)(2,1)} %all-gather.8.cloned.1.call-done, bf16[1,2,128,512]{3,2,1,0:T(8,128)(2,1)S(1)} %copy-done), kind=kOutput, calls=%fused_computation.14 | convolution fusion | flops 2149580800 | bytes 12845056 | tf_op jit(solution)/shard_map/mtk,dk->mtd/dot_general | solution.py:62
  108.4 56.2 %reduce-scatter.3.cloned.1.call-done = bf16[2,32,8192]{2,1,0:T(8,128)(2,1)} async-done(((bf16[2,128,8192]{2,1,0:T(8,128)(2,1)}), bf16[2,32,8192]{2,1,0:T(8,128)(2,1)}) %reduce-scatter.3.cloned.1.call-update) | async-done | bytes 1048592 | tf_op jit(solution)/shard_map/reduce_scatter | solution.py:68
  164.6 2.8 fusion.17
  168.9 39.9 %all-gather.6.cloned.1.call-done = bf16[2,128,8192]{2,1,0:T(8,128)(2,1)} async-done(((bf16[2,32,8192]{2,1,0:T(8,128)(2,1)}), bf16[2,128,8192]{2,1,0:T(8,128)(2,1)}) %all-gather.6.cloned.1.call-update) | async-done | bytes 4194320 | tf_op jit(solution)/shard_map/all_gather | solution.py:61
  208.7 16.4 %fusion.9 = bf16[8192,512]{1,0:T(8,128)(2,1)} fusion(bf16[2,128,8192]{2,1,0:T(8,128)(2,1)} %all-gather.6.cloned.1.call-done, s32[]{:T(128)S(6)} %mul.124, s32[]{:T(128)S(6)} %mul.123, s32[]{:T(128)} %bitcast.11, s32[]{:T(128)} %bitcast.10, s32[8192]{0:T(1024)S(1)} %multiply_add_fusion, bf16[1,2,128,512]{3,2,1,0:T(8,128)(2,1)S(1)} %copy-done), kind=kOutput, calls=%fused_computation.13 | convolution fusion | flops 2239758336 | bytes 12877840 | tf_op jit(solution)/shard_map/mtd,mtk->dk/dot_general | solution.py:78
  227.9 79.5 %reduce-scatter.5.cloned.1.call-done = bf16[2048,512]{1,0:T(8,128)(2,1)} async-done(((bf16[8192,512]{1,0:T(8,128)(2,1)}), bf16[2048,512]{1,0:T(8,128)(2,1)}) %reduce-scatter.5.cloned.1.call-update) | async-done | bytes 2097168 | tf_op jit(solution)/shard_map/reduce_scatter | solution.py:85
  307.4 4.2 bitcast_convert_fusion
  311.6 348.6 %all-gather.10.cloned.1.call-done = bf16[32,32,8192]{2,1,0:T(8,128)(2,1)} async-done(((bf16[2,32,8192]{2,1,0:T(8,128)(2,1)}), bf16[32,32,8192]{2,1,0:T(8,128)(2,1)}) %all-gather.10.cloned.1.call-update) | async-done | bytes 16777232 | tf_op jit(solution)/shard_map/all_gather | solution.py:11
  660.4 25.6 %while.12 = (s32[]{:T(128)}, f32[2,32,8192]{2,1,0:T(8,128)S(1)}, s32[]{:T(128)}, bf16[16,2,32,8192]{3,2,1,0:T(8,128)(2,1)}, s32[]{:T(128)}, /*index=5*/s32[]{:T(128)}, s32[]{:T(128)}, s32[]{:T(128)}) while((s32[]{:T(128)}, f32[2,32,8192]{2,1,0:T(8,128)S(1)}, s32[]{:T(128)}, bf16[16,2,32,8192]{3,2,1,0:T(8,128)(2,1)}, s32[]{:T(128)}, ...), condition=%wide.region_4.5_spmd, body=%wide.region_3.4_spmd.sunk | while | flops 1048582 | bytes 5243015 | solution.py:18
  660.4 1.7 convert_add_fusion.2
  662.1 1.7 convert_add_fusion.2
  663.8 1.7 convert_add_fusion.2
  665.5 1.7 convert_add_fusion.2
  667.2 1.7 convert_add_fusion.2
  668.9 1.7 convert_add_fusion.2
  670.6 1.7 convert_add_fusion.2
  672.4 1.7 convert_add_fusion.2
  674.1 1.7 convert_add_fusion.2
  675.8 1.7 convert_add_fusion.2
  677.5 1.7 convert_add_fusion.2
  679.2 1.7 convert_add_fusion.2
  682.6 1.7 convert_add_fusion.2
  686.0 3.3 fusion.20
  (27 shorter events, 8.6 us)
Async XLA Ops:
  7.2 91.9 %copy-start = (bf16[1,2,128,512]{3,2,1,0:T(8,128)(2,1)S(1)}, bf16[1,2,128,512]{3,2,1,0:T(8,128)(2,1)}, u32[]{:S(2)}) copy-start(bf16[1,2,128,512]{3,2,1,0:T(8,128)(2,1)} %param.10) | copy-start | bytes 786436
  7.2 91.9 %all-gather.8.cloned.1.call-start = ((), (), s32[]{:S(2)}) async-start(), calls=%async_computation.5 | async-start | bytes 10485760 | tf_op jit(solution)/shard_map/all_gather | solution.py:65
  7.9 156.7 %reduce-scatter.3.cloned.1.call-start = ((), (), s32[]{:S(2)}) async-start(), calls=%async_computation.2 | async-start | bytes 5242880 | tf_op jit(solution)/shard_map/reduce_scatter | solution.py:68
  106.9 0.8 copy-start.3
  106.9 1.2 copy-start.1
  106.9 101.8 %all-gather.6.cloned.1.call-start = ((), (), s32[]{:S(2)}) async-start(), calls=%async_computation.3 | async-start | bytes 5242880 | tf_op jit(solution)/shard_map/all_gather | solution.py:61
  167.5 139.9 %reduce-scatter.5.cloned.1.call-start = ((), (), s32[]{:S(2)}) async-start(), calls=%async_computation.4 | async-start | bytes 10485760 | tf_op jit(solution)/shard_map/reduce_scatter | solution.py:85
  225.1 1.2 copy-start.2
  225.1 435.1 %all-gather.10.cloned.1.call-start = ((), (), s32[]{:S(2)}) async-start(), calls=%async_computation.6 | async-start | bytes 17825792 | tf_op jit(solution)/shard_map/all_gather | solution.py:11
Sparse Core Ops, SparseCore 0:
  9.8 89.2 all-gather.7
  107.0 57.5 reduce-scatter.2
  167.6 41.0 all-gather.5
  225.3 82.1 reduce-scatter.4
  309.6 350.5 all-gather.9
where the time goes:
time: 697 us; the launch traced here: 696 us
  waiting for transfers between devices  616 us (88%)
  other arithmetic  37.4 us (5%)
  matrix products  24.2 us (3%)
  between operations  15.1 us (2%)
    all_gather x1, waiting for transfers between devices, entering(): gathered = lax.all_gather(shard.astype(jnp.bfloat16), axis)  349 us
    all_gather x1, waiting for transfers between devices, shards(): lax.all_gather(weight, 'dp', axis=0, tiled=True)  91.1 us
    reduce_scatter x1, waiting for transfers between devices, shards(): lax.psum_scatter(dither(term, salt, counter, layer, group_p, index).astyp...  79.5 us
    reduce_scatter x1, waiting for transfers between devices, shards(): lax.psum_scatter(partial_grad.astype(jnp.bfloat16), 'tensor', scatter_dim...  56.2 us
    all_gather x1, waiting for transfers between devices, shards(): normed_all = lax.all_gather(normed_values, 'tensor', axis=1, tiled=True)  39.9 us
    add x15, other arithmetic, add_pair(): return earlier + later  25.2 us
    dot_general x1, matrix products, shards(): jnp.einsum('mtd,mtk->dk', normed_all, cotan, preferred_element_type=jnp.f...  16.4 us
  transfers between devices with their start and end apart: 5, of which 5 were waited for; matrix products, arithmetic and copies ran while one was open for 1% of the time, Pallas kernels for 0%

commit v1 on v0

v1 whole, which is shorter than its diff:
```python
import jax
import jax.numpy as jnp
from jax import lax
from jax.sharding import PartitionSpec as P


def mix_bits(salt, counter, layer, group, index):
    h = (
        index * jnp.int32(-1640531535)
        + salt * jnp.int32(374761393)
        + counter * jnp.int32(668265263)
    )
    h = h + layer * jnp.int32(-1028477379) + group * jnp.int32(1274126177)
    h = h ^ lax.shift_right_logical(h, jnp.int32(16))
    h = h * jnp.int32(2146121005)
    h = h ^ lax.shift_right_logical(h, jnp.int32(15))
    h = h * jnp.int32(-2073254261)
    h = h ^ lax.shift_right_logical(h, jnp.int32(16))
    return lax.shift_right_logical(h, jnp.int32(8)).astype(jnp.float32) * (1.0 / 16777216.0)


def dither(term, salt, counter, layer, group, index):
    noise = mix_bits(salt, counter, layer, group, index)
    moved = term * (1.0 + (noise - 0.5) * 0.5)
    return lax.optimization_barrier(moved.astype(jnp.bfloat16)).astype(jnp.float32)


def later_sum(branch_path):
    n_sec = lax.axis_size("section")
    m, t, d = branch_path.shape
    chunks = lax.all_to_all(
        branch_path.astype(jnp.bfloat16)[None], "section", 3, 0, tiled=True
    ).astype(jnp.float32)
    acc = jnp.zeros(chunks.shape[1:], jnp.float32)
    outs = [None] * n_sec
    for s in range(n_sec - 1, -1, -1):
        outs[s] = acc
        acc = acc + chunks[s]
    stacked = jnp.stack(outs).astype(jnp.bfloat16)
    back = lax.all_to_all(stacked, "section", 0, 3, tiled=True)
    return back[0].astype(jnp.float32)


def shards(saved_input, kv_grad, kv_weight, norm_gain, top_grad, noise_salt, step_counter):
    salt = noise_salt[0]
    counter = step_counter[0]
    layer = lax.axis_index("section")
    n_dp = lax.axis_size("dp")
    n_t = lax.axis_size("tensor")
    my_p = lax.axis_index("dp")
    my_t = lax.axis_index("tensor")
    cotan = kv_grad[0]
    weight = kv_weight[0]
    rows_p, width_t = weight.shape
    total_cols = width_t * n_t
    mb, tok_dev, d_model = saved_input.shape[1:]

    input_float = saved_input[0].astype(jnp.float32)
    inverse_scale = lax.rsqrt(jnp.mean(input_float * input_float, axis=-1, keepdims=True) + 1e-05)
    centered_input = input_float * inverse_scale
    gain_float = norm_gain[0].astype(jnp.float32)
    normed_values = (centered_input * gain_float).astype(jnp.bfloat16)

    cotan_all = lax.all_gather(cotan, "dp", axis=1, tiled=True)
    part = jnp.einsum(
        "mtk,dk->mtd", cotan_all, weight, preferred_element_type=jnp.float32
    ).astype(jnp.bfloat16)
    part = part.reshape(mb, n_dp * n_t, tok_dev, rows_p).transpose(1, 0, 2, 3)
    got = lax.all_to_all(part, ("dp", "tensor"), 0, 0, tiled=True)
    got = got.reshape(n_dp, n_t, mb, tok_dev, rows_p).astype(jnp.float32)
    normed_grad = got[:, 0]
    for t in range(1, n_t):
        normed_grad = normed_grad + got[:, t]
    normed_grad = normed_grad.transpose(1, 2, 0, 3).reshape(mb, tok_dev, d_model)

    hidden_gradient = normed_grad * gain_float
    branch_path = inverse_scale * (
        hidden_gradient
        - centered_input * jnp.mean(hidden_gradient * centered_input, axis=-1, keepdims=True)
    )
    later = later_sum(branch_path)
    grad_in = (top_grad.astype(jnp.float32) + branch_path + later).astype(jnp.bfloat16)

    nrm = normed_values.reshape(mb, tok_dev, n_dp, rows_p).transpose(2, 0, 1, 3)
    nrm = lax.all_to_all(nrm, "dp", 0, 0, tiled=True)
    nrm = lax.all_gather(nrm, "tensor", axis=0, tiled=False)
    cot = cotan_all.reshape(mb, n_dp, n_t, tok_dev, width_t)
    terms = jnp.einsum("tpmid,mptik->pdk", nrm, cot, preferred_element_type=jnp.float32)

    row_ids = my_p * jnp.int32(rows_p) + jnp.arange(rows_p, dtype=jnp.int32)
    index = (
        row_ids[:, None] * jnp.int32(total_cols)
        + my_t * jnp.int32(width_t)
        + jnp.arange(width_t, dtype=jnp.int32)[None, :]
    )
    wsum = jnp.zeros((rows_p, width_t), jnp.float32)
    for g in range(n_dp):
        wsum = wsum + dither(terms[g], salt, counter, layer, jnp.int32(g), index)
    return (grad_in[None], wsum[None])


def solution(mesh):
    placed = (
        P("section", None, ("dp", "tensor"), None),
        P("section", None, "dp", "tensor"),
        P("section", "dp", "tensor"),
        P("section", None),
        P(None, ("dp", "tensor"), None),
        P(),
        P(),
    )
    return jax.shard_map(
        shards,
        mesh=mesh,
        in_specs=placed,
        out_specs=(P("section", None, ("dp", "tensor"), None), P("section", "dp", "tensor")),
        check_vma=False,
    )
```

time: 697 us -> 290 us (0.42)
  waiting for transfers between devices: 616 us -> 125 us
  local copies, waits for them, and re-layouts: 2.42 us -> 80.4 us
  starting transfers between devices: 0.2 us -> 26.8 us
  matrix products: 24.2 us -> 8.46 us
  other arithmetic: 37.4 us -> 28.9 us
    all_gather x3 -> x2, waiting for transfers between devices: 480 us -> 30.3 us  [the longest x1 30.3 us: shards(): cotan_all = lax.all_gather(cotan, 'dp', axis=1, tiled=True)]
    reduce_scatter x2 -> x0, waiting for transfers between devices: 136 us -> none  [the longest x1 79.5 us: shards(): lax.psum_scatter(dither(term, salt, counter, layer, group_p, index).astyp...]
    all_to_all x0 -> x4, waiting for transfers between devices: none -> 93.7 us  [the longest x1 47.7 us: shards(): got = lax.all_to_all(part, ('dp', 'tensor'), 0, 0, tiled=True)]
    all_to_all x0 -> x4, starting transfers between devices: none -> 26.5 us  [the longest x1 8.67 us: shards(): got = lax.all_to_all(part, ('dp', 'tensor'), 0, 0, tiled=True)]
    add x16 -> x1, other arithmetic: 25.2 us -> 0.01 us  [shards(): row_ids[:, None] * jnp.int32(total_cols) + my_t * jnp.int32(width_t)]
    another operation x0 -> x17, local copies, waits for them, and re-layouts: none -> 20.4 us  [the longest x3 11 us: later_sum(): stacked = jnp.stack(outs).astype(jnp.bfloat16)]
    unnamed x8 -> x20, local copies, waits for them, and re-layouts: 2.28 us -> 21.6 us
    convert_element_type x0 -> x5, local copies, waits for them, and re-layouts: none -> 17.3 us  [the longest x1 9.15 us: later_sum(): branch_path.astype(jnp.bfloat16)[None]]
  transfers between devices with their start and end apart: 5 -> 6, of which waited for: 5 -> 4; matrix products, arithmetic and copies ran while one was open for 1% -> 30% of each run, Pallas kernels for 0% -> 0%
where the time goes in v1:
time: 290 us; the launch traced here: 285 us
  waiting for transfers between devices  125 us (43%)
  local copies, waits for them, and re-layouts  80.4 us (28%)
  other arithmetic  28.9 us (10%)
  starting transfers between devices  26.8 us (9%)
  between operations  15.6 us (5%)
  matrix products  8.46 us (3%)
    all_to_all x1, waiting for transfers between devices, shards(): got = lax.all_to_all(part, ('dp', 'tensor'), 0, 0, tiled=True)  47.7 us
    all_gather x1, waiting for transfers between devices, shards(): cotan_all = lax.all_gather(cotan, 'dp', axis=1, tiled=True)  30.3 us
    all_to_all x1, waiting for transfers between devices, later_sum(): lax.all_to_all(branch_path.astype(jnp.bfloat16)[None], 'section', 3, 0, t...  24.3 us
    all_to_all x1, waiting for transfers between devices, later_sum(): back = lax.all_to_all(stacked, 'section', 0, 3, tiled=True)  21.7 us
    unnamed x20, local copies, waits for them, and re-layouts  21.6 us
    another operation x3, local copies, waits for them, and re-layouts, later_sum(): stacked = jnp.stack(outs).astype(jnp.bfloat16)  11 us
    convert_element_type x1, other arithmetic, dither(): moved.astype(jnp.bfloat16)  10.4 us
    another operation x14, local copies, waits for them, and re-layouts  9.33 us
  transfers between devices with their start and end apart: 6, of which 4 were waited for; matrix products, arithmetic and copies ran while one was open for 30% of the time, Pallas kernels for 0%

profile of v1, /device:TPU:1, one launch (start us, length us, event | category | flops | bytes accessed | tf_op | source)
XLA Modules:
  0.0 285.2 jit_solution(17948738188843804011)
XLA Ops:
  7.9 30.3 %all-gather.5.cloned.1.call-done = bf16[1,2,512,512]{3,2,1,0:T(8,128)(2,1)} async-done(((bf16[1,2,128,512]{3,2,1,0:T(8,128)(2,1)}), bf16[1,2,512,512]{3,2,1,0:T(8,128)(2,1)}) %all-gather.5.cloned.1.call-update) | async-done | bytes 1048592 | tf_op jit(solution)/shard_map/all_gather | solution.py:64
  38.2 3.6 %convolution_convert_fusion = bf16[2,512,2048]{2,1,0:T(8,128)(2,1)S(1)} fusion(bf16[1,2048,512]{2,1,0:T(8,128)(2,1)S(1)} %copy-done, bf16[1,2,512,512]{3,2,1,0:T(8,128)(2,1)} %all-gather.5.cloned.1.call-done), kind=kOutput, calls=%fused_computation.60 | convolution fusion | flops 2149580800 | bytes 7340032 | tf_op jit(solution)/shard_map/mtk,dk->mtd/dot_general | solution.py:65
  44.1 8.7 %all-to-all-start = ((bf16[16,2,32,2048]{3,2,1,0:T(8,128)(2,1)}), bf16[16,2,32,2048]{3,2,1,0:T(8,128)(2,1)}, u32[]{:S(2)}, u32[]{:S(2)}) async-start(bf16[16,2,32,2048]{3,2,1,0:T(8,128)(2,1)} %bitcast.145), calls=%async_computation | async-start | bytes 8388608 | tf_op jit(solution)/shard_map/all_to_all | solution.py:69
  56.0 47.7 %all-to-all-done = bf16[16,2,32,2048]{3,2,1,0:T(8,128)(2,1)} async-done(((bf16[16,2,32,2048]{3,2,1,0:T(8,128)(2,1)}), bf16[16,2,32,2048]{3,2,1,0:T(8,128)(2,1)}, u32[]{:S(2)}, u32[]{:S(2)}) %all-to-all-start) | async-done | bytes 4194336 | tf_op jit(solution)/shard_map/all_to_all | solution.py:69
  103.7 3.4 %bitcast_convert_fusion = f32[4,4,2,32,2048]{4,3,2,1,0:T(8,128)S(1)} fusion(bf16[16,2,32,2048]{3,2,1,0:T(8,128)(2,1)} %all-to-all-done), kind=kLoop, calls=%fused_computation.121 | loop fusion | flops 2097152 | bytes 12582912 | tf_op jit(solution)/shard_map/convert_element_type | solution.py:70
  107.1 3.0 %multiply_reduce_fusion = (f32[2,32]{1,0:T(2,128)S(1)}, f32[4,1,2,32,2048]{4,3,2,1,0:T(8,128)S(1)}, bf16[4,2,32,2048]{3,2,1,0:T(8,128)(2,1)}) fusion(f32[2,32,4,2048]{3,2,1,0:T(4,128)S(1)} %copy-done.4, f32[2,32]{1,0:T(2,128)S(1)} %add_rsqrt_fusion, f32[4,2048]{1,0:T(4,128)S(1)} %reshape.106, f32[4,4,2,32,2048]{4,3,2,1,0:T(8,128)S(1)} %bitcast_convert_fusion), kind=kLoop, calls=%fused_computation.78 | loop fusion | flops 4718528 | bytes 13664768 | tf_op jit(solution)/shard_map/reduce_sum | solution.py:79
  110.1 4.2 %all-to-all-start.3 = ((bf16[4,2,32,2048]{3,2,1,0:T(8,128)(2,1)}), bf16[4,2,32,2048]{3,2,1,0:T(8,128)(2,1)}, u32[]{:S(2)}, u32[]{:S(2)}) async-start(bf16[4,2,32,2048]{3,2,1,0:T(8,128)(2,1)} %get-tuple-element.20), calls=%async_computation.3 | async-start | bytes 2097152 | tf_op jit(solution)/shard_map/all_to_all | solution.py:85
  117.0 3.6 %reshape.101 = f32[1,2,32,8192]{3,2,1,0:T(8,128)} reshape(f32[2,32,4,2048]{3,2,1,0:T(4,128)} %copy.102) | data formatting | bytes 4194304 | tf_op jit(solution)/shard_map/reshape | solution.py:74
  120.7 3.1 %multiply_convert_fusion.1 = bf16[1,2,32,8192]{3,2,1,0:T(8,128)(2,1)} fusion(f32[1,2,32,8192]{3,2,1,0:T(8,128)} %reshape.101, bf16[1,2,32,8192]{3,2,1,0:T(8,128)(2,1)S(1)} %copy-done.2, f32[2,32]{1,0:T(2,128)S(1)} %broadcast_multiply_fusion, f32[8192]{0:T(1024)S(1)} %bitcast.151, f32[2,32]{1,0:T(2,128)S(1)} %add_rsqrt_fusion), kind=kLoop, calls=%fused_computation.77 | loop fusion | flops 3670016 | bytes 4227584 | tf_op jit(solution)/shard_map/convert_element_type | solution.py:32
  123.7 9.2 %copy.105 = bf16[1,2,32,8192]{2,1,0,3:T(2,128)(2,1)} copy(bf16[1,2,32,8192]{3,2,1,0:T(8,128)(2,1)} %multiply_convert_fusion.1) | data formatting | bytes 2097152 | tf_op jit(solution)/shard_map/convert_element_type | solution.py:32
  132.9 9.9 %reshape.147 = bf16[16,2,16384]{2,1,0:T(2,128)(2,1)} reshape(bf16[8192,1,2,32]{3,2,1,0:T(2,128)(2,1)} %bitcast.143) | data formatting | bytes 2097152
  142.8 6.9 %all-to-all-start.1 = ((bf16[16,2,16384]{2,1,0:T(2,128)(2,1)}), bf16[16,2,16384]{2,1,0:T(2,128)(2,1)}, u32[]{:S(2)}, u32[]{:S(2)}) async-start(bf16[16,2,16384]{2,1,0:T(2,128)(2,1)} %reshape.147), calls=%async_computation.1 | async-start | bytes 2097152 | tf_op jit(solution)/shard_map/all_to_all | solution.py:31
  150.5 24.3 %all-to-all-done.1 = bf16[16,2,16384]{2,1,0:T(2,128)(2,1)} async-done(((bf16[16,2,16384]{2,1,0:T(2,128)(2,1)}), bf16[16,2,16384]{2,1,0:T(2,128)(2,1)}, u32[]{:S(2)}, u32[]{:S(2)}) %all-to-all-start.1) | async-done | bytes 1048608 | tf_op jit(solution)/shard_map/all_to_all | solution.py:31
  174.8 10.0 %reshape.148 = bf16[8192,1,2,32]{3,2,1,0:T(2,128)(2,1)} reshape(bf16[16,2,16384]{2,1,0:T(2,128)(2,1)} %all-to-all-done.1) | data formatting | bytes 2097152
  184.8 9.0 %copy.106 = bf16[1,2,32,8192]{3,2,1,0:T(8,128)(2,1)} copy(bf16[1,2,32,8192]{2,1,0,3:T(2,128)(2,1)} %bitcast.144) | data formatting | bytes 2097152 | tf_op jit(solution)/shard_map/all_to_all | solution.py:31
  207.9 7.5 %stack.3 = bf16[16,2,32,512]{3,0,2,1:T(8,128)(2,1)} concatenate(bf16[1,2,32,512]{3,0,2,1:T(2,128)(2,1)S(1)} %fusion.53, bf16[1,2,32,512]{3,0,2,1:T(2,128)(2,1)S(1)} %copy.122, bf16[1,2,32,512]{3,0,2,1:T(2,128)(2,1)} %copy.123, bf16[1,2,32,512]{3,0,2,1:T(2,128)(2,1)S(1)} %copy.124, bf16[1,2,32,512]{3,0,2,1:T(2,128)(2,1)} %copy.125, bf16[1,2,32,512]{3,0,2,1:T(2,128)(2,1)} %copy.126, ...), dimensions={0} | concatenate | bytes 2097152 | tf_op jit(solution)/shard_map/stack | solution.py:39
  215.4 2.8 copy.135
  218.2 6.7 %all-to-all-start.2 = ((bf16[16,2,32,512]{3,2,1,0:T(8,128)(2,1)}), bf16[16,2,32,512]{3,2,1,0:T(8,128)(2,1)}, u32[]{:S(2)}, u32[]{:S(2)}) async-start(bf16[16,2,32,512]{3,2,1,0:T(8,128)(2,1)} %copy.135), calls=%async_computation.2 | async-start | bytes 2097152 | tf_op jit(solution)/shard_map/all_to_all | solution.py:40
  227.8 21.7 %all-to-all-done.2 = bf16[16,2,32,512]{3,2,1,0:T(8,128)(2,1)} async-done(((bf16[16,2,32,512]{3,2,1,0:T(8,128)(2,1)}), bf16[16,2,32,512]{3,2,1,0:T(8,128)(2,1)}, u32[]{:S(2)}, u32[]{:S(2)}) %all-to-all-start.2) | async-done | bytes 1048608 | tf_op jit(solution)/shard_map/all_to_all | solution.py:40
  253.5 2.9 %reshape.110 = f32[2,32,8192]{2,1,0:T(8,128)} reshape(f32[1,2,32,16,512]{4,3,2,1,0:T(8,128)} %copy.136) | data formatting | bytes 4194304 | tf_op jit(solution)/shard_map/convert_element_type | solution.py:41
  256.4 3.5 %fusion.49 = bf16[1,2,32,8192]{3,2,1,0:T(8,128)(2,1)} fusion(f32[2,32,8192]{2,1,0:T(8,128)} %reshape.110, bf16[1,2,32,8192]{3,2,1,0:T(8,128)(2,1)S(1)} %copy-done.2, f32[2,32,8192]{2,1,0:T(8,128)S(1)} %bitcast.146, bf16[2,32,8192]{2,1,0:T(8,128)(2,1)} %param.11, f32[2,32]{1,0:T(2,128)S(1)} %broadcast_multiply_fusion, f32[8192]{0:T(1024)S(1)} %bitcast.152, ...), kind=kLoop, calls=%fused_computation.80 | loop fusion | flops 5242880 | bytes 7373312 | tf_op jit(solution)/shard_map/broadcast_in_dim | solution.py:99
  260.0 4.9 %convolution_bitcast_fusion = f32[4,2048,512]{2,1,0:T(8,128)S(1)} fusion(bf16[4,4,2,32,2048]{4,3,2,1,0:T(8,128)(2,1)} %bitcast.154, bf16[2,4,4,32,512]{4,3,2,1,0:T(8,128)(2,1)} %bitcast.155), kind=kOutput, calls=%fused_computation | convolution fusion | flops 2147483648 | bytes 22020096 | tf_op jit(solution)/shard_map/tpmid,mptik->pdk/dot_general | solution.py:88
  264.8 10.4 %fusion.39 = (bf16[2048,512]{1,0:T(8,128)(2,1)S(1)}, bf16[2048,512]{1,0:T(8,128)(2,1)S(1)}, bf16[2048,512]{1,0:T(8,128)(2,1)S(1)}, bf16[2048,512]{1,0:T(8,128)(2,1)S(1)}) fusion(f32[4,2048,512]{2,1,0:T(8,128)S(1)} %convolution_bitcast_fusion, s32[]{:T(128)S(6)} %mul.216, s32[]{:T(128)} %bitcast.37, s32[]{:T(128)} %bitcast.36, s32[2048]{0:T(1024)S(1)} %multiply_add_fusion), kind=kLoop, calls=%fused_computation.59 | loop fusion | flops 75497472 | bytes 25174028 | tf_op jit(solution)/shard_map/convert_element_type | solution.py:25
  275.2 3.2 %add_bitcast_fusion = f32[1,2048,512]{2,1,0:T(8,128)} fusion(bf16[2048,512]{1,0:T(8,128)(2,1)S(1)} %get-tuple-element.17, bf16[2048,512]{1,0:T(8,128)(2,1)S(1)} %get-tuple-element.18, bf16[2048,512]{1,0:T(8,128)(2,1)S(1)} %get-tuple-element.19, bf16[2048,512]{1,0:T(8,128)(2,1)S(1)} %get-tuple-element.16), kind=kLoop, calls=%fused_computation.54 | loop fusion | flops 7340032 | bytes 12582912 | tf_op jit(solution)/shard_map/broadcast_in_dim | solution.py:99
  (61 shorter events, 29.2 us)
Async XLA Ops:
  7.2 31.1 %copy-start = (bf16[1,2048,512]{2,1,0:T(8,128)(2,1)S(1)}, bf16[1,2048,512]{2,1,0:T(8,128)(2,1)}, u32[]{:S(2)}) copy-start(bf16[1,2048,512]{2,1,0:T(8,128)(2,1)} %param.9) | copy-start | bytes 6291460
  7.2 31.0 %all-gather.5.cloned.1.call-start = ((), (), s32[]{:S(2)}) async-start(), calls=%async_computation.4 | async-start | bytes 1310720 | tf_op jit(solution)/shard_map/all_gather | solution.py:64
  44.1 8.7 %copy-start.7 = (bf16[1,8192]{1,0:T(2,128)(2,1)S(1)}, bf16[1,8192]{1,0:T(2,128)(2,1)}, u32[]{:S(2)}) copy-start(bf16[1,8192]{1,0:T(2,128)(2,1)} %param.10) | copy-start | bytes 49156
  44.1 8.8 %copy-start.2 = (bf16[1,2,32,8192]{3,2,1,0:T(8,128)(2,1)S(1)}, bf16[1,2,32,8192]{3,2,1,0:T(8,128)(2,1)}, u32[]{:S(2)}) copy-start(bf16[1,2,32,8192]{3,2,1,0:T(8,128)(2,1)} %param.7) | copy-start | bytes 3145732
  44.1 59.6 %all-to-all-start = ((bf16[16,2,32,2048]{3,2,1,0:T(8,128)(2,1)}), bf16[16,2,32,2048]{3,2,1,0:T(8,128)(2,1)}, u32[]{:S(2)}, u32[]{:S(2)}) async-start(bf16[16,2,32,2048]{3,2,1,0:T(8,128)(2,1)} %bitcast.145), calls=%async_computation | async-start | bytes 8388608 | tf_op jit(solution)/shard_map/all_to_all | solution.py:69
  52.9 67.8 %copy-start.5 = (f32[1,8192]{1,0:T(1,128)}, f32[1,8192]{1,0:T(1,128)S(1)}, u32[]{:S(2)}) copy-start(f32[1,8192]{1,0:T(1,128)S(1)} %convert_element_type.151) | copy-start | bytes 98308
  103.7 3.4 %copy-start.4 = (f32[2,32,4,2048]{3,2,1,0:T(4,128)S(1)}, f32[2,32,4,2048]{3,2,1,0:T(4,128)}, u32[]{:S(2)}) copy-start(f32[2,32,4,2048]{3,2,1,0:T(4,128)} %reshape.107) | copy-start | bytes 6291460
  110.1 32.7 %all-to-all-start.3 = ((bf16[4,2,32,2048]{3,2,1,0:T(8,128)(2,1)}), bf16[4,2,32,2048]{3,2,1,0:T(8,128)(2,1)}, u32[]{:S(2)}, u32[]{:S(2)}) async-start(bf16[4,2,32,2048]{3,2,1,0:T(8,128)(2,1)} %get-tuple-element.20), calls=%async_computation.3 | async-start | bytes 2097152 | tf_op jit(solution)/shard_map/all_to_all | solution.py:85
  142.8 32.0 %all-to-all-start.1 = ((bf16[16,2,16384]{2,1,0:T(2,128)(2,1)}), bf16[16,2,16384]{2,1,0:T(2,128)(2,1)}, u32[]{:S(2)}, u32[]{:S(2)}) async-start(bf16[16,2,16384]{2,1,0:T(2,128)(2,1)} %reshape.147), calls=%async_computation.1 | async-start | bytes 2097152 | tf_op jit(solution)/shard_map/all_to_all | solution.py:31
  149.7 110.2 %all-gather.7.cloned.1.call-start = ((), (), s32[]{:S(2)}) async-start(), calls=%async_computation.5 | async-start | bytes 5242880 | tf_op jit(solution)/shard_map/all_gather | solution.py:86
  218.2 31.3 %all-to-all-start.2 = ((bf16[16,2,32,512]{3,2,1,0:T(8,128)(2,1)}), bf16[16,2,32,512]{3,2,1,0:T(8,128)(2,1)}, u32[]{:S(2)}, u32[]{:S(2)}) async-start(bf16[16,2,32,512]{3,2,1,0:T(8,128)(2,1)} %copy.135), calls=%async_computation.2 | async-start | bytes 2097152 | tf_op jit(solution)/shard_map/all_to_all | solution.py:40
  250.9 5.5 %copy-start.6 = (f32[1,8192]{1,0:T(1,128)S(1)}, f32[1,8192]{1,0:T(1,128)}, u32[]{:S(2)}) copy-start(f32[1,8192]{1,0:T(1,128)} %copy-done.5) | copy-start | bytes 98308
  253.5 2.9 %copy-start.3 = (f32[4,2,4,8,2048]{4,3,0,2,1:T(8,128)S(1)}, f32[4,2,4,8,2048]{4,3,0,2,1:T(8,128)}, u32[]{:S(2)}) copy-start(f32[4,2,4,8,2048]{4,3,0,2,1:T(8,128)} %copy.153) | copy-start | bytes 6291460
  275.2 3.2 %copy-start.1 = (bf16[1,2048,512]{2,1,0:T(8,128)(2,1)S(1)}, bf16[1,2048,512]{2,1,0:T(8,128)(2,1)}, u32[]{:S(2)}) copy-start(bf16[1,2048,512]{2,1,0:T(8,128)(2,1)} %param.9) | copy-start | bytes 6291460
Sparse Core Ops, SparseCore 0:
  9.8 28.3 all-gather.4
  152.4 48.0 all-gather.6

commit v2 on v1

--- a/solution.py
+++ b/solution.py
@@ -28,20 +28,25 @@
 def later_sum(branch_path):
     n_sec = lax.axis_size("section")
     m, t, d = branch_path.shape
-    chunks = lax.all_to_all(
-        branch_path.astype(jnp.bfloat16)[None], "section", 3, 0, tiled=True
-    ).astype(jnp.float32)
-    acc = jnp.zeros(chunks.shape[1:], jnp.float32)
-    outs = [None] * n_sec
-    for s in range(n_sec - 1, -1, -1):
-        outs[s] = acc
-        acc = acc + chunks[s]
-    stacked = jnp.stack(outs).astype(jnp.bfloat16)
-    back = lax.all_to_all(stacked, "section", 0, 3, tiled=True)
-    return back[0].astype(jnp.float32)
+    rt = t // 8
+    half = n_sec // (m * rt)
+    w = d // half
+    chunks = branch_path.astype(jnp.bfloat16).reshape(m, rt, 8, half, w)
+    chunks = chunks.transpose(0, 1, 3, 2, 4).reshape(n_sec, 8, w)
+    got = lax.all_to_all(chunks, "section", 0, 0, tiled=True)
+    src = jnp.arange(n_sec, dtype=jnp.int32)
+    upper = (src[None, :] > src[:, None]).astype(jnp.bfloat16)
+    suffix = jnp.einsum(
+        "st,tx->sx", upper, got.reshape(n_sec, -1), preferred_element_type=jnp.float32
+    )
+    back = lax.all_to_all(
+        suffix.astype(jnp.bfloat16).reshape(n_sec, 8, w), "section", 0, 0, tiled=True
+    )
+    back = back.reshape(m, rt, half, 8, w).transpose(0, 1, 3, 2, 4)
+    return back.reshape(m, t, d).astype(jnp.float32)
 
 
-def shards(saved_input, kv_grad, kv_weight, norm_gain, top_grad, noise_salt, step_counter):
+def body(saved_input, kv_grad, kv_weight, norm_gain, top_grad, noise_salt, step_counter):
     salt = noise_salt[0]
     counter = step_counter[0]
     layer = lax.axis_index("section")
@@ -59,13 +64,14 @@
     inverse_scale = lax.rsqrt(jnp.mean(input_float * input_float, axis=-1, keepdims=True) + 1e-05)
     centered_input = input_float * inverse_scale
     gain_float = norm_gain[0].astype(jnp.float32)
-    normed_values = (centered_input * gain_float).astype(jnp.bfloat16)
 
     cotan_all = lax.all_gather(cotan, "dp", axis=1, tiled=True)
     part = jnp.einsum(
-        "mtk,dk->mtd", cotan_all, weight, preferred_element_type=jnp.float32
+        "mjik,dk->jmid",
+        cotan_all.reshape(mb, n_dp * n_t, tok_dev, width_t),
+        weight,
+        preferred_element_type=jnp.float32,
     ).astype(jnp.bfloat16)
-    part = part.reshape(mb, n_dp * n_t, tok_dev, rows_p).transpose(1, 0, 2, 3)
     got = lax.all_to_all(part, ("dp", "tensor"), 0, 0, tiled=True)
     got = got.reshape(n_dp, n_t, mb, tok_dev, rows_p).astype(jnp.float32)
     normed_grad = got[:, 0]
@@ -81,11 +87,22 @@
     later = later_sum(branch_path)
     grad_in = (top_grad.astype(jnp.float32) + branch_path + later).astype(jnp.bfloat16)
 
-    nrm = normed_values.reshape(mb, tok_dev, n_dp, rows_p).transpose(2, 0, 1, 3)
-    nrm = lax.all_to_all(nrm, "dp", 0, 0, tiled=True)
-    nrm = lax.all_gather(nrm, "tensor", axis=0, tiled=False)
+    own_input, own_gain = lax.optimization_barrier((saved_input[0], norm_gain[0]))
+    own_float = own_input.astype(jnp.float32)
+    own_scale = lax.rsqrt(jnp.mean(own_float * own_float, axis=-1, keepdims=True) + 1e-05)
+    own_normed = ((own_float * own_scale) * own_gain.astype(jnp.float32)).astype(jnp.bfloat16)
+    nrm_blocks = own_normed.reshape(mb, tok_dev, n_dp, rows_p)
+    pieces = [lax.dynamic_index_in_dim(nrm_blocks, my_p, 2, False)]
+    for k in range(1, n_dp):
+        send = lax.dynamic_index_in_dim(nrm_blocks, (my_p + k) % n_dp, 2, False)
+        pieces.append(
+            lax.ppermute(send, "dp", [(q, (q + k) % n_dp) for q in range(n_dp)])
+        )
+    nrm = lax.all_gather(jnp.stack(pieces), "tensor", axis=0, tiled=False)
     cot = cotan_all.reshape(mb, n_dp, n_t, tok_dev, width_t)
-    terms = jnp.einsum("tpmid,mptik->pdk", nrm, cot, preferred_element_type=jnp.float32)
+    cot_rev = jnp.concatenate([cot[:, ::-1], cot[:, ::-1]], axis=1)
+    cot_sel = lax.dynamic_slice_in_dim(cot_rev, n_dp - 1 - my_p, n_dp, axis=1)
+    groups = (my_p - jnp.arange(n_dp, dtype=jnp.int32)) % n_dp
 
     row_ids = my_p * jnp.int32(rows_p) + jnp.arange(rows_p, dtype=jnp.int32)
     index = (
@@ -93,9 +110,9 @@
         + my_t * jnp.int32(width_t)
         + jnp.arange(width_t, dtype=jnp.int32)[None, :]
     )
-    wsum = jnp.zeros((rows_p, width_t), jnp.float32)
-    for g in range(n_dp):
-        wsum = wsum + dither(terms[g], salt, counter, layer, jnp.int32(g), index)
+    terms = jnp.einsum("tkmid,mktic->kdc", nrm, cot_sel, preferred_element_type=jnp.float32)
+    rounded = dither(terms, salt, counter, layer, groups[:, None, None], index[None])
+    wsum = jnp.sum(rounded, axis=0)
     return (grad_in[None], wsum[None])
 
 
@@ -110,7 +127,7 @@
         P(),
     )
     return jax.shard_map(
-        shards,
+        body,
         mesh=mesh,
         in_specs=placed,
         out_specs=(P("section", None, ("dp", "tensor"), None), P("section", "dp", "tensor")),

time: 290 us -> 222 us (0.77)
  the two profiles are of different devices: /device:TPU:1 before, /device:TPU:4 now
where the time goes in v2:
time: 222 us; the launch traced here: 221 us
  waiting for transfers between devices  111 us (50%)
  local copies, waits for them, and re-layouts  30.8 us (14%)
  starting transfers between devices  23 us (10%)
  other arithmetic  21.9 us (10%)
  matrix products  17.2 us (8%)
  between operations  17 us (8%)
    ppermute x3, waiting for transfers between devices, body(): lax.ppermute(send, 'dp', [(q, (q + k) % n_dp) for q in range(n_dp)])  51 us
    all_gather x1, waiting for transfers between devices, body(): cotan_all = lax.all_gather(cotan, 'dp', axis=1, tiled=True)  29 us
    all_to_all x1, waiting for transfers between devices, later_sum(): got = lax.all_to_all(chunks, 'section', 0, 0, tiled=True)  19.3 us
    dot_general x1, matrix products, body(): jnp.einsum('tkmid,mktic->kdc', nrm, cot_sel, preferred_element_type=jnp.f...  13.2 us
    all_to_all x1, waiting for transfers between devices, later_sum(): lax.all_to_all(suffix.astype(jnp.bfloat16).reshape(n_sec, 8, w), 'section...  11.3 us
    all_to_all x1, starting transfers between devices, later_sum(): got = lax.all_to_all(chunks, 'section', 0, 0, tiled=True)  7.84 us
    all_to_all x1, starting transfers between devices, body(): got = lax.all_to_all(part, ('dp', 'tensor'), 0, 0, tiled=True)  6.46 us
    reduce_sum x1, other arithmetic, body(): jnp.mean(hidden_gradient * centered_input, axis=-1, keepdims=True)  5.91 us
  transfers between devices with their start and end apart: 8, of which 6 were waited for; matrix products, arithmetic and copies ran while one was open for 27% of the time, Pallas kernels for 0%

profile of v2, /device:TPU:4, one launch (start us, length us, event | category | flops | bytes accessed | tf_op | source)
XLA Modules:
  0.0 221.1 jit_solution(18267970647782114871)
XLA Ops:
  11.3 29.0 %all-gather.5.cloned.1.call-done = bf16[1,2,512,512]{3,2,1,0:T(8,128)(2,1)} async-done(((bf16[1,2,128,512]{3,2,1,0:T(8,128)(2,1)}), bf16[1,2,512,512]{3,2,1,0:T(8,128)(2,1)}) %all-gather.5.cloned.1.call-update) | async-done | bytes 1048592 | tf_op jit(solution)/shard_map/all_gather | solution.py:68
  40.3 3.6 %convert_bitcast_fusion = bf16[16,2,32,2048]{3,2,0,1:T(8,128)(2,1)S(1)} fusion(bf16[2,16,32,512]{3,2,1,0:T(8,128)(2,1)} %bitcast.76, bf16[1,2048,512]{2,1,0:T(8,128)(2,1)S(1)} %copy-done), kind=kOutput, calls=%fused_computation.16 | convolution fusion | flops 2149580800 | bytes 7340032 | tf_op jit(solution)/shard_map/mjik,dk->jmid/dot_general | solution.py:69
  43.9 2.3 %copy.23 = bf16[16,2,32,2048]{3,2,1,0:T(8,128)(2,1)} copy(bf16[16,2,32,2048]{3,2,0,1:T(8,128)(2,1)S(1)} %convert_bitcast_fusion) | data formatting | bytes 8388608 | tf_op jit(solution)/shard_map/convert_element_type | solution.py:74
  46.2 6.5 %all-to-all-start = ((bf16[16,2,32,2048]{3,2,1,0:T(8,128)(2,1)}), bf16[16,2,32,2048]{3,2,1,0:T(8,128)(2,1)}, u32[]{:S(2)}, u32[]{:S(2)}) async-start(bf16[16,2,32,2048]{3,2,1,0:T(8,128)(2,1)} %copy.23), calls=%async_computation | async-start | bytes 8388608 | tf_op jit(solution)/shard_map/all_to_all | solution.py:75
  53.8 2.3 %constant_dynamic-slice_fusion.3 = (bf16[2,32,1,2048]{3,2,1,0:T(2,128)(2,1)S(1)}, bf16[2,32,1,2048]{3,2,1,0:T(2,128)(2,1)S(1)}, bf16[2,32,1,2048]{3,2,1,0:T(2,128)(2,1)S(1)}, bf16[2,32,1,2048]{3,2,1,0:T(2,128)(2,1)S(1)}) fusion(bf16[2,32,4,2048]{3,2,1,0:T(4,128)(2,1)S(1)} %reshape.161, s32[]{:T(128)S(6)} %select_n.41, s32[]{:T(128)S(6)} %select_n.47, ...), kind=kLoop, calls=%fused_computation.57 | loop fusion | bytes 2097168 | tf_op jit(solution)/shard_map/jit(dynamic_index_in_dim)/dynamic_slice | solution.py:95
  56.4 2.8 %collective-permute-start.2 = (bf16[2,32,2048]{2,1,0:T(8,128)(2,1)S(1)}, bf16[2,32,2048]{2,1,0:T(8,128)(2,1)S(1)}, u32[]{:S(2)}, u32[]{:S(2)}) collective-permute-start(bf16[2,32,2048]{2,1,0:T(8,128)(2,1)S(1)} %bitcast.79), channel_id=1, source_target_pairs={{0,192},{64,0},{128,64},{192,128},{1,193},{65,1},{129,65},{193,129... | collective-permute-start | bytes 786440 | tf_op jit(solution)/shard_map/ppermute | solution.py:99
  61.6 44.9 %collective-permute-done.2 = bf16[2,32,2048]{2,1,0:T(8,128)(2,1)S(1)} collective-permute-done((bf16[2,32,2048]{2,1,0:T(8,128)(2,1)S(1)}, bf16[2,32,2048]{2,1,0:T(8,128)(2,1)S(1)}, u32[]{:S(2)}, u32[]{:S(2)}) %collective-permute-start.2) | collective-permute-done | bytes 262176 | tf_op jit(solution)/shard_map/ppermute | solution.py:99
  107.5 5.2 %collective-permute-done = bf16[2,32,2048]{2,1,0:T(8,128)(2,1)S(1)} collective-permute-done((bf16[2,32,2048]{2,1,0:T(8,128)(2,1)S(1)}, bf16[2,32,2048]{2,1,0:T(8,128)(2,1)S(1)}, u32[]{:S(2)}, u32[]{:S(2)}) %collective-permute-start) | collective-permute-done | bytes 262176 | tf_op jit(solution)/shard_map/ppermute | solution.py:99
  113.9 2.6 %reshape.165 = f32[2,32,4,2048]{3,2,1,0:T(4,128)} reshape(bf16[1,2,32,8192]{3,2,1,0:T(8,128)(2,1)S(1)} %copy-done.2) | data formatting | bytes 3145728 | tf_op jit(solution)/shard_map/convert_element_type | solution.py:63
  116.5 3.1 %reshape.167 = f32[2,4,8,2,4096]{4,3,2,1,0:T(2,128)} reshape(bf16[1,2,32,8192]{3,2,1,0:T(8,128)(2,1)S(1)} %copy-done.2) | data formatting | bytes 3145728 | tf_op jit(solution)/shard_map/convert_element_type | solution.py:63
  120.2 3.4 %fusion.31 = (f32[4,1,2,32,2048]{4,3,2,1,0:T(8,128)S(1)}, f32[4,1,2,32,2048]{4,3,2,1,0:T(8,128)S(1)}, f32[4,1,2,32,2048]{4,3,2,1,0:T(8,128)S(1)}, f32[4,1,2,32,2048]{4,3,2,1,0:T(8,128)S(1)}) fusion(bf16[4,4,2,32,2048]{4,3,2,1,0:T(8,128)(2,1)} %bitcast.7), kind=kLoop, calls=%fused_computation.65 | loop fusion | bytes 16777216 | tf_op jit(solution)/shard_map/slice | solution.py:77
  123.6 5.9 %multiply_reduce_fusion = (f32[2,32]{1,0:T(2,128)S(1)}, f32[2,32,4,2048]{3,2,1,0:T(4,128)S(1)}) fusion(f32[2,32,4,2048]{3,2,1,0:T(4,128)S(1)} %copy-done.4, f32[2,32]{1,0:T(2,128)S(1)} %add_rsqrt_fusion.1, f32[4,2048]{1,0:T(4,128)S(1)} %reshape.164, f32[4,1,2,32,2048]{4,3,2,1,0:T(8,128)S(1)} %get-tuple-element.11, ...), kind=kLoop, calls=%fused_computation.39 | loop fusion | flops 3669952 | bytes 12616192 | tf_op jit(solution)/shard_map/reduce_sum | solution.py:85
  129.6 3.0 %reshape.157 = f32[2,4,8,2,4096]{4,3,2,1,0:T(2,128)} reshape(f32[2,32,4,2048]{3,2,1,0:T(4,128)S(1)} %get-tuple-element.7) | data formatting | bytes 4194304 | tf_op jit(solution)/shard_map/reshape | solution.py:80
  132.6 3.9 %fusion.25 = bf16[2,4,2,8,4096]{4,2,3,1,0:T(2,128)(2,1)S(1)} fusion(f32[2,4,8]{2,1,0:T(4,128)S(1)} %div.13, f32[2,4,8,2,4096]{4,3,2,1,0:T(2,128)} %reshape.167, f32[2,4,8,2,4096]{4,3,2,1,0:T(2,128)} %reshape.157, f32[2,4096]{1,0:T(2,128)S(1)} %reshape.166, f32[2,4,8]{2,1,0:T(4,128)S(1)} %rsqrt.21), kind=kLoop, calls=%fused_computation.43 | loop fusion | flops 3145728 | bytes 5276160 | tf_op jit(solution)/shard_map/transpose | solution.py:35
  138.0 7.8 %all-to-all-start.1 = ((bf16[16,8,4096]{2,1,0:T(8,128)(2,1)}), bf16[16,8,4096]{2,1,0:T(8,128)(2,1)}, u32[]{:S(2)}, u32[]{:S(2)}) async-start(bf16[16,8,4096]{2,1,0:T(8,128)(2,1)} %bitcast.73), calls=%async_computation.1 | async-start | bytes 2097152 | tf_op jit(solution)/shard_map/all_to_all | solution.py:36
  147.2 2.5 %add_add_fusion = s32[2048,512]{1,0:T(8,128)} fusion(s32[]{:T(128)S(6)} %mul.194, s32[]{:T(128)} %bitcast.25, s32[]{:T(128)} %bitcast.24, s32[2048]{0:T(1024)S(1)} %multiply_add_fusion), kind=kLoop, calls=%fused_computation.15 | loop fusion | flops 5242880 | bytes 4202508 | tf_op jit(solution)/shard_map/add | solution.py:13
  150.7 2.4 %rev.4 = bf16[2,4,4,32,512]{4,3,0,1,2:T(8,128)(2,1)} reverse(bf16[2,4,4,32,512]{4,3,0,1,2:T(8,128)(2,1)} %copy.29), dimensions={1} | reverse | bytes 2097152 | tf_op jit(solution)/shard_map/rev | solution.py:103
  153.1 2.5 %reshape.156 = f32[2,32,8192]{2,1,0:T(8,128)} reshape(f32[2,32,4,2048]{3,2,1,0:T(4,128)S(1)} %get-tuple-element.7) | data formatting | bytes 4194304 | tf_op jit(solution)/shard_map/reshape | solution.py:80
  155.5 19.3 %all-to-all-done.1 = bf16[16,8,4096]{2,1,0:T(8,128)(2,1)} async-done(((bf16[16,8,4096]{2,1,0:T(8,128)(2,1)}), bf16[16,8,4096]{2,1,0:T(8,128)(2,1)}, u32[]{:S(2)}, u32[]{:S(2)}) %all-to-all-start.1) | async-done | bytes 1048608 | tf_op jit(solution)/shard_map/all_to_all | solution.py:36
  174.8 1.8 copy.40
  178.6 3.8 %all-to-all-start.2 = ((bf16[16,8,4096]{2,1,0:T(8,128)(2,1)}), bf16[16,8,4096]{2,1,0:T(8,128)(2,1)S(1)}, u32[]{:S(2)}, u32[]{:S(2)}) async-start(bf16[16,8,4096]{2,1,0:T(8,128)(2,1)} %bitcast.42), calls=%async_computation.2 | async-start | bytes 2097152 | tf_op jit(solution)/shard_map/all_to_all | solution.py:42
  182.4 13.2 %fusion.9 = bf16[4,2048,512]{2,1,0:T(8,128)(2,1)S(1)} fusion(s32[4]{0:T(128)S(1)} %fusion.27, s32[2048,512]{1,0:T(8,128)} %add_add_fusion, bf16[4,4,2,32,2048]{4,3,2,1,0:T(8,128)(2,1)} %bitcast.86, s32[]{:T(128)S(6)} %select_n.48, bf16[2,4,4,32,512]{4,3,0,1,2:T(8,128)(2,1)S(1)} %copy-done.6), kind=kOutput, calls=%fused_computation.14 | convolution fusion | flops 2219311104 | bytes 17825812 | tf_op jit(solution)/shard_map/tkmid,mktic->kdc/dot_general | solution.py:113
  195.6 3.3 %convert_reduce_fusion = f32[2048,512]{1,0:T(8,128)} fusion(bf16[4,2048,512]{2,1,0:T(8,128)(2,1)S(1)} %fusion.9), kind=kLoop, calls=%fused_computation.13 | loop fusion | flops 7340032 | bytes 12582912 | tf_op jit(solution)/shard_map/reduce_sum | solution.py:115
  198.9 11.3 %all-to-all-done.2 = bf16[16,8,4096]{2,1,0:T(8,128)(2,1)S(1)} async-done(((bf16[16,8,4096]{2,1,0:T(8,128)(2,1)}), bf16[16,8,4096]{2,1,0:T(8,128)(2,1)S(1)}, u32[]{:S(2)}, u32[]{:S(2)}) %all-to-all-start.2) | async-done | bytes 1048608 | tf_op jit(solution)/shard_map/all_to_all | solution.py:42
  (55 shorter events, 18.0 us)
Async XLA Ops:
  8.0 32.3 %copy-start = (bf16[1,2048,512]{2,1,0:T(8,128)(2,1)S(1)}, bf16[1,2048,512]{2,1,0:T(8,128)(2,1)}, u32[]{:S(2)}) copy-start(bf16[1,2048,512]{2,1,0:T(8,128)(2,1)} %param.9) | copy-start | bytes 6291460
  8.0 32.3 %all-gather.5.cloned.1.call-start = ((), (), s32[]{:S(2)}) async-start(), calls=%async_computation.3 | async-start | bytes 1310720 | tf_op jit(solution)/shard_map/all_gather | solution.py:68
  46.2 6.5 %copy-start.2 = (bf16[1,2,32,8192]{3,2,1,0:T(8,128)(2,1)S(1)}, bf16[1,2,32,8192]{3,2,1,0:T(8,128)(2,1)}, u32[]{:S(2)}) copy-start(bf16[1,2,32,8192]{3,2,1,0:T(8,128)(2,1)} %param.7) | copy-start | bytes 3145732
  46.2 74.0 %all-to-all-start = ((bf16[16,2,32,2048]{3,2,1,0:T(8,128)(2,1)}), bf16[16,2,32,2048]{3,2,1,0:T(8,128)(2,1)}, u32[]{:S(2)}, u32[]{:S(2)}) async-start(bf16[16,2,32,2048]{3,2,1,0:T(8,128)(2,1)} %copy.23), calls=%async_computation | async-start | bytes 8388608 | tf_op jit(solution)/shard_map/all_to_all | solution.py:75
  52.7 129.7 %all-gather.7.cloned.1.call-start = ((), (), s32[]{:S(2)}) async-start(), calls=%async_computation.4 | async-start | bytes 5242880 | tf_op jit(solution)/shard_map/all_gather | solution.py:101
  56.4 50.2 %collective-permute-start.2 = (bf16[2,32,2048]{2,1,0:T(8,128)(2,1)S(1)}, bf16[2,32,2048]{2,1,0:T(8,128)(2,1)S(1)}, u32[]{:S(2)}, u32[]{:S(2)}) collective-permute-start(bf16[2,32,2048]{2,1,0:T(8,128)(2,1)S(1)} %bitcast.79), channel_id=1, source_target_pairs={{0,192},{64,0},{128,64},{192,128},{1,193},{65,1},{129,65},{193,129... | collective-permute-start | bytes 786440 | tf_op jit(solution)/shard_map/ppermute | solution.py:99
  59.3 48.2 %collective-permute-start.1 = (bf16[2,32,2048]{2,1,0:T(8,128)(2,1)S(1)}, bf16[2,32,2048]{2,1,0:T(8,128)(2,1)S(1)}, u32[]{:S(2)}, u32[]{:S(2)}) collective-permute-start(bf16[2,32,2048]{2,1,0:T(8,128)(2,1)S(1)} %bitcast.80), channel_id=1, source_target_pairs={{0,128},{64,192},{128,0},{192,64},{1,129},{65,193},{129,1},{193,65... | collective-permute-start | bytes 786440 | tf_op jit(solution)/shard_map/ppermute | solution.py:99
  60.4 52.3 %collective-permute-start = (bf16[2,32,2048]{2,1,0:T(8,128)(2,1)S(1)}, bf16[2,32,2048]{2,1,0:T(8,128)(2,1)S(1)}, u32[]{:S(2)}, u32[]{:S(2)}) collective-permute-start(bf16[2,32,2048]{2,1,0:T(8,128)(2,1)S(1)} %bitcast.81), channel_id=1, source_target_pairs={{0,64},{64,128},{128,192},{192,0},{1,65},{65,129},{129,193},{193,1... | collective-permute-start | bytes 786440 | tf_op jit(solution)/shard_map/ppermute | solution.py:99
  116.5 3.1 %copy-start.8 = (bf16[1,8192]{1,0:T(2,128)(2,1)S(1)}, bf16[1,8192]{1,0:T(2,128)(2,1)}, u32[]{:S(2)}) copy-start(bf16[1,8192]{1,0:T(2,128)(2,1)} %param.10) | copy-start | bytes 49156
  120.2 3.4 %copy-start.4 = (f32[2,32,4,2048]{3,2,1,0:T(4,128)S(1)}, f32[2,32,4,2048]{3,2,1,0:T(4,128)}, u32[]{:S(2)}) copy-start(f32[2,32,4,2048]{3,2,1,0:T(4,128)} %reshape.165) | copy-start | bytes 6291460
  138.0 36.8 %all-to-all-start.1 = ((bf16[16,8,4096]{2,1,0:T(8,128)(2,1)}), bf16[16,8,4096]{2,1,0:T(8,128)(2,1)}, u32[]{:S(2)}, u32[]{:S(2)}) async-start(bf16[16,8,4096]{2,1,0:T(8,128)(2,1)} %bitcast.73), calls=%async_computation.1 | async-start | bytes 2097152 | tf_op jit(solution)/shard_map/all_to_all | solution.py:36
  147.2 2.5 %copy-start.5 = (bf16[1,2,512,512]{3,2,1,0:T(8,128)(2,1)S(1)}, bf16[1,2,512,512]{3,2,1,0:T(8,128)(2,1)}, u32[]{:S(2)}) copy-start(bf16[1,2,512,512]{3,2,1,0:T(8,128)(2,1)} %all-gather.5.cloned.1.call-done) | copy-start | bytes 3145732
  178.6 3.8 %copy-start.6 = (bf16[2,4,4,32,512]{4,3,0,1,2:T(8,128)(2,1)S(1)}, bf16[2,4,4,32,512]{4,3,0,1,2:T(8,128)(2,1)}, u32[]{:S(2)}) copy-start(bf16[2,4,4,32,512]{4,3,0,1,2:T(8,128)(2,1)} %rev.4) | copy-start | bytes 3145732
  178.6 31.6 %all-to-all-start.2 = ((bf16[16,8,4096]{2,1,0:T(8,128)(2,1)}), bf16[16,8,4096]{2,1,0:T(8,128)(2,1)S(1)}, u32[]{:S(2)}, u32[]{:S(2)}) async-start(bf16[16,8,4096]{2,1,0:T(8,128)(2,1)} %bitcast.42), calls=%async_computation.2 | async-start | bytes 2097152 | tf_op jit(solution)/shard_map/all_to_all | solution.py:42
  210.2 1.6 copy-start.3
  210.2 1.9 copy-start.7
  210.4 3.3 %copy-start.1 = (bf16[1,2048,512]{2,1,0:T(8,128)(2,1)S(1)}, bf16[1,2048,512]{2,1,0:T(8,128)(2,1)}, u32[]{:S(2)}) copy-start(bf16[1,2048,512]{2,1,0:T(8,128)(2,1)} %param.9) | copy-start | bytes 6291460
Sparse Core Ops, SparseCore 0:
  10.6 29.5 all-gather.4
Sparse Core Ops, SparseCore 1:
  114.0 39.5 all-gather.6

commit v3 on v2

--- a/solution.py
+++ b/solution.py
@@ -72,12 +72,19 @@
         weight,
         preferred_element_type=jnp.float32,
     ).astype(jnp.bfloat16)
-    got = lax.all_to_all(part, ("dp", "tensor"), 0, 0, tiled=True)
-    got = got.reshape(n_dp, n_t, mb, tok_dev, rows_p).astype(jnp.float32)
-    normed_grad = got[:, 0]
-    for t in range(1, n_t):
-        normed_grad = normed_grad + got[:, t]
-    normed_grad = normed_grad.transpose(1, 2, 0, 3).reshape(mb, tok_dev, d_model)
+    part = part.reshape(n_dp, n_t // 2, 2, mb, tok_dev, rows_p)
+    my_core = my_t % 2
+    my_hi = my_t // 2
+    keep = lax.dynamic_index_in_dim(part, my_core, 2, False)
+    send = lax.dynamic_index_in_dim(part, 1 - my_core, 2, False)
+    recv = lax.ppermute(send, "tensor", [(q, q ^ 1) for q in range(n_t)])
+    pair = keep.astype(jnp.float32) + recv.astype(jnp.float32)
+    keep = lax.dynamic_index_in_dim(pair, my_hi, 1, False)
+    send = lax.dynamic_index_in_dim(pair, 1 - my_hi, 1, False)
+    recv = lax.ppermute(send, "tensor", [(q, q ^ 2) for q in range(n_t)])
+    total = (keep + recv).astype(jnp.bfloat16)
+    got = lax.all_to_all(total, "dp", 0, 0, tiled=True)
+    normed_grad = got.astype(jnp.float32).transpose(1, 2, 0, 3).reshape(mb, tok_dev, d_model)
 
     hidden_gradient = normed_grad * gain_float
     branch_path = inverse_scale * (

time: 222 us -> 232 us (1.045)
  the two profiles are of different devices: /device:TPU:4 before, /device:TPU:1 now
where the time goes in v3:
time: 232 us; the launch traced here: 228 us
  waiting for transfers between devices  111 us (48%)
  local copies, waits for them, and re-layouts  29.7 us (13%)
  starting transfers between devices  27.3 us (12%)
  other arithmetic  25.6 us (11%)
  matrix products  17.2 us (7%)
  between operations  17.1 us (7%)
    ppermute x1, waiting for transfers between devices, body(): recv = lax.ppermute(send, 'tensor', [(q, q ^ 2) for q in range(n_t)])  36.3 us
    all_gather x1, waiting for transfers between devices, body(): cotan_all = lax.all_gather(cotan, 'dp', axis=1, tiled=True)  30.2 us
    all_to_all x1, waiting for transfers between devices, later_sum(): got = lax.all_to_all(chunks, 'section', 0, 0, tiled=True)  18.1 us
    dot_general x1, matrix products, body(): jnp.einsum('tkmid,mktic->kdc', nrm, cot_sel, preferred_element_type=jnp.f...  13.2 us
    ppermute x3, waiting for transfers between devices, body(): lax.ppermute(send, 'dp', [(q, (q + k) % n_dp) for q in range(n_dp)])  10.4 us
    all_to_all x1, starting transfers between devices, later_sum(): got = lax.all_to_all(chunks, 'section', 0, 0, tiled=True)  7.26 us
    all_to_all x1, starting transfers between devices, later_sum(): lax.all_to_all(suffix.astype(jnp.bfloat16).reshape(n_sec, 8, w), 'section...  6.7 us
    all_to_all x1, waiting for transfers between devices, later_sum(): lax.all_to_all(suffix.astype(jnp.bfloat16).reshape(n_sec, 8, w), 'section...  6.23 us
  transfers between devices with their start and end apart: 10, of which 9 were waited for; matrix products, arithmetic and copies ran while one was open for 25% of the time, Pallas kernels for 0%

profile of v3, /device:TPU:1, one launch (start us, length us, event | category | flops | bytes accessed | tf_op | source)
XLA Modules:
  0.0 227.9 jit_solution(5840091944875353045)
XLA Ops:
  8.8 30.2 %all-gather.5.cloned.1.call-done = bf16[1,2,512,512]{3,2,1,0:T(8,128)(2,1)} async-done(((bf16[1,2,128,512]{3,2,1,0:T(8,128)(2,1)}), bf16[1,2,512,512]{3,2,1,0:T(8,128)(2,1)}) %all-gather.5.cloned.1.call-update) | async-done | bytes 1048592 | tf_op jit(solution)/shard_map/all_gather | solution.py:68
  39.1 3.6 %convolution_convert_fusion.1 = bf16[2048,2,16,32]{0,3,2,1:T(8,128)(2,1)S(1)} fusion(bf16[2,16,32,512]{3,2,1,0:T(8,128)(2,1)} %bitcast.92, bf16[1,2048,512]{2,1,0:T(8,128)(2,1)S(1)} %copy-done), kind=kOutput, calls=%fused_computation.17 | convolution fusion | flops 2149580800 | bytes 7340032 | tf_op jit(solution)/shard_map/mjik,dk->jmid/dot_general | solution.py:69
  46.1 2.8 %collective-permute-start = (bf16[4,2,2,32,2048]{4,3,2,0,1:T(8,128)(2,1)}, bf16[4,2,2,32,2048]{4,3,2,0,1:T(8,128)(2,1)S(1)}, u32[]{:S(2)}, u32[]{:S(2)}) collective-permute-start(bf16[4,2,2,32,2048]{4,3,2,0,1:T(8,128)(2,1)} %bitcast.78), channel_id=1, source_target_pairs={{0,1},{1,0},{2,3},{3,2},{4,5},{5,4},{6,7},{7,6},{8,9},{9,8},{10,11... | collective-permute-start | bytes 6291464 | tf_op jit(solution)/shard_map/ppermute | solution.py:80
  49.3 3.5 %collective-permute-done = bf16[4,2,2,32,2048]{4,3,2,0,1:T(8,128)(2,1)S(1)} collective-permute-done((bf16[4,2,2,32,2048]{4,3,2,0,1:T(8,128)(2,1)}, bf16[4,2,2,32,2048]{4,3,2,0,1:T(8,128)(2,1)S(1)}, u32[]{:S(2)}, u32[]{:S(2)}) %collective-permute-start) | collective-permute-done | bytes 2097184 | tf_op jit(solution)/shard_map/ppermute | solution.py:80
  57.9 2.7 %collective-permute-start.1 = (f32[4,2,32,2048]{3,2,1,0:T(8,128)}, f32[4,2,32,2048]{3,2,1,0:T(8,128)}, u32[]{:S(2)}, u32[]{:S(2)}) collective-permute-start(f32[4,2,32,2048]{3,2,1,0:T(8,128)} %dynamic-slice_bitcast_fusion), channel_id=1, source_target_pairs={{0,2},{1,3},{2,0},{3,1},{4,6},{5,7},{6,4},{7,5},{8,10},{9,11},{10,... | collective-permute-start | bytes 6291464 | tf_op jit(solution)/shard_map/ppermute | solution.py:84
  64.5 2.5 %collective-permute-start.3 = (bf16[2,32,2048]{2,1,0:T(8,128)(2,1)S(1)}, bf16[2,32,2048]{2,1,0:T(8,128)(2,1)S(1)}, u32[]{:S(2)}, u32[]{:S(2)}) collective-permute-start(bf16[2,32,2048]{2,1,0:T(8,128)(2,1)S(1)} %bitcast.96), channel_id=1, source_target_pairs={{0,128},{64,192},{128,0},{192,64},{1,129},{65,193},{129,1},{193,65... | collective-permute-start | bytes 786440 | tf_op jit(solution)/shard_map/ppermute | solution.py:106
  68.8 4.3 %collective-permute-done.2 = bf16[2,32,2048]{2,1,0:T(8,128)(2,1)S(1)} collective-permute-done((bf16[2,32,2048]{2,1,0:T(8,128)(2,1)S(1)}, bf16[2,32,2048]{2,1,0:T(8,128)(2,1)S(1)}, u32[]{:S(2)}, u32[]{:S(2)}) %collective-permute-start.2) | collective-permute-done | bytes 262176 | tf_op jit(solution)/shard_map/ppermute | solution.py:106
  73.1 5.2 %collective-permute-done.3 = bf16[2,32,2048]{2,1,0:T(8,128)(2,1)S(1)} collective-permute-done((bf16[2,32,2048]{2,1,0:T(8,128)(2,1)S(1)}, bf16[2,32,2048]{2,1,0:T(8,128)(2,1)S(1)}, u32[]{:S(2)}, u32[]{:S(2)}) %collective-permute-start.3) | collective-permute-done | bytes 262176 | tf_op jit(solution)/shard_map/ppermute | solution.py:106
  80.4 36.3 %collective-permute-done.1 = f32[4,2,32,2048]{3,2,1,0:T(8,128)} collective-permute-done((f32[4,2,32,2048]{3,2,1,0:T(8,128)}, f32[4,2,32,2048]{3,2,1,0:T(8,128)}, u32[]{:S(2)}, u32[]{:S(2)}) %collective-permute-start.1) | collective-permute-done | bytes 2097184 | tf_op jit(solution)/shard_map/ppermute | solution.py:84
  116.7 3.5 %fusion.21 = bf16[4,2,32,2048]{3,2,1,0:T(8,128)(2,1)} fusion(f32[4,2,32,2048]{3,2,1,0:T(8,128)} %collective-permute-done.1, f32[4,2,2,32,2048]{4,3,2,0,1:T(8,128)} %copy-done.3, s32[]{:T(128)S(6)} %select_n.67), kind=kLoop, calls=%fused_computation.39 | loop fusion | flops 1048576 | bytes 5242884 | tf_op jit(solution)/shard_map/convert_element_type | solution.py:85
  120.2 3.7 %all-to-all-start = ((bf16[4,2,32,2048]{3,2,1,0:T(8,128)(2,1)}), bf16[4,2,32,2048]{3,2,1,0:T(8,128)(2,1)S(1)}, u32[]{:S(2)}, u32[]{:S(2)}) async-start(bf16[4,2,32,2048]{3,2,1,0:T(8,128)(2,1)} %fusion.21), calls=%async_computation | async-start | bytes 2097152 | tf_op jit(solution)/shard_map/all_to_all | solution.py:86
  123.9 2.7 %reshape.165 = f32[2,32,4,2048]{3,2,1,0:T(4,128)} reshape(bf16[1,2,32,8192]{3,2,1,0:T(8,128)(2,1)S(1)} %copy-done.2) | data formatting | bytes 3145728 | tf_op jit(solution)/shard_map/convert_element_type | solution.py:63
  126.5 3.1 %reshape.167 = f32[2,4,8,2,4096]{4,3,2,1,0:T(2,128)} reshape(bf16[1,2,32,8192]{3,2,1,0:T(8,128)(2,1)S(1)} %copy-done.2) | data formatting | bytes 3145728 | tf_op jit(solution)/shard_map/convert_element_type | solution.py:63
  130.2 5.5 %all-to-all-done = bf16[4,2,32,2048]{3,2,1,0:T(8,128)(2,1)S(1)} async-done(((bf16[4,2,32,2048]{3,2,1,0:T(8,128)(2,1)}), bf16[4,2,32,2048]{3,2,1,0:T(8,128)(2,1)S(1)}, u32[]{:S(2)}, u32[]{:S(2)}) %all-to-all-start) | async-done | bytes 1048608 | tf_op jit(solution)/shard_map/all_to_all | solution.py:86
  137.2 2.7 %copy.29 = f32[2,32,4,2048]{3,2,1,0:T(4,128)} copy(f32[2,32,4,2048]{3,1,0,2:T(8,128)S(1)} %get-tuple-element.13) | data formatting | bytes 4194304 | tf_op jit(solution)/shard_map/transpose | solution.py:87
  139.9 4.2 %reshape.157 = f32[2,4,8,2,4096]{4,3,2,1,0:T(2,128)} reshape(f32[2,32,4,2048]{3,2,1,0:T(4,128)} %copy.29) | data formatting | bytes 4194304 | tf_op jit(solution)/shard_map/reshape | solution.py:87
  144.1 2.9 %fusion.23 = f32[2,32]{1,0:T(2,128)S(1)} fusion(f32[2,32,4,2048]{3,2,1,0:T(4,128)} %reshape.165, f32[2,32]{1,0:T(2,128)S(1)} %add_rsqrt_fusion.1, f32[4,2048]{1,0:T(4,128)S(1)} %reshape.164, bf16[4,2,32,2048]{3,2,1,0:T(8,128)(2,1)S(1)} %all-to-all-done), kind=kLoop, calls=%fused_computation.42 | loop fusion | flops 2621376 | bytes 3179008 | tf_op jit(solution)/shard_map/reduce_sum | solution.py:92
  147.1 3.9 %fusion.27 = bf16[2,4,2,8,4096]{4,2,3,1,0:T(2,128)(2,1)S(1)} fusion(f32[2,4,8]{2,1,0:T(4,128)S(1)} %div.24, f32[2,4,8,2,4096]{4,3,2,1,0:T(2,128)} %reshape.167, f32[2,4,8,2,4096]{4,3,2,1,0:T(2,128)} %reshape.157, f32[2,4096]{1,0:T(2,128)S(1)} %reshape.166, f32[2,4,8]{2,1,0:T(4,128)S(1)} %rsqrt.21), kind=kLoop, calls=%fused_computation.49 | loop fusion | flops 3145728 | bytes 5276160 | tf_op jit(solution)/shard_map/transpose | solution.py:35
  152.5 7.3 %all-to-all-start.1 = ((bf16[16,8,4096]{2,1,0:T(8,128)(2,1)}), bf16[16,8,4096]{2,1,0:T(8,128)(2,1)S(1)}, u32[]{:S(2)}, u32[]{:S(2)}) async-start(bf16[16,8,4096]{2,1,0:T(8,128)(2,1)} %bitcast.14), calls=%async_computation.1 | async-start | bytes 2097152 | tf_op jit(solution)/shard_map/all_to_all | solution.py:36
  164.8 18.1 %all-to-all-done.1 = bf16[16,8,4096]{2,1,0:T(8,128)(2,1)S(1)} async-done(((bf16[16,8,4096]{2,1,0:T(8,128)(2,1)}), bf16[16,8,4096]{2,1,0:T(8,128)(2,1)S(1)}, u32[]{:S(2)}, u32[]{:S(2)}) %all-to-all-start.1) | async-done | bytes 1048608 | tf_op jit(solution)/shard_map/all_to_all | solution.py:36
  185.5 6.7 %all-to-all-start.2 = ((bf16[16,8,4096]{2,1,0:T(8,128)(2,1)}), bf16[16,8,4096]{2,1,0:T(8,128)(2,1)}, u32[]{:S(2)}, u32[]{:S(2)}) async-start(bf16[16,8,4096]{2,1,0:T(8,128)(2,1)} %bitcast.47), calls=%async_computation.2 | async-start | bytes 2097152 | tf_op jit(solution)/shard_map/all_to_all | solution.py:42
  192.2 13.2 %fusion.9 = bf16[4,2048,512]{2,1,0:T(8,128)(2,1)S(1)} fusion(s32[4]{0:T(128)S(1)} %fusion.29, s32[2048,512]{1,0:T(8,128)} %add_add_fusion, bf16[4,4,2,32,2048]{4,3,2,1,0:T(8,128)(2,1)} %bitcast.102, s32[]{:T(128)S(6)} %select_n.76, bf16[2,4,4,32,512]{4,3,0,1,2:T(8,128)(2,1)S(1)} %copy-done.7), kind=kOutput, calls=%fused_computation.14 | convolution fusion | flops 2219311104 | bytes 17825812 | tf_op jit(solution)/shard_map/tkmid,mktic->kdc/dot_general | solution.py:120
  205.4 3.4 %convert_reduce_fusion = f32[2048,512]{1,0:T(8,128)} fusion(bf16[4,2048,512]{2,1,0:T(8,128)(2,1)S(1)} %fusion.9), kind=kLoop, calls=%fused_computation.13 | loop fusion | flops 7340032 | bytes 12582912 | tf_op jit(solution)/shard_map/reduce_sum | solution.py:122
  210.4 6.2 %all-to-all-done.2 = bf16[16,8,4096]{2,1,0:T(8,128)(2,1)} async-done(((bf16[16,8,4096]{2,1,0:T(8,128)(2,1)}), bf16[16,8,4096]{2,1,0:T(8,128)(2,1)}, u32[]{:S(2)}, u32[]{:S(2)}) %all-to-all-start.2) | async-done | bytes 1048608 | tf_op jit(solution)/shard_map/all_to_all | solution.py:42
  (66 shorter events, 32.9 us)
Async XLA Ops:
  8.0 31.1 %copy-start = (bf16[1,2048,512]{2,1,0:T(8,128)(2,1)S(1)}, bf16[1,2048,512]{2,1,0:T(8,128)(2,1)}, u32[]{:S(2)}) copy-start(bf16[1,2048,512]{2,1,0:T(8,128)(2,1)} %param.9) | copy-start | bytes 6291460
  8.0 31.0 %all-gather.5.cloned.1.call-start = ((), (), s32[]{:S(2)}) async-start(), calls=%async_computation.3 | async-start | bytes 1310720 | tf_op jit(solution)/shard_map/all_gather | solution.py:68
  8.7 183.5 %all-gather.7.cloned.1.call-start = ((), (), s32[]{:S(2)}) async-start(), calls=%async_computation.4 | async-start | bytes 5242880 | tf_op jit(solution)/shard_map/all_gather | solution.py:108
  44.5 4.3 %copy-start.9 = (bf16[1,8192]{1,0:T(2,128)(2,1)S(1)}, bf16[1,8192]{1,0:T(2,128)(2,1)}, u32[]{:S(2)}) copy-start(bf16[1,8192]{1,0:T(2,128)(2,1)} %param.10) | copy-start | bytes 49156
  44.5 4.5 %copy-start.2 = (bf16[1,2,32,8192]{3,2,1,0:T(8,128)(2,1)S(1)}, bf16[1,2,32,8192]{3,2,1,0:T(8,128)(2,1)}, u32[]{:S(2)}) copy-start(bf16[1,2,32,8192]{3,2,1,0:T(8,128)(2,1)} %param.7) | copy-start | bytes 3145732
  46.1 6.7 %collective-permute-start = (bf16[4,2,2,32,2048]{4,3,2,0,1:T(8,128)(2,1)}, bf16[4,2,2,32,2048]{4,3,2,0,1:T(8,128)(2,1)S(1)}, u32[]{:S(2)}, u32[]{:S(2)}) collective-permute-start(bf16[4,2,2,32,2048]{4,3,2,0,1:T(8,128)(2,1)} %bitcast.78), channel_id=1, source_target_pairs={{0,1},{1,0},{2,3},{3,2},{4,5},{5,4},{6,7},{7,6},{8,9},{9,8},{10,11... | collective-permute-start | bytes 6291464 | tf_op jit(solution)/shard_map/ppermute | solution.py:80
  55.2 2.6 %copy-start.3 = (f32[4,2,2,32,2048]{4,3,2,0,1:T(8,128)}, f32[4,2,2,32,2048]{4,3,2,0,1:T(8,128)S(1)}, u32[]{:S(2)}) copy-start(f32[4,2,2,32,2048]{4,3,2,0,1:T(8,128)S(1)} %convert_add_fusion) | copy-start | bytes 12582916
  57.9 58.8 %collective-permute-start.1 = (f32[4,2,32,2048]{3,2,1,0:T(8,128)}, f32[4,2,32,2048]{3,2,1,0:T(8,128)}, u32[]{:S(2)}, u32[]{:S(2)}) collective-permute-start(f32[4,2,32,2048]{3,2,1,0:T(8,128)} %dynamic-slice_bitcast_fusion), channel_id=1, source_target_pairs={{0,2},{1,3},{2,0},{3,1},{4,6},{5,7},{6,4},{7,5},{8,10},{9,11},{10,... | collective-permute-start | bytes 6291464 | tf_op jit(solution)/shard_map/ppermute | solution.py:84
  64.3 8.8 %collective-permute-start.2 = (bf16[2,32,2048]{2,1,0:T(8,128)(2,1)S(1)}, bf16[2,32,2048]{2,1,0:T(8,128)(2,1)S(1)}, u32[]{:S(2)}, u32[]{:S(2)}) collective-permute-start(bf16[2,32,2048]{2,1,0:T(8,128)(2,1)S(1)} %bitcast.95), channel_id=1, source_target_pairs={{0,64},{64,128},{128,192},{192,0},{1,65},{65,129},{129,193},{193,1... | collective-permute-start | bytes 786440 | tf_op jit(solution)/shard_map/ppermute | solution.py:106
  64.5 13.8 %collective-permute-start.3 = (bf16[2,32,2048]{2,1,0:T(8,128)(2,1)S(1)}, bf16[2,32,2048]{2,1,0:T(8,128)(2,1)S(1)}, u32[]{:S(2)}, u32[]{:S(2)}) collective-permute-start(bf16[2,32,2048]{2,1,0:T(8,128)(2,1)S(1)} %bitcast.96), channel_id=1, source_target_pairs={{0,128},{64,192},{128,0},{192,64},{1,129},{65,193},{129,1},{193,65... | collective-permute-start | bytes 786440 | tf_op jit(solution)/shard_map/ppermute | solution.py:106
  67.2 12.0 %collective-permute-start.4 = (bf16[2,32,2048]{2,1,0:T(8,128)(2,1)S(1)}, bf16[2,32,2048]{2,1,0:T(8,128)(2,1)S(1)}, u32[]{:S(2)}, u32[]{:S(2)}) collective-permute-start(bf16[2,32,2048]{2,1,0:T(8,128)(2,1)S(1)} %bitcast.97), channel_id=1, source_target_pairs={{0,192},{64,0},{128,64},{192,128},{1,193},{65,1},{129,65},{193,129... | collective-permute-start | bytes 786440 | tf_op jit(solution)/shard_map/ppermute | solution.py:106
  120.2 15.5 %all-to-all-start = ((bf16[4,2,32,2048]{3,2,1,0:T(8,128)(2,1)}), bf16[4,2,32,2048]{3,2,1,0:T(8,128)(2,1)S(1)}, u32[]{:S(2)}, u32[]{:S(2)}) async-start(bf16[4,2,32,2048]{3,2,1,0:T(8,128)(2,1)} %fusion.21), calls=%async_computation | async-start | bytes 2097152 | tf_op jit(solution)/shard_map/all_to_all | solution.py:86
  152.5 30.4 %all-to-all-start.1 = ((bf16[16,8,4096]{2,1,0:T(8,128)(2,1)}), bf16[16,8,4096]{2,1,0:T(8,128)(2,1)S(1)}, u32[]{:S(2)}, u32[]{:S(2)}) async-start(bf16[16,8,4096]{2,1,0:T(8,128)(2,1)} %bitcast.14), calls=%async_computation.1 | async-start | bytes 2097152 | tf_op jit(solution)/shard_map/all_to_all | solution.py:36
  161.1 2.5 %copy-start.6 = (bf16[1,2,512,512]{3,2,1,0:T(8,128)(2,1)S(1)}, bf16[1,2,512,512]{3,2,1,0:T(8,128)(2,1)}, u32[]{:S(2)}) copy-start(bf16[1,2,512,512]{3,2,1,0:T(8,128)(2,1)} %all-gather.5.cloned.1.call-done) | copy-start | bytes 3145732
  183.9 8.3 %copy-start.7 = (bf16[2,4,4,32,512]{4,3,0,1,2:T(8,128)(2,1)S(1)}, bf16[2,4,4,32,512]{4,3,0,1,2:T(8,128)(2,1)}, u32[]{:S(2)}) copy-start(bf16[2,4,4,32,512]{4,3,0,1,2:T(8,128)(2,1)} %rev.4) | copy-start | bytes 3145732
  185.5 31.1 %all-to-all-start.2 = ((bf16[16,8,4096]{2,1,0:T(8,128)(2,1)}), bf16[16,8,4096]{2,1,0:T(8,128)(2,1)}, u32[]{:S(2)}, u32[]{:S(2)}) async-start(bf16[16,8,4096]{2,1,0:T(8,128)(2,1)} %bitcast.47), calls=%async_computation.2 | async-start | bytes 2097152 | tf_op jit(solution)/shard_map/all_to_all | solution.py:42
  205.4 3.4 %copy-start.4 = (f32[4,2,4,8,2048]{4,3,2,1,0:T(8,128)S(1)}, f32[4,2,4,8,2048]{4,3,2,1,0:T(8,128)}, u32[]{:S(2)}) copy-start(f32[4,2,4,8,2048]{4,3,2,1,0:T(8,128)} %get-tuple-element.12) | copy-start | bytes 6291460
  216.6 1.9 copy-start.5
  216.6 2.2 copy-start.8
  218.2 2.3 copy-start.1
Sparse Core Ops, SparseCore 0:
  10.6 28.3 all-gather.4
Sparse Core Ops, SparseCore 1:
  80.4 50.9 all-gather.6

commit v4 on v3

--- a/solution.py
+++ b/solution.py
@@ -54,6 +54,8 @@
     n_t = lax.axis_size("tensor")
     my_p = lax.axis_index("dp")
     my_t = lax.axis_index("tensor")
+    my_core = my_t % 2
+    my_hi = my_t // 2
     cotan = kv_grad[0]
     weight = kv_weight[0]
     rows_p, width_t = weight.shape
@@ -65,7 +67,15 @@
     centered_input = input_float * inverse_scale
     gain_float = norm_gain[0].astype(jnp.float32)
 
-    cotan_all = lax.all_gather(cotan, "dp", axis=1, tiled=True)
+    kv_pieces = [cotan]
+    for k in range(1, n_dp):
+        kv_pieces.append(
+            lax.ppermute(cotan, "dp", [(q, (q + k) % n_dp) for q in range(n_dp)])
+        )
+    kv_sel = jnp.stack(kv_pieces)
+    kv_rev = jnp.concatenate([kv_sel[::-1], kv_sel[::-1]], axis=0)
+    cotan_all = lax.dynamic_slice_in_dim(kv_rev, n_dp - 1 - my_p, n_dp, axis=0)
+    cotan_all = cotan_all.transpose(1, 0, 2, 3).reshape(mb, n_dp * cotan.shape[1], width_t)
     part = jnp.einsum(
         "mjik,dk->jmid",
         cotan_all.reshape(mb, n_dp * n_t, tok_dev, width_t),
@@ -73,16 +83,14 @@
         preferred_element_type=jnp.float32,
     ).astype(jnp.bfloat16)
     part = part.reshape(n_dp, n_t // 2, 2, mb, tok_dev, rows_p)
-    my_core = my_t % 2
-    my_hi = my_t // 2
     keep = lax.dynamic_index_in_dim(part, my_core, 2, False)
     send = lax.dynamic_index_in_dim(part, 1 - my_core, 2, False)
     recv = lax.ppermute(send, "tensor", [(q, q ^ 1) for q in range(n_t)])
-    pair = keep.astype(jnp.float32) + recv.astype(jnp.float32)
+    pair = (keep.astype(jnp.float32) + recv.astype(jnp.float32)).astype(jnp.bfloat16)
     keep = lax.dynamic_index_in_dim(pair, my_hi, 1, False)
     send = lax.dynamic_index_in_dim(pair, 1 - my_hi, 1, False)
     recv = lax.ppermute(send, "tensor", [(q, q ^ 2) for q in range(n_t)])
-    total = (keep + recv).astype(jnp.bfloat16)
+    total = (keep.astype(jnp.float32) + recv.astype(jnp.float32)).astype(jnp.bfloat16)
     got = lax.all_to_all(total, "dp", 0, 0, tiled=True)
     normed_grad = got.astype(jnp.float32).transpose(1, 2, 0, 3).reshape(mb, tok_dev, d_model)
 
@@ -105,10 +113,14 @@
         pieces.append(
             lax.ppermute(send, "dp", [(q, (q + k) % n_dp) for q in range(n_dp)])
         )
-    nrm = lax.all_gather(jnp.stack(pieces), "tensor", axis=0, tiled=False)
-    cot = cotan_all.reshape(mb, n_dp, n_t, tok_dev, width_t)
-    cot_rev = jnp.concatenate([cot[:, ::-1], cot[:, ::-1]], axis=1)
-    cot_sel = lax.dynamic_slice_in_dim(cot_rev, n_dp - 1 - my_p, n_dp, axis=1)
+    mine = jnp.stack(pieces)
+    far = lax.ppermute(mine, "tensor", [(q, q ^ 2) for q in range(n_t)])
+    on_chip = jnp.stack([mine, far])
+    hi_order = jnp.where(my_hi == 0, on_chip, on_chip[::-1])
+    other = lax.ppermute(hi_order, "tensor", [(q, q ^ 1) for q in range(n_t)])
+    both = jnp.where(my_core == 0, jnp.stack([hi_order, other]), jnp.stack([other, hi_order]))
+    nrm = both.transpose(1, 0, 2, 3, 4, 5).reshape((n_t,) + mine.shape)
+    cot_sel = kv_sel.reshape(n_dp, mb, n_t, tok_dev, width_t).transpose(1, 0, 2, 3, 4)
     groups = (my_p - jnp.arange(n_dp, dtype=jnp.int32)) % n_dp
 
     row_ids = my_p * jnp.int32(rows_p) + jnp.arange(rows_p, dtype=jnp.int32)

time: 232 us -> 192 us (0.83)
  waiting for transfers between devices: 111 us -> 57.3 us
  between operations: 17.1 us -> 2.31 us
  other arithmetic: 25.6 us -> 39.3 us
  starting transfers between devices: 27.3 us -> 38 us
  local copies, waits for them, and re-layouts: 29.7 us -> 35.5 us
    all_gather x2 -> x0, waiting for transfers between devices: 30.3 us -> none  [the longest x1 30.2 us: body(): cotan_all = lax.all_gather(cotan, 'dp', axis=1, tiled=True)]
    ppermute x1, waiting for transfers between devices: 36.3 us -> 7.37 us  [body(): recv = lax.ppermute(send, 'tensor', [(q, q ^ 2) for q in range(n_t)])]
    ppermute x0 -> x5, waiting for transfers between devices: none -> 23.5 us  [the longest x1 15.6 us: body(): far = lax.ppermute(mine, 'tensor', [(q, q ^ 2) for q in range(n_t)])]
    ppermute x0 -> x5, starting transfers between devices: none -> 10.3 us  [the longest x3 5.88 us: body(): lax.ppermute(cotan, 'dp', [(q, (q + k) % n_dp) for q in range(n_dp)])]
    ppermute x3, waiting for transfers between devices: 10.4 us -> 3.85 us  [body(): lax.ppermute(send, 'dp', [(q, (q + k) % n_dp) for q in range(n_dp)])]
    another operation x1 -> x4, other arithmetic: 1.11 us -> 6.82 us  [the longest x2 4.29 us: body(): on_chip = jnp.stack([mine, far])]
    all_to_all x1, waiting for transfers between devices: 5.47 us -> 0.01 us  [body(): got = lax.all_to_all(total, 'dp', 0, 0, tiled=True)]
    ppermute x1, waiting for transfers between devices: 3.52 us -> 0.01 us  [body(): recv = lax.ppermute(send, 'tensor', [(q, q ^ 1) for q in range(n_t)])]
  transfers between devices with their start and end apart: 10 -> 13, of which waited for: 9 -> 7; matrix products, arithmetic and copies ran while one was open for 25% -> 39% of each run, Pallas kernels for 0% -> 0%
where the time goes in v4:
time: 192 us; the launch traced here: 189 us
  waiting for transfers between devices  57.3 us (30%)
  other arithmetic  39.3 us (20%)
  starting transfers between devices  38 us (20%)
  local copies, waits for them, and re-layouts  35.5 us (18%)
  matrix products  16.5 us (9%)
  between operations  2.31 us (1%)
    all_to_all x1, waiting for transfers between devices, later_sum(): got = lax.all_to_all(chunks, 'section', 0, 0, tiled=True)  16.7 us
    ppermute x1, waiting for transfers between devices, body(): far = lax.ppermute(mine, 'tensor', [(q, q ^ 2) for q in range(n_t)])  15.6 us
    dot_general x1, matrix products, body(): jnp.einsum('tkmid,mktic->kdc', nrm, cot_sel, preferred_element_type=jnp.f...  13.7 us
    all_to_all x1, starting transfers between devices, later_sum(): got = lax.all_to_all(chunks, 'section', 0, 0, tiled=True)  9.27 us
    ppermute x3, waiting for transfers between devices, body(): lax.ppermute(cotan, 'dp', [(q, (q + k) % n_dp) for q in range(n_dp)])  7.95 us
    unnamed x42, local copies, waits for them, and re-layouts  7.49 us
    ppermute x1, waiting for transfers between devices, body(): recv = lax.ppermute(send, 'tensor', [(q, q ^ 2) for q in range(n_t)])  7.37 us
    ppermute x3, starting transfers between devices, body(): lax.ppermute(cotan, 'dp', [(q, (q + k) % n_dp) for q in range(n_dp)])  5.88 us
  transfers between devices with their start and end apart: 13, of which 7 were waited for; matrix products, arithmetic and copies ran while one was open for 39% of the time, Pallas kernels for 0%

profile of v4, /device:TPU:1, one launch (start us, length us, event | category | flops | bytes accessed | tf_op | source)
XLA Modules:
  0.0 188.8 jit_solution(12251862644938677976)
XLA Ops:
  2.8 2.6 %collective-permute-start.1 = (bf16[2,128,512]{2,1,0:T(8,128)(2,1)}, bf16[2,128,512]{2,1,0:T(8,128)(2,1)S(1)}, u32[]{:S(2)}, u32[]{:S(2)}) collective-permute-start(bf16[2,128,512]{2,1,0:T(8,128)(2,1)} %bitcast.116), channel_id=1, source_target_pairs={{0,128},{64,192},{128,0},{192,64},{1,129},{65,193},{129,1},{193,65... | collective-permute-start | bytes 786440 | tf_op jit(solution)/shard_map/ppermute | solution.py:73
  9.1 7.9 %collective-permute-done.1 = bf16[2,128,512]{2,1,0:T(8,128)(2,1)S(1)} collective-permute-done((bf16[2,128,512]{2,1,0:T(8,128)(2,1)}, bf16[2,128,512]{2,1,0:T(8,128)(2,1)S(1)}, u32[]{:S(2)}, u32[]{:S(2)}) %collective-permute-start.1) | collective-permute-done | bytes 262176 | tf_op jit(solution)/shard_map/ppermute | solution.py:73
  30.2 3.2 %constant_dynamic-slice_fusion.3 = (bf16[2,32,1,2048]{3,2,1,0:T(2,128)(2,1)}, bf16[2,32,1,2048]{3,2,1,0:T(2,128)(2,1)S(1)}, bf16[2,32,1,2048]{3,2,1,0:T(2,128)(2,1)S(1)}, bf16[2,32,1,2048]{3,2,1,0:T(2,128)(2,1)S(1)}) fusion(bf16[2,32,4,2048]{3,2,1,0:T(4,128)(2,1)S(1)} %reshape.167, s32[]{:T(128)S(6)} %select_n.88, s32[]{:T(128)S(6)} %select_n.94, ...), kind=kLoop, calls=%fused_computation.69 | loop fusion | bytes 2097168 | tf_op jit(solution)/shard_map/jit(dynamic_index_in_dim)/dynamic_slice | solution.py:110
  43.6 2.7 %collective-permute-start.4 = (bf16[4,2,32,2048]{3,2,1,0:T(8,128)(2,1)}, bf16[4,2,32,2048]{3,2,1,0:T(8,128)(2,1)}, u32[]{:S(2)}, u32[]{:S(2)}) collective-permute-start(bf16[4,2,32,2048]{3,2,1,0:T(8,128)(2,1)} %dynamic-slice_bitcast_fusion), channel_id=1, source_target_pairs={{0,2},{1,3},{2,0},{3,1},{4,6},{5,7},{6,4},{7,5},{8,10},{9,11},{10,... | collective-permute-start | bytes 3145736 | tf_op jit(solution)/shard_map/ppermute | solution.py:92
  46.5 3.0 %collective-permute-done.6 = bf16[2,32,2048]{2,1,0:T(8,128)(2,1)} collective-permute-done((bf16[2,32,2048]{2,1,0:T(8,128)(2,1)}, bf16[2,32,2048]{2,1,0:T(8,128)(2,1)}, u32[]{:S(2)}, u32[]{:S(2)}) %collective-permute-start.6) | collective-permute-done | bytes 262176 | tf_op jit(solution)/shard_map/ppermute | solution.py:114
  52.9 2.7 %collective-permute-start.8 = (bf16[4,2,32,2048]{3,2,1,0:T(8,128)(2,1)}, bf16[4,2,32,2048]{3,2,1,0:T(8,128)(2,1)}, u32[]{:S(2)}, u32[]{:S(2)}) collective-permute-start(bf16[4,2,32,2048]{3,2,1,0:T(8,128)(2,1)} %get-tuple-element.9), channel_id=1, source_target_pairs={{0,2},{1,3},{2,0},{3,1},{4,6},{5,7},{6,4},{7,5},{8,10},{9,11},{10,... | collective-permute-start | bytes 3145736 | tf_op jit(solution)/shard_map/ppermute | solution.py:117
  55.7 2.6 %reshape.172 = f32[2,32,4,2048]{3,2,1,0:T(4,128)} reshape(bf16[1,2,32,8192]{3,2,1,0:T(8,128)(2,1)S(1)} %copy-done.2) | data formatting | bytes 3145728 | tf_op jit(solution)/shard_map/convert_element_type | solution.py:65
  58.3 3.0 %reshape.174 = f32[2,4,8,2,4096]{4,3,2,1,0:T(2,128)} reshape(bf16[1,2,32,8192]{3,2,1,0:T(8,128)(2,1)S(1)} %copy-done.2) | data formatting | bytes 3145728 | tf_op jit(solution)/shard_map/convert_element_type | solution.py:65
  61.9 7.4 %collective-permute-done.4 = bf16[4,2,32,2048]{3,2,1,0:T(8,128)(2,1)} collective-permute-done((bf16[4,2,32,2048]{3,2,1,0:T(8,128)(2,1)}, bf16[4,2,32,2048]{3,2,1,0:T(8,128)(2,1)}, u32[]{:S(2)}, u32[]{:S(2)}) %collective-permute-start.4) | collective-permute-done | bytes 1048608 | tf_op jit(solution)/shard_map/ppermute | solution.py:92
  69.3 2.6 %fusion.22 = bf16[4,2,32,2048]{3,2,1,0:T(8,128)(2,1)} fusion(bf16[4,2,32,2048]{3,2,1,0:T(8,128)(2,1)} %collective-permute-done.4, bf16[4,2,2,32,2048]{4,3,2,0,1:T(8,128)(2,1)S(1)} %copy-done.5, s32[]{:T(128)S(6)} %select_n.84), kind=kLoop, calls=%fused_computation.43 | loop fusion | flops 2097152 | bytes 3145732 | tf_op jit(solution)/shard_map/convert_element_type | solution.py:93
  71.9 4.3 %all-to-all-start = ((bf16[4,2,32,2048]{3,2,1,0:T(8,128)(2,1)}), bf16[4,2,32,2048]{3,2,1,0:T(8,128)(2,1)}, u32[]{:S(2)}, u32[]{:S(2)}) async-start(bf16[4,2,32,2048]{3,2,1,0:T(8,128)(2,1)} %fusion.22), calls=%async_computation | async-start | bytes 2097152 | tf_op jit(solution)/shard_map/all_to_all | solution.py:94
  76.2 15.6 %collective-permute-done.8 = bf16[4,2,32,2048]{3,2,1,0:T(8,128)(2,1)} collective-permute-done((bf16[4,2,32,2048]{3,2,1,0:T(8,128)(2,1)}, bf16[4,2,32,2048]{3,2,1,0:T(8,128)(2,1)}, u32[]{:S(2)}, u32[]{:S(2)}) %collective-permute-start.8) | collective-permute-done | bytes 1048608 | tf_op jit(solution)/shard_map/ppermute | solution.py:117
  97.1 2.9 %convert_bitcast_fusion = (f32[4,2,4,8,2048]{4,3,2,1,0:T(8,128)}, f32[2,32,4,2048]{3,1,0,2:T(8,128)S(1)}) fusion(bf16[4,2,32,2048]{3,2,1,0:T(8,128)(2,1)} %all-to-all-done), kind=kLoop, calls=%fused_computation.22 | loop fusion | flops 524288 | bytes 5242880
  100.0 2.7 %copy.41 = f32[2,32,4,2048]{3,2,1,0:T(4,128)} copy(f32[2,32,4,2048]{3,1,0,2:T(8,128)S(1)} %get-tuple-element.15) | data formatting | bytes 4194304 | tf_op jit(solution)/shard_map/transpose | solution.py:95
  102.7 4.2 %reshape.163 = f32[2,4,8,2,4096]{4,3,2,1,0:T(2,128)} reshape(f32[2,32,4,2048]{3,2,1,0:T(4,128)} %copy.41) | data formatting | bytes 4194304 | tf_op jit(solution)/shard_map/reshape | solution.py:95
  106.8 3.2 %fusion.25 = f32[2,32]{1,0:T(2,128)S(1)} fusion(f32[2,32,4,2048]{3,2,1,0:T(4,128)} %reshape.172, f32[2,32]{1,0:T(2,128)S(1)} %add_rsqrt_fusion.1, f32[4,2048]{1,0:T(4,128)S(1)} %reshape.171, bf16[4,2,32,2048]{3,2,1,0:T(8,128)(2,1)} %all-to-all-done), kind=kLoop, calls=%fused_computation.47 | loop fusion | flops 2621376 | bytes 3179008 | tf_op jit(solution)/shard_map/reduce_sum | solution.py:100
  110.1 3.9 %fusion.31 = bf16[2,4,2,8,4096]{4,2,3,1,0:T(2,128)(2,1)S(1)} fusion(f32[2,4,8]{2,1,0:T(4,128)S(1)} %div.24, f32[2,4,8,2,4096]{4,3,2,1,0:T(2,128)} %reshape.174, f32[2,4,8,2,4096]{4,3,2,1,0:T(2,128)} %reshape.163, f32[2,4096]{1,0:T(2,128)S(1)} %reshape.173, f32[2,4,8]{2,1,0:T(4,128)S(1)} %rsqrt.21), kind=kLoop, calls=%fused_computation.59 | loop fusion | flops 3145728 | bytes 5276160 | tf_op jit(solution)/shard_map/transpose | solution.py:35
  115.6 9.3 %all-to-all-start.1 = ((bf16[16,8,4096]{2,1,0:T(8,128)(2,1)}), bf16[16,8,4096]{2,1,0:T(8,128)(2,1)}, u32[]{:S(2)}, u32[]{:S(2)}) async-start(bf16[16,8,4096]{2,1,0:T(8,128)(2,1)} %bitcast.109), calls=%async_computation.1 | async-start | bytes 2097152 | tf_op jit(solution)/shard_map/all_to_all | solution.py:36
  129.1 3.0 %fusion.10 = bf16[2,2,4,2,32,2048]{5,4,3,2,0,1:T(8,128)(2,1)S(1)} fusion(bf16[1,2,4,2,32,2048]{5,4,3,2,1,0:T(8,128)(2,1)} %bitcast.30, bf16[1,2,4,2,32,2048]{5,4,3,2,1,0:T(8,128)(2,1)S(1)} %fusion.39, pred[]{:T(512)S(6)} %eq.13), kind=kLoop, calls=%fused_computation.16 | loop fusion | flops 6291456 | bytes 8388609 | tf_op jit(solution)/shard_map/transpose | solution.py:122
  134.4 16.7 %all-to-all-done.1 = bf16[16,8,4096]{2,1,0:T(8,128)(2,1)} async-done(((bf16[16,8,4096]{2,1,0:T(8,128)(2,1)}), bf16[16,8,4096]{2,1,0:T(8,128)(2,1)}, u32[]{:S(2)}, u32[]{:S(2)}) %all-to-all-start.1) | async-done | bytes 1048608 | tf_op jit(solution)/shard_map/all_to_all | solution.py:36
  154.9 5.6 %all-to-all-start.2 = ((bf16[16,8,4096]{2,1,0:T(8,128)(2,1)}), bf16[16,8,4096]{2,1,0:T(8,128)(2,1)}, u32[]{:S(2)}, u32[]{:S(2)}) async-start(bf16[16,8,4096]{2,1,0:T(8,128)(2,1)} %bitcast.62), calls=%async_computation.2 | async-start | bytes 2097152 | tf_op jit(solution)/shard_map/all_to_all | solution.py:42
  160.5 13.7 %fusion.9 = bf16[4,2048,512]{2,1,0:T(8,128)(2,1)S(1)} fusion(s32[4]{0:T(128)S(1)} %fusion.32, s32[2048,512]{1,0:T(8,128)} %add_add_fusion, bf16[4,4,2,32,2048]{4,3,2,1,0:T(8,128)(2,1)} %bitcast.107, bf16[1,2,4,32,512]{4,3,2,1,0:T(8,128)(2,1)S(1)} %bitcast.124, bf16[1,2,4,32,512]{4,3,2,1,0:T(8,128)(2,1)S(1)} %bitcast.122, ...), kind=kOutput, calls=%fused_computation.14 | convolution fusion | flops 2220359680 | bytes 17825808 | tf_op jit(solution)/shard_map/tkmid,mktic->kdc/dot_general | solution.py:132
  174.2 3.4 %convert_reduce_fusion = f32[2048,512]{1,0:T(8,128)} fusion(bf16[4,2048,512]{2,1,0:T(8,128)(2,1)S(1)} %fusion.9), kind=kLoop, calls=%fused_computation.13 | loop fusion | flops 7340032 | bytes 12582912 | tf_op jit(solution)/shard_map/reduce_sum | solution.py:134
  179.1 5.8 %all-to-all-done.2 = bf16[16,8,4096]{2,1,0:T(8,128)(2,1)} async-done(((bf16[16,8,4096]{2,1,0:T(8,128)(2,1)}), bf16[16,8,4096]{2,1,0:T(8,128)(2,1)}, u32[]{:S(2)}, u32[]{:S(2)}) %all-to-all-start.2) | async-done | bytes 1048608 | tf_op jit(solution)/shard_map/all_to_all | solution.py:42
  (93 shorter events, 54.6 us)
Async XLA Ops:
  0.6 21.0 %copy-start = (bf16[1,2048,512]{2,1,0:T(8,128)(2,1)S(1)}, bf16[1,2048,512]{2,1,0:T(8,128)(2,1)}, u32[]{:S(2)}) copy-start(bf16[1,2048,512]{2,1,0:T(8,128)(2,1)} %param.9) | copy-start | bytes 6291460
  0.6 8.4 %collective-permute-start = (bf16[2,128,512]{2,1,0:T(8,128)(2,1)}, bf16[2,128,512]{2,1,0:T(8,128)(2,1)S(1)}, u32[]{:S(2)}, u32[]{:S(2)}) collective-permute-start(bf16[2,128,512]{2,1,0:T(8,128)(2,1)} %bitcast.115), channel_id=1, source_target_pairs={{0,64},{64,128},{128,192},{192,0},{1,65},{65,129},{129,193},{193,1... | collective-permute-start | bytes 786440 | tf_op jit(solution)/shard_map/ppermute | solution.py:73
  2.8 14.2 %collective-permute-start.1 = (bf16[2,128,512]{2,1,0:T(8,128)(2,1)}, bf16[2,128,512]{2,1,0:T(8,128)(2,1)S(1)}, u32[]{:S(2)}, u32[]{:S(2)}) collective-permute-start(bf16[2,128,512]{2,1,0:T(8,128)(2,1)} %bitcast.116), channel_id=1, source_target_pairs={{0,128},{64,192},{128,0},{192,64},{1,129},{65,193},{129,1},{193,65... | collective-permute-start | bytes 786440 | tf_op jit(solution)/shard_map/ppermute | solution.py:73
  5.5 11.6 %collective-permute-start.2 = (bf16[2,128,512]{2,1,0:T(8,128)(2,1)}, bf16[2,128,512]{2,1,0:T(8,128)(2,1)S(1)}, u32[]{:S(2)}, u32[]{:S(2)}) collective-permute-start(bf16[2,128,512]{2,1,0:T(8,128)(2,1)} %bitcast.117), channel_id=1, source_target_pairs={{0,192},{64,0},{128,64},{192,128},{1,193},{65,1},{129,65},{193,129... | collective-permute-start | bytes 786440 | tf_op jit(solution)/shard_map/ppermute | solution.py:73
  9.1 8.0 %copy-start.11 = (bf16[2,128,512]{2,1,0:T(8,128)(2,1)}, bf16[2,128,512]{2,1,0:T(8,128)(2,1)S(1)}, u32[]{:S(2)}) copy-start(bf16[2,128,512]{2,1,0:T(8,128)(2,1)S(1)} %collective-permute-done) | copy-start | bytes 786436
  27.5 12.6 %collective-permute-start.3 = (bf16[4,2,2,32,2048]{4,3,2,0,1:T(8,128)(2,1)}, bf16[4,2,2,32,2048]{4,3,2,0,1:T(8,128)(2,1)}, u32[]{:S(2)}, u32[]{:S(2)}) collective-permute-start(bf16[4,2,2,32,2048]{4,3,2,0,1:T(8,128)(2,1)} %bitcast.97), channel_id=1, source_target_pairs={{0,1},{1,0},{2,3},{3,2},{4,5},{5,4},{6,7},{7,6},{8,9},{9,8},{10,11... | collective-permute-start | bytes 6291464 | tf_op jit(solution)/shard_map/ppermute | solution.py:88
  33.4 6.8 %copy-start.3 = (bf16[4,2,1,2,32,2048]{5,4,2,1,0,3:T(8,128)(2,1)S(1)}, bf16[4,2,1,2,32,2048]{5,4,2,1,0,3:T(8,128)(2,1)}, u32[]{:S(2)}) copy-start(bf16[4,2,1,2,32,2048]{5,4,2,1,0,3:T(8,128)(2,1)} %get-tuple-element.6) | copy-start | bytes 6291460
  34.2 12.3 %collective-permute-start.5 = (bf16[2,32,2048]{2,1,0:T(8,128)(2,1)}, bf16[2,32,2048]{2,1,0:T(8,128)(2,1)S(1)}, u32[]{:S(2)}, u32[]{:S(2)}) collective-permute-start(bf16[2,32,2048]{2,1,0:T(8,128)(2,1)} %bitcast.100), channel_id=1, source_target_pairs={{0,64},{64,128},{128,192},{192,0},{1,65},{65,129},{129,193},{193,1... | collective-permute-start | bytes 786440 | tf_op jit(solution)/shard_map/ppermute | solution.py:114
  35.9 13.6 %collective-permute-start.6 = (bf16[2,32,2048]{2,1,0:T(8,128)(2,1)}, bf16[2,32,2048]{2,1,0:T(8,128)(2,1)}, u32[]{:S(2)}, u32[]{:S(2)}) collective-permute-start(bf16[2,32,2048]{2,1,0:T(8,128)(2,1)} %bitcast.99), channel_id=1, source_target_pairs={{0,128},{64,192},{128,0},{192,64},{1,129},{65,193},{129,1},{193,65... | collective-permute-start | bytes 786440 | tf_op jit(solution)/shard_map/ppermute | solution.py:114
  38.9 11.5 %collective-permute-start.7 = (bf16[2,32,2048]{2,1,0:T(8,128)(2,1)}, bf16[2,32,2048]{2,1,0:T(8,128)(2,1)}, u32[]{:S(2)}, u32[]{:S(2)}) collective-permute-start(bf16[2,32,2048]{2,1,0:T(8,128)(2,1)} %bitcast.98), channel_id=1, source_target_pairs={{0,192},{64,0},{128,64},{192,128},{1,193},{65,1},{129,65},{193,129... | collective-permute-start | bytes 786440 | tf_op jit(solution)/shard_map/ppermute | solution.py:114
  42.6 10.4 %copy-start.4 = (bf16[4,2,2,32,2048]{4,3,2,0,1:T(8,128)(2,1)}, bf16[4,2,2,32,2048]{4,3,2,0,1:T(8,128)(2,1)S(1)}, u32[]{:S(2)}) copy-start(bf16[4,2,2,32,2048]{4,3,2,0,1:T(8,128)(2,1)S(1)} %fusion.11) | copy-start | bytes 6291460
  42.6 3.8 %copy-start.8 = (bf16[2,32,1,2048]{3,2,1,0:T(2,128)(2,1)S(1)}, bf16[2,32,1,2048]{3,2,1,0:T(2,128)(2,1)}, u32[]{:S(2)}) copy-start(bf16[2,32,1,2048]{3,2,1,0:T(2,128)(2,1)} %get-tuple-element.10) | copy-start | bytes 786436
  43.6 25.7 %collective-permute-start.4 = (bf16[4,2,32,2048]{3,2,1,0:T(8,128)(2,1)}, bf16[4,2,32,2048]{3,2,1,0:T(8,128)(2,1)}, u32[]{:S(2)}, u32[]{:S(2)}) collective-permute-start(bf16[4,2,32,2048]{3,2,1,0:T(8,128)(2,1)} %dynamic-slice_bitcast_fusion), channel_id=1, source_target_pairs={{0,2},{1,3},{2,0},{3,1},{4,6},{5,7},{6,4},{7,5},{8,10},{9,11},{10,... | collective-permute-start | bytes 3145736 | tf_op jit(solution)/shard_map/ppermute | solution.py:92
  52.9 38.8 %collective-permute-start.8 = (bf16[4,2,32,2048]{3,2,1,0:T(8,128)(2,1)}, bf16[4,2,32,2048]{3,2,1,0:T(8,128)(2,1)}, u32[]{:S(2)}, u32[]{:S(2)}) collective-permute-start(bf16[4,2,32,2048]{3,2,1,0:T(8,128)(2,1)} %get-tuple-element.9), channel_id=1, source_target_pairs={{0,2},{1,3},{2,0},{3,1},{4,6},{5,7},{6,4},{7,5},{8,10},{9,11},{10,... | collective-permute-start | bytes 3145736 | tf_op jit(solution)/shard_map/ppermute | solution.py:117
  58.3 11.0 %copy-start.5 = (bf16[4,2,2,32,2048]{4,3,2,0,1:T(8,128)(2,1)S(1)}, bf16[4,2,2,32,2048]{4,3,2,0,1:T(8,128)(2,1)}, u32[]{:S(2)}) copy-start(bf16[4,2,2,32,2048]{4,3,2,0,1:T(8,128)(2,1)} %copy-done.4) | copy-start | bytes 6291460
  71.9 25.2 %all-to-all-start = ((bf16[4,2,32,2048]{3,2,1,0:T(8,128)(2,1)}), bf16[4,2,32,2048]{3,2,1,0:T(8,128)(2,1)}, u32[]{:S(2)}, u32[]{:S(2)}) async-start(bf16[4,2,32,2048]{3,2,1,0:T(8,128)(2,1)} %fusion.22), calls=%async_computation | async-start | bytes 2097152 | tf_op jit(solution)/shard_map/all_to_all | solution.py:94
  95.4 33.7 %collective-permute-start.9 = (bf16[2,4,2,32,2048]{4,3,2,1,0:T(8,128)(2,1)}, bf16[2,4,2,32,2048]{4,3,2,1,0:T(8,128)(2,1)}, u32[]{:S(2)}, u32[]{:S(2)}) collective-permute-start(bf16[2,4,2,32,2048]{4,3,2,1,0:T(8,128)(2,1)} %reverse_select_fusion), channel_id=1, source_target_pairs={{0,1},{1,0},{2,3},{3,2},{4,5},{5,4},{6,7},{7,6},{8,9},{9,8},{10,11... | collective-permute-start | bytes 6291464 | tf_op jit(solution)/shard_map/ppermute | solution.py:120
  115.6 35.5 %all-to-all-start.1 = ((bf16[16,8,4096]{2,1,0:T(8,128)(2,1)}), bf16[16,8,4096]{2,1,0:T(8,128)(2,1)}, u32[]{:S(2)}, u32[]{:S(2)}) async-start(bf16[16,8,4096]{2,1,0:T(8,128)(2,1)} %bitcast.109), calls=%async_computation.1 | async-start | bytes 2097152 | tf_op jit(solution)/shard_map/all_to_all | solution.py:36
  153.3 7.2 %copy-start.10 = (bf16[1,2,128,512]{3,2,1,0:T(8,128)(2,1)S(1)}, bf16[1,2,128,512]{3,2,1,0:T(8,128)(2,1)}, u32[]{:S(2)}) copy-start(bf16[1,2,128,512]{3,2,1,0:T(8,128)(2,1)} %param.8) | copy-start | bytes 786436
  153.3 7.2 %copy-start.12 = (bf16[2,128,512]{2,1,0:T(8,128)(2,1)S(1)}, bf16[2,128,512]{2,1,0:T(8,128)(2,1)}, u32[]{:S(2)}) copy-start(bf16[2,128,512]{2,1,0:T(8,128)(2,1)} %copy-done.11) | copy-start | bytes 786436
  153.3 7.2 %copy-start.14 = (bf16[2,128,512]{2,1,0:T(8,128)(2,1)S(1)}, bf16[2,128,512]{2,1,0:T(8,128)(2,1)}, u32[]{:S(2)}) copy-start(bf16[2,128,512]{2,1,0:T(8,128)(2,1)} %copy-done.13) | copy-start | bytes 786436
  153.3 7.2 %copy-start.16 = (bf16[2,128,512]{2,1,0:T(8,128)(2,1)S(1)}, bf16[2,128,512]{2,1,0:T(8,128)(2,1)}, u32[]{:S(2)}) copy-start(bf16[2,128,512]{2,1,0:T(8,128)(2,1)} %copy-done.15) | copy-start | bytes 786436
  154.9 30.1 %all-to-all-start.2 = ((bf16[16,8,4096]{2,1,0:T(8,128)(2,1)}), bf16[16,8,4096]{2,1,0:T(8,128)(2,1)}, u32[]{:S(2)}, u32[]{:S(2)}) async-start(bf16[16,8,4096]{2,1,0:T(8,128)(2,1)} %bitcast.62), calls=%async_computation.2 | async-start | bytes 2097152 | tf_op jit(solution)/shard_map/all_to_all | solution.py:42
  174.2 3.4 %copy-start.6 = (f32[4,2,4,8,2048]{4,3,2,1,0:T(8,128)S(1)}, f32[4,2,4,8,2048]{4,3,2,1,0:T(8,128)}, u32[]{:S(2)}) copy-start(f32[4,2,4,8,2048]{4,3,2,1,0:T(8,128)} %get-tuple-element.14) | copy-start | bytes 6291460
  (7 other events, 14.0 us)

commit v5 on v4

--- a/solution.py
+++ b/solution.py
@@ -34,14 +34,9 @@
     chunks = branch_path.astype(jnp.bfloat16).reshape(m, rt, 8, half, w)
     chunks = chunks.transpose(0, 1, 3, 2, 4).reshape(n_sec, 8, w)
     got = lax.all_to_all(chunks, "section", 0, 0, tiled=True)
-    src = jnp.arange(n_sec, dtype=jnp.int32)
-    upper = (src[None, :] > src[:, None]).astype(jnp.bfloat16)
-    suffix = jnp.einsum(
-        "st,tx->sx", upper, got.reshape(n_sec, -1), preferred_element_type=jnp.float32
-    )
-    back = lax.all_to_all(
-        suffix.astype(jnp.bfloat16).reshape(n_sec, 8, w), "section", 0, 0, tiled=True
-    )
+    shifted = jnp.concatenate([got[1:], jnp.zeros_like(got[:1])], axis=0)
+    suffix = lax.cumsum(shifted.astype(jnp.float32), axis=0, reverse=True)
+    back = lax.all_to_all(suffix.astype(jnp.bfloat16), "section", 0, 0, tiled=True)
     back = back.reshape(m, rt, half, 8, w).transpose(0, 1, 3, 2, 4)
     return back.reshape(m, t, d).astype(jnp.float32)
 

time: 192 us -> 191 us (level)
  local copies, waits for them, and re-layouts: 35.5 us -> 33.5 us
    unnamed x42 -> x40, local copies, waits for them, and re-layouts: 7.49 us -> 4.21 us
where the time goes in v5:
time: 191 us; the launch traced here: 188 us
  waiting for transfers between devices  57.4 us (30%)
  other arithmetic  40.8 us (21%)
  starting transfers between devices  37.9 us (20%)
  local copies, waits for them, and re-layouts  33.5 us (18%)
  matrix products  16 us (8%)
  between operations  2.31 us (1%)
    all_to_all x1, waiting for transfers between devices, later_sum(): got = lax.all_to_all(chunks, 'section', 0, 0, tiled=True)  16.8 us
    ppermute x1, waiting for transfers between devices, body(): far = lax.ppermute(mine, 'tensor', [(q, q ^ 2) for q in range(n_t)])  15.6 us
    dot_general x1, matrix products, body(): jnp.einsum('tkmid,mktic->kdc', nrm, cot_sel, preferred_element_type=jnp.f...  13.7 us
    all_to_all x1, starting transfers between devices, later_sum(): got = lax.all_to_all(chunks, 'section', 0, 0, tiled=True)  9.27 us
    ppermute x3, waiting for transfers between devices, body(): lax.ppermute(cotan, 'dp', [(q, (q + k) % n_dp) for q in range(n_dp)])  7.95 us
    ppermute x1, waiting for transfers between devices, body(): recv = lax.ppermute(send, 'tensor', [(q, q ^ 2) for q in range(n_t)])  7.31 us
    ppermute x3, starting transfers between devices, body(): lax.ppermute(cotan, 'dp', [(q, (q + k) % n_dp) for q in range(n_dp)])  5.88 us
    all_to_all x1, waiting for transfers between devices, later_sum(): lax.all_to_all(suffix.astype(jnp.bfloat16), 'section', 0, 0, tiled=True)  5.84 us
  transfers between devices with their start and end apart: 13, of which 7 were waited for; matrix products, arithmetic and copies ran while one was open for 39% of the time, Pallas kernels for 0%

profile of v5, /device:TPU:1, one launch (start us, length us, event | category | flops | bytes accessed | tf_op | source)
XLA Modules:
  0.0 187.9 jit_solution(4892910877952200125)
XLA Ops:
  2.8 2.6 %collective-permute-start.1 = (bf16[2,128,512]{2,1,0:T(8,128)(2,1)}, bf16[2,128,512]{2,1,0:T(8,128)(2,1)S(1)}, u32[]{:S(2)}, u32[]{:S(2)}) collective-permute-start(bf16[2,128,512]{2,1,0:T(8,128)(2,1)} %bitcast.109), channel_id=1, source_target_pairs={{0,128},{64,192},{128,0},{192,64},{1,129},{65,193},{129,1},{193,65... | collective-permute-start | bytes 786440 | tf_op jit(solution)/shard_map/ppermute | solution.py:68
  9.1 7.9 %collective-permute-done.1 = bf16[2,128,512]{2,1,0:T(8,128)(2,1)S(1)} collective-permute-done((bf16[2,128,512]{2,1,0:T(8,128)(2,1)}, bf16[2,128,512]{2,1,0:T(8,128)(2,1)S(1)}, u32[]{:S(2)}, u32[]{:S(2)}) %collective-permute-start.1) | collective-permute-done | bytes 262176 | tf_op jit(solution)/shard_map/ppermute | solution.py:68
  30.2 3.2 %constant_dynamic-slice_fusion.3 = (bf16[2,32,1,2048]{3,2,1,0:T(2,128)(2,1)}, bf16[2,32,1,2048]{3,2,1,0:T(2,128)(2,1)S(1)}, bf16[2,32,1,2048]{3,2,1,0:T(2,128)(2,1)S(1)}, bf16[2,32,1,2048]{3,2,1,0:T(2,128)(2,1)S(1)}) fusion(bf16[2,32,4,2048]{3,2,1,0:T(4,128)(2,1)S(1)} %reshape.159, s32[]{:T(128)S(6)} %select_n.88, s32[]{:T(128)S(6)} %select_n.94, ...), kind=kLoop, calls=%fused_computation.70 | loop fusion | bytes 2097168 | tf_op jit(solution)/shard_map/jit(dynamic_index_in_dim)/dynamic_slice | solution.py:105
  43.6 2.7 %collective-permute-start.4 = (bf16[4,2,32,2048]{3,2,1,0:T(8,128)(2,1)}, bf16[4,2,32,2048]{3,2,1,0:T(8,128)(2,1)}, u32[]{:S(2)}, u32[]{:S(2)}) collective-permute-start(bf16[4,2,32,2048]{3,2,1,0:T(8,128)(2,1)} %dynamic-slice_bitcast_fusion), channel_id=1, source_target_pairs={{0,2},{1,3},{2,0},{3,1},{4,6},{5,7},{6,4},{7,5},{8,10},{9,11},{10,... | collective-permute-start | bytes 3145736 | tf_op jit(solution)/shard_map/ppermute | solution.py:87
  46.5 2.9 %collective-permute-done.6 = bf16[2,32,2048]{2,1,0:T(8,128)(2,1)} collective-permute-done((bf16[2,32,2048]{2,1,0:T(8,128)(2,1)}, bf16[2,32,2048]{2,1,0:T(8,128)(2,1)}, u32[]{:S(2)}, u32[]{:S(2)}) %collective-permute-start.6) | collective-permute-done | bytes 262176 | tf_op jit(solution)/shard_map/ppermute | solution.py:109
  53.0 2.7 %collective-permute-start.8 = (bf16[4,2,32,2048]{3,2,1,0:T(8,128)(2,1)}, bf16[4,2,32,2048]{3,2,1,0:T(8,128)(2,1)}, u32[]{:S(2)}, u32[]{:S(2)}) collective-permute-start(bf16[4,2,32,2048]{3,2,1,0:T(8,128)(2,1)} %get-tuple-element.9), channel_id=1, source_target_pairs={{0,2},{1,3},{2,0},{3,1},{4,6},{5,7},{6,4},{7,5},{8,10},{9,11},{10,... | collective-permute-start | bytes 3145736 | tf_op jit(solution)/shard_map/ppermute | solution.py:112
  55.7 2.6 %reshape.164 = f32[2,32,4,2048]{3,2,1,0:T(4,128)} reshape(bf16[1,2,32,8192]{3,2,1,0:T(8,128)(2,1)S(1)} %copy-done.2) | data formatting | bytes 3145728 | tf_op jit(solution)/shard_map/convert_element_type | solution.py:60
  58.4 3.1 %reshape.166 = f32[2,4,8,2,4096]{4,3,2,1,0:T(2,128)} reshape(bf16[1,2,32,8192]{3,2,1,0:T(8,128)(2,1)S(1)} %copy-done.2) | data formatting | bytes 3145728 | tf_op jit(solution)/shard_map/convert_element_type | solution.py:60
  62.0 7.3 %collective-permute-done.4 = bf16[4,2,32,2048]{3,2,1,0:T(8,128)(2,1)} collective-permute-done((bf16[4,2,32,2048]{3,2,1,0:T(8,128)(2,1)}, bf16[4,2,32,2048]{3,2,1,0:T(8,128)(2,1)}, u32[]{:S(2)}, u32[]{:S(2)}) %collective-permute-start.4) | collective-permute-done | bytes 1048608 | tf_op jit(solution)/shard_map/ppermute | solution.py:87
  69.3 2.6 %fusion.22 = bf16[4,2,32,2048]{3,2,1,0:T(8,128)(2,1)} fusion(bf16[4,2,32,2048]{3,2,1,0:T(8,128)(2,1)} %collective-permute-done.4, bf16[4,2,2,32,2048]{4,3,2,0,1:T(8,128)(2,1)S(1)} %copy-done.5, s32[]{:T(128)S(6)} %select_n.84), kind=kLoop, calls=%fused_computation.43 | loop fusion | flops 2097152 | bytes 3145732 | tf_op jit(solution)/shard_map/convert_element_type | solution.py:88
  71.9 4.3 %all-to-all-start = ((bf16[4,2,32,2048]{3,2,1,0:T(8,128)(2,1)}), bf16[4,2,32,2048]{3,2,1,0:T(8,128)(2,1)}, u32[]{:S(2)}, u32[]{:S(2)}) async-start(bf16[4,2,32,2048]{3,2,1,0:T(8,128)(2,1)} %fusion.22), calls=%async_computation | async-start | bytes 2097152 | tf_op jit(solution)/shard_map/all_to_all | solution.py:89
  76.2 15.6 %collective-permute-done.8 = bf16[4,2,32,2048]{3,2,1,0:T(8,128)(2,1)} collective-permute-done((bf16[4,2,32,2048]{3,2,1,0:T(8,128)(2,1)}, bf16[4,2,32,2048]{3,2,1,0:T(8,128)(2,1)}, u32[]{:S(2)}, u32[]{:S(2)}) %collective-permute-start.8) | collective-permute-done | bytes 1048608 | tf_op jit(solution)/shard_map/ppermute | solution.py:112
  97.1 2.9 %convert_bitcast_fusion = (f32[4,2,4,8,2048]{4,3,2,1,0:T(8,128)}, f32[2,32,4,2048]{3,1,0,2:T(8,128)S(1)}) fusion(bf16[4,2,32,2048]{3,2,1,0:T(8,128)(2,1)} %all-to-all-done), kind=kLoop, calls=%fused_computation.22 | loop fusion | flops 524288 | bytes 5242880
  100.0 2.7 %copy.41 = f32[2,32,4,2048]{3,2,1,0:T(4,128)} copy(f32[2,32,4,2048]{3,1,0,2:T(8,128)S(1)} %get-tuple-element.15) | data formatting | bytes 4194304 | tf_op jit(solution)/shard_map/transpose | solution.py:90
  102.7 4.2 %reshape.157 = f32[2,4,8,2,4096]{4,3,2,1,0:T(2,128)} reshape(f32[2,32,4,2048]{3,2,1,0:T(4,128)} %copy.41) | data formatting | bytes 4194304 | tf_op jit(solution)/shard_map/reshape | solution.py:90
  106.9 3.2 %fusion.25 = f32[2,32]{1,0:T(2,128)S(1)} fusion(f32[2,32,4,2048]{3,2,1,0:T(4,128)} %reshape.164, f32[2,32]{1,0:T(2,128)S(1)} %add_rsqrt_fusion.1, f32[4,2048]{1,0:T(4,128)S(1)} %reshape.163, bf16[4,2,32,2048]{3,2,1,0:T(8,128)(2,1)} %all-to-all-done), kind=kLoop, calls=%fused_computation.47 | loop fusion | flops 2621376 | bytes 3179008 | tf_op jit(solution)/shard_map/reduce_sum | solution.py:95
  110.2 3.9 %fusion.33 = bf16[2,4,2,8,4096]{4,2,3,1,0:T(2,128)(2,1)S(1)} fusion(f32[2,4,8]{2,1,0:T(4,128)S(1)} %div.24, f32[2,4,8,2,4096]{4,3,2,1,0:T(2,128)} %reshape.166, f32[2,4,8,2,4096]{4,3,2,1,0:T(2,128)} %reshape.157, f32[2,4096]{1,0:T(2,128)S(1)} %reshape.165, f32[2,4,8]{2,1,0:T(4,128)S(1)} %rsqrt.21), kind=kLoop, calls=%fused_computation.61 | loop fusion | flops 3145728 | bytes 5276160 | tf_op jit(solution)/shard_map/transpose | solution.py:35
  115.6 9.3 %all-to-all-start.1 = ((bf16[16,8,4096]{2,1,0:T(8,128)(2,1)}), bf16[16,8,4096]{2,1,0:T(8,128)(2,1)}, u32[]{:S(2)}, u32[]{:S(2)}) async-start(bf16[16,8,4096]{2,1,0:T(8,128)(2,1)} %bitcast.104), calls=%async_computation.1 | async-start | bytes 2097152 | tf_op jit(solution)/shard_map/all_to_all | solution.py:36
  129.2 2.9 %fusion.10 = bf16[2,2,4,2,32,2048]{5,4,3,2,0,1:T(8,128)(2,1)S(1)} fusion(bf16[1,2,4,2,32,2048]{5,4,3,2,1,0:T(8,128)(2,1)} %bitcast.30, bf16[1,2,4,2,32,2048]{5,4,3,2,1,0:T(8,128)(2,1)S(1)} %fusion.41, pred[]{:T(512)S(6)} %eq.13), kind=kLoop, calls=%fused_computation.16 | loop fusion | flops 6291456 | bytes 8388609 | tf_op jit(solution)/shard_map/transpose | solution.py:117
  134.3 16.8 %all-to-all-done.1 = bf16[16,8,4096]{2,1,0:T(8,128)(2,1)} async-done(((bf16[16,8,4096]{2,1,0:T(8,128)(2,1)}), bf16[16,8,4096]{2,1,0:T(8,128)(2,1)}, u32[]{:S(2)}, u32[]{:S(2)}) %all-to-all-start.1) | async-done | bytes 1048608 | tf_op jit(solution)/shard_map/all_to_all | solution.py:36
  154.0 5.6 %all-to-all-start.2 = ((bf16[16,8,4096]{2,1,0:T(8,128)(2,1)}), bf16[16,8,4096]{2,1,0:T(8,128)(2,1)}, u32[]{:S(2)}, u32[]{:S(2)}) async-start(bf16[16,8,4096]{2,1,0:T(8,128)(2,1)} %reduce-window_convert_fusion), calls=%async_computation.2 | async-start | bytes 2097152 | tf_op jit(solution)/shard_map/all_to_all | solution.py:39
  159.6 13.7 %fusion.9 = bf16[4,2048,512]{2,1,0:T(8,128)(2,1)S(1)} fusion(s32[4]{0:T(128)S(1)} %fusion.34, s32[2048,512]{1,0:T(8,128)} %add_add_fusion, bf16[4,4,2,32,2048]{4,3,2,1,0:T(8,128)(2,1)} %bitcast.102, bf16[1,2,4,32,512]{4,3,2,1,0:T(8,128)(2,1)S(1)} %bitcast.117, bf16[1,2,4,32,512]{4,3,2,1,0:T(8,128)(2,1)S(1)} %bitcast.115, ...), kind=kOutput, calls=%fused_computation.13 | convolution fusion | flops 2220359680 | bytes 17825808 | tf_op jit(solution)/shard_map/tkmid,mktic->kdc/dot_general | solution.py:127
  173.3 3.4 %convert_reduce_fusion = f32[2048,512]{1,0:T(8,128)} fusion(bf16[4,2048,512]{2,1,0:T(8,128)(2,1)S(1)} %fusion.9), kind=kLoop, calls=%fused_computation.12 | loop fusion | flops 7340032 | bytes 12582912 | tf_op jit(solution)/shard_map/reduce_sum | solution.py:129
  178.2 5.8 %all-to-all-done.2 = bf16[16,8,4096]{2,1,0:T(8,128)(2,1)} async-done(((bf16[16,8,4096]{2,1,0:T(8,128)(2,1)}), bf16[16,8,4096]{2,1,0:T(8,128)(2,1)}, u32[]{:S(2)}, u32[]{:S(2)}) %all-to-all-start.2) | async-done | bytes 1048608 | tf_op jit(solution)/shard_map/all_to_all | solution.py:39
  (92 shorter events, 53.8 us)
Async XLA Ops:
  0.6 21.0 %copy-start = (bf16[1,2048,512]{2,1,0:T(8,128)(2,1)S(1)}, bf16[1,2048,512]{2,1,0:T(8,128)(2,1)}, u32[]{:S(2)}) copy-start(bf16[1,2048,512]{2,1,0:T(8,128)(2,1)} %param.9) | copy-start | bytes 6291460
  0.6 8.4 %collective-permute-start = (bf16[2,128,512]{2,1,0:T(8,128)(2,1)}, bf16[2,128,512]{2,1,0:T(8,128)(2,1)S(1)}, u32[]{:S(2)}, u32[]{:S(2)}) collective-permute-start(bf16[2,128,512]{2,1,0:T(8,128)(2,1)} %bitcast.108), channel_id=1, source_target_pairs={{0,64},{64,128},{128,192},{192,0},{1,65},{65,129},{129,193},{193,1... | collective-permute-start | bytes 786440 | tf_op jit(solution)/shard_map/ppermute | solution.py:68
  2.8 14.2 %collective-permute-start.1 = (bf16[2,128,512]{2,1,0:T(8,128)(2,1)}, bf16[2,128,512]{2,1,0:T(8,128)(2,1)S(1)}, u32[]{:S(2)}, u32[]{:S(2)}) collective-permute-start(bf16[2,128,512]{2,1,0:T(8,128)(2,1)} %bitcast.109), channel_id=1, source_target_pairs={{0,128},{64,192},{128,0},{192,64},{1,129},{65,193},{129,1},{193,65... | collective-permute-start | bytes 786440 | tf_op jit(solution)/shard_map/ppermute | solution.py:68
  5.5 11.6 %collective-permute-start.2 = (bf16[2,128,512]{2,1,0:T(8,128)(2,1)}, bf16[2,128,512]{2,1,0:T(8,128)(2,1)S(1)}, u32[]{:S(2)}, u32[]{:S(2)}) collective-permute-start(bf16[2,128,512]{2,1,0:T(8,128)(2,1)} %bitcast.110), channel_id=1, source_target_pairs={{0,192},{64,0},{128,64},{192,128},{1,193},{65,1},{129,65},{193,129... | collective-permute-start | bytes 786440 | tf_op jit(solution)/shard_map/ppermute | solution.py:68
  9.1 8.0 %copy-start.11 = (bf16[2,128,512]{2,1,0:T(8,128)(2,1)}, bf16[2,128,512]{2,1,0:T(8,128)(2,1)S(1)}, u32[]{:S(2)}) copy-start(bf16[2,128,512]{2,1,0:T(8,128)(2,1)S(1)} %collective-permute-done) | copy-start | bytes 786436
  27.5 12.7 %collective-permute-start.3 = (bf16[4,2,2,32,2048]{4,3,2,0,1:T(8,128)(2,1)}, bf16[4,2,2,32,2048]{4,3,2,0,1:T(8,128)(2,1)}, u32[]{:S(2)}, u32[]{:S(2)}) collective-permute-start(bf16[4,2,2,32,2048]{4,3,2,0,1:T(8,128)(2,1)} %bitcast.92), channel_id=1, source_target_pairs={{0,1},{1,0},{2,3},{3,2},{4,5},{5,4},{6,7},{7,6},{8,9},{9,8},{10,11... | collective-permute-start | bytes 6291464 | tf_op jit(solution)/shard_map/ppermute | solution.py:83
  33.3 6.8 %copy-start.3 = (bf16[4,2,1,2,32,2048]{5,4,2,1,0,3:T(8,128)(2,1)S(1)}, bf16[4,2,1,2,32,2048]{5,4,2,1,0,3:T(8,128)(2,1)}, u32[]{:S(2)}) copy-start(bf16[4,2,1,2,32,2048]{5,4,2,1,0,3:T(8,128)(2,1)} %get-tuple-element.6) | copy-start | bytes 6291460
  34.2 12.3 %collective-permute-start.5 = (bf16[2,32,2048]{2,1,0:T(8,128)(2,1)}, bf16[2,32,2048]{2,1,0:T(8,128)(2,1)S(1)}, u32[]{:S(2)}, u32[]{:S(2)}) collective-permute-start(bf16[2,32,2048]{2,1,0:T(8,128)(2,1)} %bitcast.95), channel_id=1, source_target_pairs={{0,64},{64,128},{128,192},{192,0},{1,65},{65,129},{129,193},{193,1... | collective-permute-start | bytes 786440 | tf_op jit(solution)/shard_map/ppermute | solution.py:109
  35.9 13.6 %collective-permute-start.6 = (bf16[2,32,2048]{2,1,0:T(8,128)(2,1)}, bf16[2,32,2048]{2,1,0:T(8,128)(2,1)}, u32[]{:S(2)}, u32[]{:S(2)}) collective-permute-start(bf16[2,32,2048]{2,1,0:T(8,128)(2,1)} %bitcast.94), channel_id=1, source_target_pairs={{0,128},{64,192},{128,0},{192,64},{1,129},{65,193},{129,1},{193,65... | collective-permute-start | bytes 786440 | tf_op jit(solution)/shard_map/ppermute | solution.py:109
  38.9 11.5 %collective-permute-start.7 = (bf16[2,32,2048]{2,1,0:T(8,128)(2,1)}, bf16[2,32,2048]{2,1,0:T(8,128)(2,1)}, u32[]{:S(2)}, u32[]{:S(2)}) collective-permute-start(bf16[2,32,2048]{2,1,0:T(8,128)(2,1)} %bitcast.93), channel_id=1, source_target_pairs={{0,192},{64,0},{128,64},{192,128},{1,193},{65,1},{129,65},{193,129... | collective-permute-start | bytes 786440 | tf_op jit(solution)/shard_map/ppermute | solution.py:109
  42.6 10.4 %copy-start.4 = (bf16[4,2,2,32,2048]{4,3,2,0,1:T(8,128)(2,1)}, bf16[4,2,2,32,2048]{4,3,2,0,1:T(8,128)(2,1)S(1)}, u32[]{:S(2)}) copy-start(bf16[4,2,2,32,2048]{4,3,2,0,1:T(8,128)(2,1)S(1)} %fusion.11) | copy-start | bytes 6291460
  42.6 3.8 %copy-start.8 = (bf16[2,32,1,2048]{3,2,1,0:T(2,128)(2,1)S(1)}, bf16[2,32,1,2048]{3,2,1,0:T(2,128)(2,1)}, u32[]{:S(2)}) copy-start(bf16[2,32,1,2048]{3,2,1,0:T(2,128)(2,1)} %get-tuple-element.10) | copy-start | bytes 786436
  43.6 25.7 %collective-permute-start.4 = (bf16[4,2,32,2048]{3,2,1,0:T(8,128)(2,1)}, bf16[4,2,32,2048]{3,2,1,0:T(8,128)(2,1)}, u32[]{:S(2)}, u32[]{:S(2)}) collective-permute-start(bf16[4,2,32,2048]{3,2,1,0:T(8,128)(2,1)} %dynamic-slice_bitcast_fusion), channel_id=1, source_target_pairs={{0,2},{1,3},{2,0},{3,1},{4,6},{5,7},{6,4},{7,5},{8,10},{9,11},{10,... | collective-permute-start | bytes 3145736 | tf_op jit(solution)/shard_map/ppermute | solution.py:87
  53.0 38.8 %collective-permute-start.8 = (bf16[4,2,32,2048]{3,2,1,0:T(8,128)(2,1)}, bf16[4,2,32,2048]{3,2,1,0:T(8,128)(2,1)}, u32[]{:S(2)}, u32[]{:S(2)}) collective-permute-start(bf16[4,2,32,2048]{3,2,1,0:T(8,128)(2,1)} %get-tuple-element.9), channel_id=1, source_target_pairs={{0,2},{1,3},{2,0},{3,1},{4,6},{5,7},{6,4},{7,5},{8,10},{9,11},{10,... | collective-permute-start | bytes 3145736 | tf_op jit(solution)/shard_map/ppermute | solution.py:112
  58.4 10.9 %copy-start.5 = (bf16[4,2,2,32,2048]{4,3,2,0,1:T(8,128)(2,1)S(1)}, bf16[4,2,2,32,2048]{4,3,2,0,1:T(8,128)(2,1)}, u32[]{:S(2)}) copy-start(bf16[4,2,2,32,2048]{4,3,2,0,1:T(8,128)(2,1)} %copy-done.4) | copy-start | bytes 6291460
  71.9 25.2 %all-to-all-start = ((bf16[4,2,32,2048]{3,2,1,0:T(8,128)(2,1)}), bf16[4,2,32,2048]{3,2,1,0:T(8,128)(2,1)}, u32[]{:S(2)}, u32[]{:S(2)}) async-start(bf16[4,2,32,2048]{3,2,1,0:T(8,128)(2,1)} %fusion.22), calls=%async_computation | async-start | bytes 2097152 | tf_op jit(solution)/shard_map/all_to_all | solution.py:89
  95.4 33.7 %collective-permute-start.9 = (bf16[2,4,2,32,2048]{4,3,2,1,0:T(8,128)(2,1)}, bf16[2,4,2,32,2048]{4,3,2,1,0:T(8,128)(2,1)}, u32[]{:S(2)}, u32[]{:S(2)}) collective-permute-start(bf16[2,4,2,32,2048]{4,3,2,1,0:T(8,128)(2,1)} %reverse_select_fusion), channel_id=1, source_target_pairs={{0,1},{1,0},{2,3},{3,2},{4,5},{5,4},{6,7},{7,6},{8,9},{9,8},{10,11... | collective-permute-start | bytes 6291464 | tf_op jit(solution)/shard_map/ppermute | solution.py:115
  115.6 35.5 %all-to-all-start.1 = ((bf16[16,8,4096]{2,1,0:T(8,128)(2,1)}), bf16[16,8,4096]{2,1,0:T(8,128)(2,1)}, u32[]{:S(2)}, u32[]{:S(2)}) async-start(bf16[16,8,4096]{2,1,0:T(8,128)(2,1)} %bitcast.104), calls=%async_computation.1 | async-start | bytes 2097152 | tf_op jit(solution)/shard_map/all_to_all | solution.py:36
  152.4 7.1 %copy-start.10 = (bf16[1,2,128,512]{3,2,1,0:T(8,128)(2,1)S(1)}, bf16[1,2,128,512]{3,2,1,0:T(8,128)(2,1)}, u32[]{:S(2)}) copy-start(bf16[1,2,128,512]{3,2,1,0:T(8,128)(2,1)} %param.8) | copy-start | bytes 786436
  152.4 7.1 %copy-start.12 = (bf16[2,128,512]{2,1,0:T(8,128)(2,1)S(1)}, bf16[2,128,512]{2,1,0:T(8,128)(2,1)}, u32[]{:S(2)}) copy-start(bf16[2,128,512]{2,1,0:T(8,128)(2,1)} %copy-done.11) | copy-start | bytes 786436
  152.4 7.1 %copy-start.14 = (bf16[2,128,512]{2,1,0:T(8,128)(2,1)S(1)}, bf16[2,128,512]{2,1,0:T(8,128)(2,1)}, u32[]{:S(2)}) copy-start(bf16[2,128,512]{2,1,0:T(8,128)(2,1)} %copy-done.13) | copy-start | bytes 786436
  152.4 7.1 %copy-start.16 = (bf16[2,128,512]{2,1,0:T(8,128)(2,1)S(1)}, bf16[2,128,512]{2,1,0:T(8,128)(2,1)}, u32[]{:S(2)}) copy-start(bf16[2,128,512]{2,1,0:T(8,128)(2,1)} %copy-done.15) | copy-start | bytes 786436
  154.0 30.1 %all-to-all-start.2 = ((bf16[16,8,4096]{2,1,0:T(8,128)(2,1)}), bf16[16,8,4096]{2,1,0:T(8,128)(2,1)}, u32[]{:S(2)}, u32[]{:S(2)}) async-start(bf16[16,8,4096]{2,1,0:T(8,128)(2,1)} %reduce-window_convert_fusion), calls=%async_computation.2 | async-start | bytes 2097152 | tf_op jit(solution)/shard_map/all_to_all | solution.py:39
  173.3 3.4 %copy-start.6 = (f32[4,2,4,8,2048]{4,3,2,1,0:T(8,128)S(1)}, f32[4,2,4,8,2048]{4,3,2,1,0:T(8,128)}, u32[]{:S(2)}) copy-start(f32[4,2,4,8,2048]{4,3,2,1,0:T(8,128)} %get-tuple-element.14) | copy-start | bytes 6291460
  (7 other events, 14.1 us)

commit v6 on v5

--- a/solution.py
+++ b/solution.py
@@ -25,20 +25,14 @@
     return lax.optimization_barrier(moved.astype(jnp.bfloat16)).astype(jnp.float32)
 
 
-def later_sum(branch_path):
+def later_sum(branch4):
     n_sec = lax.axis_size("section")
-    m, t, d = branch_path.shape
-    rt = t // 8
-    half = n_sec // (m * rt)
-    w = d // half
-    chunks = branch_path.astype(jnp.bfloat16).reshape(m, rt, 8, half, w)
-    chunks = chunks.transpose(0, 1, 3, 2, 4).reshape(n_sec, 8, w)
+    chunks = branch4.astype(jnp.bfloat16).reshape(n_sec, -1, branch4.shape[-1])
     got = lax.all_to_all(chunks, "section", 0, 0, tiled=True)
     shifted = jnp.concatenate([got[1:], jnp.zeros_like(got[:1])], axis=0)
     suffix = lax.cumsum(shifted.astype(jnp.float32), axis=0, reverse=True)
     back = lax.all_to_all(suffix.astype(jnp.bfloat16), "section", 0, 0, tiled=True)
-    back = back.reshape(m, rt, half, 8, w).transpose(0, 1, 3, 2, 4)
-    return back.reshape(m, t, d).astype(jnp.float32)
+    return back.reshape(branch4.shape).astype(jnp.float32)
 
 
 def body(saved_input, kv_grad, kv_weight, norm_gain, top_grad, noise_salt, step_counter):
@@ -59,7 +53,6 @@
 
     input_float = saved_input[0].astype(jnp.float32)
     inverse_scale = lax.rsqrt(jnp.mean(input_float * input_float, axis=-1, keepdims=True) + 1e-05)
-    centered_input = input_float * inverse_scale
     gain_float = norm_gain[0].astype(jnp.float32)
 
     kv_pieces = [cotan]
@@ -87,15 +80,21 @@
     recv = lax.ppermute(send, "tensor", [(q, q ^ 2) for q in range(n_t)])
     total = (keep.astype(jnp.float32) + recv.astype(jnp.float32)).astype(jnp.bfloat16)
     got = lax.all_to_all(total, "dp", 0, 0, tiled=True)
-    normed_grad = got.astype(jnp.float32).transpose(1, 2, 0, 3).reshape(mb, tok_dev, d_model)
-
-    hidden_gradient = normed_grad * gain_float
-    branch_path = inverse_scale * (
+    normed_grad = got.astype(jnp.float32)
+    x4 = saved_input[0].reshape(mb, tok_dev, n_dp, rows_p).transpose(2, 0, 1, 3)
+    scale4 = inverse_scale[None]
+    centered4 = x4.astype(jnp.float32) * scale4
+    gain4 = gain_float.reshape(n_dp, 1, 1, rows_p)
+    hidden_gradient = normed_grad * gain4
+    branch4 = scale4 * (
         hidden_gradient
-        - centered_input * jnp.mean(hidden_gradient * centered_input, axis=-1, keepdims=True)
+        - centered4 * jnp.mean(hidden_gradient * centered4, axis=(0, 3), keepdims=True)
     )
-    later = later_sum(branch_path)
-    grad_in = (top_grad.astype(jnp.float32) + branch_path + later).astype(jnp.bfloat16)
+    later4 = later_sum(branch4)
+    grad_in = (
+        top_grad.astype(jnp.float32)
+        + (branch4 + later4).transpose(1, 2, 0, 3).reshape(mb, tok_dev, d_model)
+    ).astype(jnp.bfloat16)
 
     own_input, own_gain = lax.optimization_barrier((saved_input[0], norm_gain[0]))
     own_float = own_input.astype(jnp.float32)

time: 191 us -> 186 us (0.974)
  local copies, waits for them, and re-layouts: 33.5 us -> 24 us
  waiting for transfers between devices: 57.4 us -> 63.4 us
    transpose x2 -> x0, local copies, waits for them, and re-layouts: 4.23 us -> none  [the longest x1 2.68 us: body(): got.astype(jnp.float32).transpose(1, 2, 0, 3).reshape(mb, tok_dev, d_model)]
    ppermute x1, waiting for transfers between devices: 7.31 us -> 11.5 us  [body(): recv = lax.ppermute(send, 'tensor', [(q, q ^ 2) for q in range(n_t)])]
    unnamed x2 -> x1, other arithmetic: 3.82 us -> 0.85 us
    convert_element_type x2, local copies, waits for them, and re-layouts: 5.71 us -> 3.23 us  [the longest x1 1.68 us: body(): centered4 = x4.astype(jnp.float32) * scale4]
    reduce_sum x1, other arithmetic: 3.2 us -> 1.26 us  [body(): jnp.mean(hidden_gradient * centered4, axis=(0, 3), keepdims=True)]
    reshape x2 -> x1, local copies, waits for them, and re-layouts: 5.75 us -> 3.83 us  [body(): (branch4 + later4).transpose(1, 2, 0, 3).reshape(mb, tok_dev, d_model)]
    unnamed x40 -> x32, local copies, waits for them, and re-layouts: 4.21 us -> 3.6 us
  transfers between devices with their start and end apart: 13 -> 13, of which waited for: 7 -> 7; matrix products, arithmetic and copies ran while one was open for 39% -> 30% of each run, Pallas kernels for 0% -> 0%
where the time goes in v6:
time: 186 us; the launch traced here: 182 us
  waiting for transfers between devices  63.4 us (34%)
  other arithmetic  39.1 us (21%)
  starting transfers between devices  37.2 us (20%)
  local copies, waits for them, and re-layouts  24 us (13%)
  matrix products  16.4 us (9%)
  between operations  2.26 us (1%)
    all_to_all x1, waiting for transfers between devices, later_sum(): got = lax.all_to_all(chunks, 'section', 0, 0, tiled=True)  16.8 us
    ppermute x1, waiting for transfers between devices, body(): far = lax.ppermute(mine, 'tensor', [(q, q ^ 2) for q in range(n_t)])  16 us
    dot_general x1, matrix products, body(): jnp.einsum('tkmid,mktic->kdc', nrm, cot_sel, preferred_element_type=jnp.f...  14 us
    ppermute x1, waiting for transfers between devices, body(): recv = lax.ppermute(send, 'tensor', [(q, q ^ 2) for q in range(n_t)])  11.5 us
    all_to_all x1, starting transfers between devices, later_sum(): got = lax.all_to_all(chunks, 'section', 0, 0, tiled=True)  9.26 us
    ppermute x3, waiting for transfers between devices, body(): lax.ppermute(cotan, 'dp', [(q, (q + k) % n_dp) for q in range(n_dp)])  8.05 us
    all_to_all x1, waiting for transfers between devices, later_sum(): lax.all_to_all(suffix.astype(jnp.bfloat16), 'section', 0, 0, tiled=True)  7.14 us
    ppermute x3, starting transfers between devices, body(): lax.ppermute(cotan, 'dp', [(q, (q + k) % n_dp) for q in range(n_dp)])  5.88 us
  transfers between devices with their start and end apart: 13, of which 7 were waited for; matrix products, arithmetic and copies ran while one was open for 30% of the time, Pallas kernels for 0%

profile of v6, /device:TPU:1, one launch (start us, length us, event | category | flops | bytes accessed | tf_op | source)
XLA Modules:
  0.0 182.4 jit_solution(3612735300990810545)
XLA Ops:
  2.8 2.6 %collective-permute-start.1 = (bf16[2,128,512]{2,1,0:T(8,128)(2,1)}, bf16[2,128,512]{2,1,0:T(8,128)(2,1)S(1)}, u32[]{:S(2)}, u32[]{:S(2)}) collective-permute-start(bf16[2,128,512]{2,1,0:T(8,128)(2,1)} %bitcast.106), channel_id=1, source_target_pairs={{0,128},{64,192},{128,0},{192,64},{1,129},{65,193},{129,1},{193,65... | collective-permute-start | bytes 786440 | tf_op jit(solution)/shard_map/ppermute | solution.py:61
  9.0 8.0 %collective-permute-done.1 = bf16[2,128,512]{2,1,0:T(8,128)(2,1)S(1)} collective-permute-done((bf16[2,128,512]{2,1,0:T(8,128)(2,1)}, bf16[2,128,512]{2,1,0:T(8,128)(2,1)S(1)}, u32[]{:S(2)}, u32[]{:S(2)}) %collective-permute-start.1) | collective-permute-done | bytes 262176 | tf_op jit(solution)/shard_map/ppermute | solution.py:61
  21.7 2.4 %convolution_convert_fusion = bf16[2,16,32,2048]{3,2,1,0:T(8,128)(2,1)S(1)} fusion(bf16[2,16,32,512]{3,2,1,0:T(8,128)(2,1)S(1)} %bitcast.103, bf16[1,2048,512]{2,1,0:T(8,128)(2,1)S(1)} %copy-done), kind=kOutput, calls=%fused_computation.19 | convolution fusion | flops 2149580800 | bytes 7340032 | tf_op jit(solution)/shard_map/mjik,dk->jmid/dot_general | solution.py:67
  30.2 3.1 %constant_dynamic-slice_fusion.3 = (bf16[2,32,1,2048]{3,2,1,0:T(2,128)(2,1)}, bf16[2,32,1,2048]{3,2,1,0:T(2,128)(2,1)S(1)}, bf16[2,32,1,2048]{3,2,1,0:T(2,128)(2,1)S(1)}, bf16[2,32,1,2048]{3,2,1,0:T(2,128)(2,1)S(1)}) fusion(bf16[2,32,4,2048]{3,2,1,0:T(4,128)(2,1)S(1)} %reshape.126, s32[]{:T(128)S(6)} %select_n.88, s32[]{:T(128)S(6)} %select_n.94, ...), kind=kLoop, calls=%fused_computation.66 | loop fusion | bytes 2097168 | tf_op jit(solution)/shard_map/jit(dynamic_index_in_dim)/dynamic_slice | solution.py:104
  40.2 2.4 %fusion.11 = bf16[4,2,2,32,2048]{4,3,2,0,1:T(8,128)(2,1)S(1)} fusion(bf16[4,2,2,32,2048]{4,3,2,0,1:T(8,128)(2,1)} %collective-permute-done.3, bf16[4,2,1,2,32,2048]{5,4,2,1,0,3:T(8,128)(2,1)S(1)} %copy-done.5), kind=kLoop, calls=%fused_computation.17 | loop fusion | flops 4194304 | bytes 6291456 | tf_op jit(solution)/shard_map/convert_element_type | solution.py:77
  43.7 2.7 %collective-permute-start.4 = (bf16[4,2,32,2048]{3,2,1,0:T(8,128)(2,1)}, bf16[4,2,32,2048]{3,2,1,0:T(8,128)(2,1)}, u32[]{:S(2)}, u32[]{:S(2)}) collective-permute-start(bf16[4,2,32,2048]{3,2,1,0:T(8,128)(2,1)} %dynamic-slice_bitcast_fusion), channel_id=1, source_target_pairs={{0,2},{1,3},{2,0},{3,1},{4,6},{5,7},{6,4},{7,5},{8,10},{9,11},{10,... | collective-permute-start | bytes 3145736 | tf_op jit(solution)/shard_map/ppermute | solution.py:80
  46.6 2.9 %collective-permute-done.6 = bf16[2,32,2048]{2,1,0:T(8,128)(2,1)} collective-permute-done((bf16[2,32,2048]{2,1,0:T(8,128)(2,1)}, bf16[2,32,2048]{2,1,0:T(8,128)(2,1)}, u32[]{:S(2)}, u32[]{:S(2)}) %collective-permute-start.6) | collective-permute-done | bytes 262176 | tf_op jit(solution)/shard_map/ppermute | solution.py:108
  50.4 2.5 %fusion.32 = (bf16[1,4,2,32,2048]{4,3,2,1,0:T(8,128)(2,1)}, bf16[4,2,32,2048]{3,2,1,0:T(8,128)(2,1)}) fusion(bf16[1,2,32,2048]{3,2,1,0:T(8,128)(2,1)} %bitcast.24, bf16[1,2,32,2048]{3,2,1,0:T(8,128)(2,1)} %bitcast.23, bf16[1,2,32,2048]{3,2,1,0:T(8,128)(2,1)S(1)} %bitcast.104, bf16[1,2,32,2048]{3,2,1,0:T(8,128)(2,1)S(1)} %bitcast.102), kind=kLoop, calls=%fused_computation.78 | loop fusion | flops 1572864 | bytes 3145728 | tf_op jit(solution)/shard_map/stack | solution.py:112
  53.0 2.7 %collective-permute-start.8 = (bf16[4,2,32,2048]{3,2,1,0:T(8,128)(2,1)}, bf16[4,2,32,2048]{3,2,1,0:T(8,128)(2,1)}, u32[]{:S(2)}, u32[]{:S(2)}) collective-permute-start(bf16[4,2,32,2048]{3,2,1,0:T(8,128)(2,1)} %get-tuple-element.9), channel_id=1, source_target_pairs={{0,2},{1,3},{2,0},{3,1},{4,6},{5,7},{6,4},{7,5},{8,10},{9,11},{10,... | collective-permute-start | bytes 3145736 | tf_op jit(solution)/shard_map/ppermute | solution.py:111
  57.8 11.5 %collective-permute-done.4 = bf16[4,2,32,2048]{3,2,1,0:T(8,128)(2,1)} collective-permute-done((bf16[4,2,32,2048]{3,2,1,0:T(8,128)(2,1)}, bf16[4,2,32,2048]{3,2,1,0:T(8,128)(2,1)}, u32[]{:S(2)}, u32[]{:S(2)}) %collective-permute-start.4) | collective-permute-done | bytes 1048608 | tf_op jit(solution)/shard_map/ppermute | solution.py:80
  69.4 2.9 %fusion.15 = bf16[4,2,32,2048]{3,2,1,0:T(8,128)(2,1)} fusion(bf16[4,2,32,2048]{3,2,1,0:T(8,128)(2,1)} %collective-permute-done.4, bf16[4,2,2,32,2048]{4,3,2,0,1:T(8,128)(2,1)} %copy-done.6, s32[]{:T(128)S(6)} %select_n.84), kind=kLoop, calls=%fused_computation.32 | loop fusion | flops 2097152 | bytes 3145732 | tf_op jit(solution)/shard_map/convert_element_type | solution.py:81
  72.3 3.5 %all-to-all-start = ((bf16[4,2,32,2048]{3,2,1,0:T(8,128)(2,1)}), bf16[4,2,32,2048]{3,2,1,0:T(8,128)(2,1)S(1)}, u32[]{:S(2)}, u32[]{:S(2)}) async-start(bf16[4,2,32,2048]{3,2,1,0:T(8,128)(2,1)} %fusion.15), calls=%async_computation | async-start | bytes 2097152 | tf_op jit(solution)/shard_map/all_to_all | solution.py:82
  75.8 16.0 %collective-permute-done.8 = bf16[4,2,32,2048]{3,2,1,0:T(8,128)(2,1)} collective-permute-done((bf16[4,2,32,2048]{3,2,1,0:T(8,128)(2,1)}, bf16[4,2,32,2048]{3,2,1,0:T(8,128)(2,1)}, u32[]{:S(2)}, u32[]{:S(2)}) %collective-permute-start.8) | collective-permute-done | bytes 1048608 | tf_op jit(solution)/shard_map/ppermute | solution.py:111
  101.9 9.3 %all-to-all-start.1 = ((bf16[16,16,2048]{2,1,0:T(8,128)(2,1)}), bf16[16,16,2048]{2,1,0:T(8,128)(2,1)}, u32[]{:S(2)}, u32[]{:S(2)}) async-start(bf16[16,16,2048]{2,1,0:T(8,128)(2,1)} %bitcast.101), calls=%async_computation.1 | async-start | bytes 2097152 | tf_op jit(solution)/shard_map/all_to_all | solution.py:31
  112.6 2.5 %add_add_fusion = s32[2048,512]{1,0:T(8,128)} fusion(s32[]{:T(128)S(6)} %mul.161, s32[]{:T(128)} %bitcast.39, s32[]{:T(128)} %bitcast.38, s32[2048]{0:T(1024)S(1)} %multiply_add_fusion), kind=kLoop, calls=%fused_computation.18 | loop fusion | flops 5242880 | bytes 4202508 | tf_op jit(solution)/shard_map/add | solution.py:13
  115.5 2.8 %fusion.10 = bf16[2,2,4,2,32,2048]{5,4,3,2,0,1:T(8,128)(2,1)S(1)} fusion(bf16[1,2,4,2,32,2048]{5,4,3,2,1,0:T(8,128)(2,1)} %bitcast.28, bf16[1,2,4,2,32,2048]{5,4,3,2,1,0:T(8,128)(2,1)S(1)} %fusion.35, pred[]{:T(512)S(6)} %eq.13), kind=kLoop, calls=%fused_computation.15 | loop fusion | flops 6291456 | bytes 8388609 | tf_op jit(solution)/shard_map/transpose | solution.py:116
  120.6 16.8 %all-to-all-done.1 = bf16[16,16,2048]{2,1,0:T(8,128)(2,1)} async-done(((bf16[16,16,2048]{2,1,0:T(8,128)(2,1)}), bf16[16,16,2048]{2,1,0:T(8,128)(2,1)}, u32[]{:S(2)}, u32[]{:S(2)}) %all-to-all-start.1) | async-done | bytes 1048608 | tf_op jit(solution)/shard_map/all_to_all | solution.py:31
  140.2 5.6 %all-to-all-start.2 = ((bf16[16,16,2048]{2,1,0:T(8,128)(2,1)}), bf16[16,16,2048]{2,1,0:T(8,128)(2,1)}, u32[]{:S(2)}, u32[]{:S(2)}) async-start(bf16[16,16,2048]{2,1,0:T(8,128)(2,1)} %reduce-window_convert_fusion), calls=%async_computation.2 | async-start | bytes 2097152 | tf_op jit(solution)/shard_map/all_to_all | solution.py:34
  145.8 14.0 %fusion.9 = bf16[4,2048,512]{2,1,0:T(8,128)(2,1)S(1)} fusion(s32[4]{0:T(128)S(1)} %fusion.29, s32[2048,512]{1,0:T(8,128)} %add_add_fusion, bf16[4,4,2,32,2048]{4,3,2,1,0:T(8,128)(2,1)} %bitcast.99, bf16[1,2,4,32,512]{4,3,2,1,0:T(8,128)(2,1)} %bitcast.114, bf16[1,2,4,32,512]{4,3,2,1,0:T(8,128)(2,1)} %bitcast.112, bf16[1,2,4,32,512]{4,3,2,1,0:T(8,128)(2,1)} %bitcast.110, ...), kind=kOutput, calls=%fused_computation.13 | convolution fusion | flops 2220359680 | bytes 17825808 | tf_op jit(solution)/shard_map/tkmid,mktic->kdc/dot_general | solution.py:126
  159.9 3.3 %convert_reduce_fusion = f32[2048,512]{1,0:T(8,128)} fusion(bf16[4,2048,512]{2,1,0:T(8,128)(2,1)S(1)} %fusion.9), kind=kLoop, calls=%fused_computation.12 | loop fusion | flops 7340032 | bytes 12582912 | tf_op jit(solution)/shard_map/reduce_sum | solution.py:128
  163.2 7.1 %all-to-all-done.2 = bf16[16,16,2048]{2,1,0:T(8,128)(2,1)} async-done(((bf16[16,16,2048]{2,1,0:T(8,128)(2,1)}), bf16[16,16,2048]{2,1,0:T(8,128)(2,1)}, u32[]{:S(2)}, u32[]{:S(2)}) %all-to-all-start.2) | async-done | bytes 1048608 | tf_op jit(solution)/shard_map/all_to_all | solution.py:34
  171.8 4.1 %fusion.20 = f32[2,32,4,2048]{3,2,1,0:T(4,128)} fusion(f32[4,2,32,2048]{3,2,1,0:T(8,128)S(1)} %convert.7, f32[2,32]{1,0:T(2,128)S(1)} %broadcast_multiply_fusion, f32[2,32,4,2048]{3,2,1,0:T(4,128)S(1)} %reshape.131, f32[2,32]{1,0:T(2,128)S(1)} %add_rsqrt_fusion.1, f32[4,2048]{1,0:T(4,128)S(1)} %reshape.130, bf16[4,2,32,2048]{3,2,1,0:T(8,128)(2,1)S(1)} %all-to-all-done), kind=kLoop, calls=%fused_computation.40 | loop fusion | flops 3670016 | bytes 7373312 | tf_op jit(solution)/shard_map/transpose | solution.py:96
  175.9 3.8 %reshape.125 = f32[2,32,8192]{2,1,0:T(8,128)} reshape(f32[2,32,4,2048]{3,2,1,0:T(4,128)} %fusion.20) | data formatting | bytes 4194304 | tf_op jit(solution)/shard_map/reshape | solution.py:96
  179.7 2.7 %fusion.22 = bf16[1,2,32,8192]{3,2,1,0:T(8,128)(2,1)} fusion(f32[2,32,8192]{2,1,0:T(8,128)} %reshape.125, bf16[2,32,8192]{2,1,0:T(8,128)(2,1)S(1)} %copy-done.8), kind=kLoop, calls=%fused_computation.46 | loop fusion | flops 1572864 | bytes 4194304 | tf_op jit(solution)/shard_map/broadcast_in_dim | solution.py:129
  (77 shorter events, 44.6 us)
Async XLA Ops:
  0.6 21.0 %copy-start = (bf16[1,2048,512]{2,1,0:T(8,128)(2,1)S(1)}, bf16[1,2048,512]{2,1,0:T(8,128)(2,1)}, u32[]{:S(2)}) copy-start(bf16[1,2048,512]{2,1,0:T(8,128)(2,1)} %param.9) | copy-start | bytes 6291460
  0.6 8.3 %collective-permute-start = (bf16[2,128,512]{2,1,0:T(8,128)(2,1)}, bf16[2,128,512]{2,1,0:T(8,128)(2,1)S(1)}, u32[]{:S(2)}, u32[]{:S(2)}) collective-permute-start(bf16[2,128,512]{2,1,0:T(8,128)(2,1)} %bitcast.105), channel_id=1, source_target_pairs={{0,64},{64,128},{128,192},{192,0},{1,65},{65,129},{129,193},{193,1... | collective-permute-start | bytes 786440 | tf_op jit(solution)/shard_map/ppermute | solution.py:61
  2.8 14.2 %collective-permute-start.1 = (bf16[2,128,512]{2,1,0:T(8,128)(2,1)}, bf16[2,128,512]{2,1,0:T(8,128)(2,1)S(1)}, u32[]{:S(2)}, u32[]{:S(2)}) collective-permute-start(bf16[2,128,512]{2,1,0:T(8,128)(2,1)} %bitcast.106), channel_id=1, source_target_pairs={{0,128},{64,192},{128,0},{192,64},{1,129},{65,193},{129,1},{193,65... | collective-permute-start | bytes 786440 | tf_op jit(solution)/shard_map/ppermute | solution.py:61
  5.5 11.6 %collective-permute-start.2 = (bf16[2,128,512]{2,1,0:T(8,128)(2,1)}, bf16[2,128,512]{2,1,0:T(8,128)(2,1)S(1)}, u32[]{:S(2)}, u32[]{:S(2)}) collective-permute-start(bf16[2,128,512]{2,1,0:T(8,128)(2,1)} %bitcast.107), channel_id=1, source_target_pairs={{0,192},{64,0},{128,64},{192,128},{1,193},{65,1},{129,65},{193,129... | collective-permute-start | bytes 786440 | tf_op jit(solution)/shard_map/ppermute | solution.py:61
  9.0 8.1 %copy-start.10 = (bf16[2,128,512]{2,1,0:T(8,128)(2,1)}, bf16[2,128,512]{2,1,0:T(8,128)(2,1)S(1)}, u32[]{:S(2)}) copy-start(bf16[2,128,512]{2,1,0:T(8,128)(2,1)S(1)} %collective-permute-done) | copy-start | bytes 786436
  25.9 3.1 %copy-start.4 = (bf16[1,2,32,8192]{3,2,1,0:T(8,128)(2,1)S(1)}, bf16[1,2,32,8192]{3,2,1,0:T(8,128)(2,1)}, u32[]{:S(2)}) copy-start(bf16[1,2,32,8192]{3,2,1,0:T(8,128)(2,1)} %param.7) | copy-start | bytes 3145732
  27.5 12.7 %collective-permute-start.3 = (bf16[4,2,2,32,2048]{4,3,2,0,1:T(8,128)(2,1)}, bf16[4,2,2,32,2048]{4,3,2,0,1:T(8,128)(2,1)}, u32[]{:S(2)}, u32[]{:S(2)}) collective-permute-start(bf16[4,2,2,32,2048]{4,3,2,0,1:T(8,128)(2,1)} %bitcast.91), channel_id=1, source_target_pairs={{0,1},{1,0},{2,3},{3,2},{4,5},{5,4},{6,7},{7,6},{8,9},{9,8},{10,11... | collective-permute-start | bytes 6291464 | tf_op jit(solution)/shard_map/ppermute | solution.py:76
  33.3 6.9 %copy-start.5 = (bf16[4,2,1,2,32,2048]{5,4,2,1,0,3:T(8,128)(2,1)S(1)}, bf16[4,2,1,2,32,2048]{5,4,2,1,0,3:T(8,128)(2,1)}, u32[]{:S(2)}) copy-start(bf16[4,2,1,2,32,2048]{5,4,2,1,0,3:T(8,128)(2,1)} %get-tuple-element.6) | copy-start | bytes 6291460
  34.2 12.4 %collective-permute-start.5 = (bf16[2,32,2048]{2,1,0:T(8,128)(2,1)}, bf16[2,32,2048]{2,1,0:T(8,128)(2,1)S(1)}, u32[]{:S(2)}, u32[]{:S(2)}) collective-permute-start(bf16[2,32,2048]{2,1,0:T(8,128)(2,1)} %bitcast.94), channel_id=1, source_target_pairs={{0,64},{64,128},{128,192},{192,0},{1,65},{65,129},{129,193},{193,1... | collective-permute-start | bytes 786440 | tf_op jit(solution)/shard_map/ppermute | solution.py:108
  35.9 13.6 %collective-permute-start.6 = (bf16[2,32,2048]{2,1,0:T(8,128)(2,1)}, bf16[2,32,2048]{2,1,0:T(8,128)(2,1)}, u32[]{:S(2)}, u32[]{:S(2)}) collective-permute-start(bf16[2,32,2048]{2,1,0:T(8,128)(2,1)} %bitcast.93), channel_id=1, source_target_pairs={{0,128},{64,192},{128,0},{192,64},{1,129},{65,193},{129,1},{193,65... | collective-permute-start | bytes 786440 | tf_op jit(solution)/shard_map/ppermute | solution.py:108
  38.9 11.5 %collective-permute-start.7 = (bf16[2,32,2048]{2,1,0:T(8,128)(2,1)}, bf16[2,32,2048]{2,1,0:T(8,128)(2,1)}, u32[]{:S(2)}, u32[]{:S(2)}) collective-permute-start(bf16[2,32,2048]{2,1,0:T(8,128)(2,1)} %bitcast.92), channel_id=1, source_target_pairs={{0,192},{64,0},{128,64},{192,128},{1,193},{65,1},{129,65},{193,129... | collective-permute-start | bytes 786440 | tf_op jit(solution)/shard_map/ppermute | solution.py:108
  42.6 10.4 %copy-start.6 = (bf16[4,2,2,32,2048]{4,3,2,0,1:T(8,128)(2,1)}, bf16[4,2,2,32,2048]{4,3,2,0,1:T(8,128)(2,1)S(1)}, u32[]{:S(2)}) copy-start(bf16[4,2,2,32,2048]{4,3,2,0,1:T(8,128)(2,1)S(1)} %fusion.11) | copy-start | bytes 6291460
  42.6 3.8 %copy-start.7 = (bf16[2,32,1,2048]{3,2,1,0:T(2,128)(2,1)S(1)}, bf16[2,32,1,2048]{3,2,1,0:T(2,128)(2,1)}, u32[]{:S(2)}) copy-start(bf16[2,32,1,2048]{3,2,1,0:T(2,128)(2,1)} %get-tuple-element.10) | copy-start | bytes 786436
  43.7 25.7 %collective-permute-start.4 = (bf16[4,2,32,2048]{3,2,1,0:T(8,128)(2,1)}, bf16[4,2,32,2048]{3,2,1,0:T(8,128)(2,1)}, u32[]{:S(2)}, u32[]{:S(2)}) collective-permute-start(bf16[4,2,32,2048]{3,2,1,0:T(8,128)(2,1)} %dynamic-slice_bitcast_fusion), channel_id=1, source_target_pairs={{0,2},{1,3},{2,0},{3,1},{4,6},{5,7},{6,4},{7,5},{8,10},{9,11},{10,... | collective-permute-start | bytes 3145736 | tf_op jit(solution)/shard_map/ppermute | solution.py:80
  53.0 4.4 %copy-start.13 = (bf16[1,8192]{1,0:T(2,128)(2,1)S(1)}, bf16[1,8192]{1,0:T(2,128)(2,1)}, u32[]{:S(2)}) copy-start(bf16[1,8192]{1,0:T(2,128)(2,1)} %param.10) | copy-start | bytes 49156
  53.0 38.9 %collective-permute-start.8 = (bf16[4,2,32,2048]{3,2,1,0:T(8,128)(2,1)}, bf16[4,2,32,2048]{3,2,1,0:T(8,128)(2,1)}, u32[]{:S(2)}, u32[]{:S(2)}) collective-permute-start(bf16[4,2,32,2048]{3,2,1,0:T(8,128)(2,1)} %get-tuple-element.9), channel_id=1, source_target_pairs={{0,2},{1,3},{2,0},{3,1},{4,6},{5,7},{6,4},{7,5},{8,10},{9,11},{10,... | collective-permute-start | bytes 3145736 | tf_op jit(solution)/shard_map/ppermute | solution.py:111
  72.3 25.0 %all-to-all-start = ((bf16[4,2,32,2048]{3,2,1,0:T(8,128)(2,1)}), bf16[4,2,32,2048]{3,2,1,0:T(8,128)(2,1)S(1)}, u32[]{:S(2)}, u32[]{:S(2)}) async-start(bf16[4,2,32,2048]{3,2,1,0:T(8,128)(2,1)} %fusion.15), calls=%async_computation | async-start | bytes 2097152 | tf_op jit(solution)/shard_map/all_to_all | solution.py:82
  95.5 20.0 %collective-permute-start.9 = (bf16[2,4,2,32,2048]{4,3,2,1,0:T(8,128)(2,1)}, bf16[2,4,2,32,2048]{4,3,2,1,0:T(8,128)(2,1)}, u32[]{:S(2)}, u32[]{:S(2)}) collective-permute-start(bf16[2,4,2,32,2048]{4,3,2,1,0:T(8,128)(2,1)} %reverse_select_fusion), channel_id=1, source_target_pairs={{0,1},{1,0},{2,3},{3,2},{4,5},{5,4},{6,7},{7,6},{8,9},{9,8},{10,11... | collective-permute-start | bytes 6291464 | tf_op jit(solution)/shard_map/ppermute | solution.py:114
  101.9 35.5 %all-to-all-start.1 = ((bf16[16,16,2048]{2,1,0:T(8,128)(2,1)}), bf16[16,16,2048]{2,1,0:T(8,128)(2,1)}, u32[]{:S(2)}, u32[]{:S(2)}) async-start(bf16[16,16,2048]{2,1,0:T(8,128)(2,1)} %bitcast.101), calls=%async_computation.1 | async-start | bytes 2097152 | tf_op jit(solution)/shard_map/all_to_all | solution.py:31
  112.6 2.5 %copy-start.3 = (bf16[2,4,2,32,2048]{4,3,2,1,0:T(8,128)(2,1)S(1)}, bf16[2,4,2,32,2048]{4,3,2,1,0:T(8,128)(2,1)}, u32[]{:S(2)}) copy-start(bf16[2,4,2,32,2048]{4,3,2,1,0:T(8,128)(2,1)} %copy-done.2) | copy-start | bytes 6291460
  138.7 7.1 %copy-start.9 = (bf16[1,2,128,512]{3,2,1,0:T(8,128)(2,1)S(1)}, bf16[1,2,128,512]{3,2,1,0:T(8,128)(2,1)}, u32[]{:S(2)}) copy-start(bf16[1,2,128,512]{3,2,1,0:T(8,128)(2,1)} %param.8) | copy-start | bytes 786436
  140.2 30.1 %all-to-all-start.2 = ((bf16[16,16,2048]{2,1,0:T(8,128)(2,1)}), bf16[16,16,2048]{2,1,0:T(8,128)(2,1)}, u32[]{:S(2)}, u32[]{:S(2)}) async-start(bf16[16,16,2048]{2,1,0:T(8,128)(2,1)} %reduce-window_convert_fusion), calls=%async_computation.2 | async-start | bytes 2097152 | tf_op jit(solution)/shard_map/all_to_all | solution.py:34
  175.9 3.8 %copy-start.8 = (bf16[2,32,8192]{2,1,0:T(8,128)(2,1)S(1)}, bf16[2,32,8192]{2,1,0:T(8,128)(2,1)}, u32[]{:S(2)}) copy-start(bf16[2,32,8192]{2,1,0:T(8,128)(2,1)} %param.11) | copy-start | bytes 3145732
  175.9 6.6 %copy-start.1 = (bf16[1,2048,512]{2,1,0:T(8,128)(2,1)S(1)}, bf16[1,2048,512]{2,1,0:T(8,128)(2,1)}, u32[]{:S(2)}) copy-start(bf16[1,2048,512]{2,1,0:T(8,128)(2,1)} %param.9) | copy-start | bytes 6291460
  (3 other events, 3.5 us)

commit v7 on v6

--- a/solution.py
+++ b/solution.py
@@ -90,11 +90,11 @@
         hidden_gradient
         - centered4 * jnp.mean(hidden_gradient * centered4, axis=(0, 3), keepdims=True)
     )
+    top4 = top_grad.reshape(mb, tok_dev, n_dp, rows_p).transpose(2, 0, 1, 3)
+    ahead = lax.optimization_barrier(top4.astype(jnp.float32) + branch4)
     later4 = later_sum(branch4)
-    grad_in = (
-        top_grad.astype(jnp.float32)
-        + (branch4 + later4).transpose(1, 2, 0, 3).reshape(mb, tok_dev, d_model)
-    ).astype(jnp.bfloat16)
+    grad4 = (ahead + later4).astype(jnp.bfloat16)
+    grad_in = grad4.transpose(1, 2, 0, 3).reshape(mb, tok_dev, d_model)
 
     own_input, own_gain = lax.optimization_barrier((saved_input[0], norm_gain[0]))
     own_float = own_input.astype(jnp.float32)

time: 186 us -> 181 us (0.973)
  the two profiles are of different devices: /device:TPU:1 before, /device:TPU:4 now
where the time goes in v7:
time: 181 us
  waiting for transfers between devices  71.6 us (40%)
  other arithmetic  36.1 us (20%)
  starting transfers between devices  28.6 us (16%)
  local copies, waits for them, and re-layouts  26.1 us (14%)
  matrix products  16.1 us (9%)
  between operations  2.29 us (1%)
    all_to_all x1, waiting for transfers between devices, later_sum(): got = lax.all_to_all(chunks, 'section', 0, 0, tiled=True)  20 us
    ppermute x1, waiting for transfers between devices, body(): far = lax.ppermute(mine, 'tensor', [(q, q ^ 2) for q in range(n_t)])  14.7 us
    dot_general x1, matrix products, body(): jnp.einsum('tkmid,mktic->kdc', nrm, cot_sel, preferred_element_type=jnp.f...  13.7 us
    ppermute x1, waiting for transfers between devices, body(): recv = lax.ppermute(send, 'tensor', [(q, q ^ 2) for q in range(n_t)])  13.2 us
    all_to_all x1, waiting for transfers between devices, later_sum(): lax.all_to_all(suffix.astype(jnp.bfloat16), 'section', 0, 0, tiled=True)  10.5 us
    all_to_all x1, starting transfers between devices, later_sum(): got = lax.all_to_all(chunks, 'section', 0, 0, tiled=True)  9.21 us
    ppermute x3, waiting for transfers between devices, body(): lax.ppermute(cotan, 'dp', [(q, (q + k) % n_dp) for q in range(n_dp)])  8.08 us
    ppermute x3, starting transfers between devices, body(): lax.ppermute(cotan, 'dp', [(q, (q + k) % n_dp) for q in range(n_dp)])  5.9 us
  transfers between devices with their start and end apart: 13, of which 8 were waited for; matrix products, arithmetic and copies ran while one was open for 33% of the time, Pallas kernels for 0%

profile of v7, /device:TPU:4, one launch (start us, length us, event | category | flops | bytes accessed | tf_op | source)
XLA Modules:
  0.0 180.7 jit_solution(14122969765671960497)
XLA Ops:
  2.3 2.9 %collective-permute-start.1 = (bf16[2,128,512]{2,1,0:T(8,128)(2,1)}, bf16[2,128,512]{2,1,0:T(8,128)(2,1)S(1)}, u32[]{:S(2)}, u32[]{:S(2)}) collective-permute-start(bf16[2,128,512]{2,1,0:T(8,128)(2,1)} %bitcast.106), channel_id=1, source_target_pairs={{0,128},{64,192},{128,0},{192,64},{1,129},{65,193},{129,1},{193,65... | collective-permute-start | bytes 786440 | tf_op jit(solution)/shard_map/ppermute | solution.py:61
  10.3 6.8 %collective-permute-done.1 = bf16[2,128,512]{2,1,0:T(8,128)(2,1)S(1)} collective-permute-done((bf16[2,128,512]{2,1,0:T(8,128)(2,1)}, bf16[2,128,512]{2,1,0:T(8,128)(2,1)S(1)}, u32[]{:S(2)}, u32[]{:S(2)}) %collective-permute-start.1) | collective-permute-done | bytes 262176 | tf_op jit(solution)/shard_map/ppermute | solution.py:61
  21.7 2.4 %convolution_convert_fusion = bf16[2,16,32,2048]{3,2,1,0:T(8,128)(2,1)S(1)} fusion(bf16[2,16,32,512]{3,2,1,0:T(8,128)(2,1)S(1)} %bitcast.103, bf16[1,2048,512]{2,1,0:T(8,128)(2,1)S(1)} %copy-done), kind=kOutput, calls=%fused_computation.19 | convolution fusion | flops 2149580800 | bytes 7340032 | tf_op jit(solution)/shard_map/mjik,dk->jmid/dot_general | solution.py:67
  28.7 3.1 %constant_dynamic-slice_fusion.3 = (bf16[2,32,1,2048]{3,2,1,0:T(2,128)(2,1)}, bf16[2,32,1,2048]{3,2,1,0:T(2,128)(2,1)S(1)}, bf16[2,32,1,2048]{3,2,1,0:T(2,128)(2,1)S(1)}, bf16[2,32,1,2048]{3,2,1,0:T(2,128)(2,1)S(1)}) fusion(bf16[2,32,4,2048]{3,2,1,0:T(4,128)(2,1)S(1)} %reshape.125, s32[]{:T(128)S(6)} %select_n.88, s32[]{:T(128)S(6)} %select_n.94, ...), kind=kLoop, calls=%fused_computation.66 | loop fusion | bytes 2097168 | tf_op jit(solution)/shard_map/jit(dynamic_index_in_dim)/dynamic_slice | solution.py:104
  34.8 2.4 %collective-permute-start.6 = (bf16[2,32,2048]{2,1,0:T(8,128)(2,1)}, bf16[2,32,2048]{2,1,0:T(8,128)(2,1)}, u32[]{:S(2)}, u32[]{:S(2)}) collective-permute-start(bf16[2,32,2048]{2,1,0:T(8,128)(2,1)} %bitcast.93), channel_id=1, source_target_pairs={{0,128},{64,192},{128,0},{192,64},{1,129},{65,193},{129,1},{193,65... | collective-permute-start | bytes 786440 | tf_op jit(solution)/shard_map/ppermute | solution.py:108
  39.6 2.4 %fusion.11 = bf16[4,2,2,32,2048]{4,3,2,0,1:T(8,128)(2,1)S(1)} fusion(bf16[4,2,2,32,2048]{4,3,2,0,1:T(8,128)(2,1)} %collective-permute-done.3, bf16[4,2,1,2,32,2048]{5,4,2,1,0,3:T(8,128)(2,1)S(1)} %copy-done.5), kind=kLoop, calls=%fused_computation.17 | loop fusion | flops 4194304 | bytes 6291456 | tf_op jit(solution)/shard_map/convert_element_type | solution.py:77
  45.0 3.9 %collective-permute-done.6 = bf16[2,32,2048]{2,1,0:T(8,128)(2,1)} collective-permute-done((bf16[2,32,2048]{2,1,0:T(8,128)(2,1)}, bf16[2,32,2048]{2,1,0:T(8,128)(2,1)}, u32[]{:S(2)}, u32[]{:S(2)}) %collective-permute-start.6) | collective-permute-done | bytes 262176 | tf_op jit(solution)/shard_map/ppermute | solution.py:108
  50.1 2.5 %fusion.32 = (bf16[1,4,2,32,2048]{4,3,2,1,0:T(8,128)(2,1)}, bf16[4,2,32,2048]{3,2,1,0:T(8,128)(2,1)}) fusion(bf16[1,2,32,2048]{3,2,1,0:T(8,128)(2,1)} %bitcast.24, bf16[1,2,32,2048]{3,2,1,0:T(8,128)(2,1)} %bitcast.23, bf16[1,2,32,2048]{3,2,1,0:T(8,128)(2,1)S(1)} %bitcast.104, bf16[1,2,32,2048]{3,2,1,0:T(8,128)(2,1)S(1)} %bitcast.102), kind=kLoop, calls=%fused_computation.78 | loop fusion | flops 1572864 | bytes 3145728 | tf_op jit(solution)/shard_map/stack | solution.py:112
  55.0 3.7 %reshape.132 = f32[2,32,4,2048]{3,2,1,0:T(4,128)} reshape(bf16[2,32,8192]{2,1,0:T(8,128)(2,1)} %param.11) | data formatting | bytes 3145728 | tf_op jit(solution)/shard_map/convert_element_type | solution.py:94
  59.0 13.2 %collective-permute-done.4 = bf16[4,2,32,2048]{3,2,1,0:T(8,128)(2,1)} collective-permute-done((bf16[4,2,32,2048]{3,2,1,0:T(8,128)(2,1)}, bf16[4,2,32,2048]{3,2,1,0:T(8,128)(2,1)}, u32[]{:S(2)}, u32[]{:S(2)}) %collective-permute-start.4) | collective-permute-done | bytes 1048608 | tf_op jit(solution)/shard_map/ppermute | solution.py:80
  72.2 2.9 %fusion.15 = bf16[4,2,32,2048]{3,2,1,0:T(8,128)(2,1)} fusion(bf16[4,2,32,2048]{3,2,1,0:T(8,128)(2,1)} %collective-permute-done.4, bf16[4,2,2,32,2048]{4,3,2,0,1:T(8,128)(2,1)} %copy-done.6, s32[]{:T(128)S(6)} %select_n.84), kind=kLoop, calls=%fused_computation.32 | loop fusion | flops 2097152 | bytes 3145732 | tf_op jit(solution)/shard_map/convert_element_type | solution.py:81
  75.1 3.5 %all-to-all-start = ((bf16[4,2,32,2048]{3,2,1,0:T(8,128)(2,1)}), bf16[4,2,32,2048]{3,2,1,0:T(8,128)(2,1)S(1)}, u32[]{:S(2)}, u32[]{:S(2)}) async-start(bf16[4,2,32,2048]{3,2,1,0:T(8,128)(2,1)} %fusion.15), calls=%async_computation | async-start | bytes 2097152 | tf_op jit(solution)/shard_map/all_to_all | solution.py:82
  78.6 14.7 %collective-permute-done.8 = bf16[4,2,32,2048]{3,2,1,0:T(8,128)(2,1)} collective-permute-done((bf16[4,2,32,2048]{3,2,1,0:T(8,128)(2,1)}, bf16[4,2,32,2048]{3,2,1,0:T(8,128)(2,1)}, u32[]{:S(2)}, u32[]{:S(2)}) %collective-permute-start.8) | collective-permute-done | bytes 1048608 | tf_op jit(solution)/shard_map/ppermute | solution.py:111
  98.7 3.4 %fusion.28 = (bf16[4,2,32,2048]{3,0,2,1:T(4,128)(2,1)S(1)}, f32[4,2,32,2048]{3,0,2,1:T(4,128)}) fusion(f32[2,32]{1,0:T(2,128)S(1)} %broadcast_multiply_fusion, f32[2,32,4,2048]{3,2,1,0:T(4,128)S(1)} %reshape.130, f32[2,32]{1,0:T(2,128)S(1)} %add_rsqrt_fusion.1, f32[4,2048]{1,0:T(4,128)S(1)} %reshape.129, bf16[4,2,32,2048]{3,2,1,0:T(8,128)(2,1)S(1)} %all-to-all-done, ...), kind=kLoop, calls=%fused_computation.60 | loop fusion | flops 4194304 | bytes 8421888 | tf_op jit(solution)/shard_map/convert_element_type | solution.py:30
  103.7 9.2 %all-to-all-start.1 = ((bf16[16,16,2048]{2,1,0:T(8,128)(2,1)}), bf16[16,16,2048]{2,1,0:T(8,128)(2,1)S(1)}, u32[]{:S(2)}, u32[]{:S(2)}) async-start(bf16[16,16,2048]{2,1,0:T(8,128)(2,1)} %bitcast.19), calls=%async_computation.1 | async-start | bytes 2097152 | tf_op jit(solution)/shard_map/all_to_all | solution.py:31
  114.2 2.5 %add_add_fusion = s32[2048,512]{1,0:T(8,128)} fusion(s32[]{:T(128)S(6)} %mul.161, s32[]{:T(128)} %bitcast.39, s32[]{:T(128)} %bitcast.38, s32[2048]{0:T(1024)S(1)} %multiply_add_fusion), kind=kLoop, calls=%fused_computation.18 | loop fusion | flops 5242880 | bytes 4202508 | tf_op jit(solution)/shard_map/add | solution.py:13
  117.2 2.8 %fusion.10 = bf16[2,2,4,2,32,2048]{5,4,3,2,0,1:T(8,128)(2,1)S(1)} fusion(bf16[1,2,4,2,32,2048]{5,4,3,2,1,0:T(8,128)(2,1)} %bitcast.28, bf16[1,2,4,2,32,2048]{5,4,3,2,1,0:T(8,128)(2,1)S(1)} %fusion.35, pred[]{:T(512)S(6)} %eq.13), kind=kLoop, calls=%fused_computation.15 | loop fusion | flops 6291456 | bytes 8388609 | tf_op jit(solution)/shard_map/transpose | solution.py:116
  120.0 2.3 %copy.50 = bf16[2,2,4,2,32,2048]{5,4,3,2,1,0:T(8,128)(2,1)} copy(bf16[2,2,4,2,32,2048]{5,4,3,2,0,1:T(8,128)(2,1)S(1)} %fusion.10) | data formatting | bytes 8388608 | tf_op jit(solution)/shard_map/transpose | solution.py:116
  122.3 20.0 %all-to-all-done.1 = bf16[16,16,2048]{2,1,0:T(8,128)(2,1)S(1)} async-done(((bf16[16,16,2048]{2,1,0:T(8,128)(2,1)}), bf16[16,16,2048]{2,1,0:T(8,128)(2,1)S(1)}, u32[]{:S(2)}, u32[]{:S(2)}) %all-to-all-start.1) | async-done | bytes 1048608 | tf_op jit(solution)/shard_map/all_to_all | solution.py:31
  144.0 3.9 %all-to-all-start.2 = ((bf16[16,16,2048]{2,1,0:T(8,128)(2,1)}), bf16[16,16,2048]{2,1,0:T(8,128)(2,1)S(1)}, u32[]{:S(2)}, u32[]{:S(2)}) async-start(bf16[16,16,2048]{2,1,0:T(8,128)(2,1)} %reduce-window_convert_fusion), calls=%async_computation.2 | async-start | bytes 2097152 | tf_op jit(solution)/shard_map/all_to_all | solution.py:34
  147.9 13.7 %fusion.9 = bf16[4,2048,512]{2,1,0:T(8,128)(2,1)S(1)} fusion(s32[4]{0:T(128)S(1)} %fusion.29, s32[2048,512]{1,0:T(8,128)} %add_add_fusion, bf16[4,4,2,32,2048]{4,3,2,1,0:T(8,128)(2,1)} %bitcast.100, bf16[1,2,4,32,512]{4,3,2,1,0:T(8,128)(2,1)S(1)} %bitcast.114, bf16[1,2,4,32,512]{4,3,2,1,0:T(8,128)(2,1)S(1)} %bitcast.112, ...), kind=kOutput, calls=%fused_computation.13 | convolution fusion | flops 2220359680 | bytes 17825808 | tf_op jit(solution)/shard_map/tkmid,mktic->kdc/dot_general | solution.py:126
  161.6 3.3 %convert_reduce_fusion = f32[2048,512]{1,0:T(8,128)} fusion(bf16[4,2048,512]{2,1,0:T(8,128)(2,1)S(1)} %fusion.9), kind=kLoop, calls=%fused_computation.12 | loop fusion | flops 7340032 | bytes 12582912 | tf_op jit(solution)/shard_map/reduce_sum | solution.py:128
  165.0 10.5 %all-to-all-done.2 = bf16[16,16,2048]{2,1,0:T(8,128)(2,1)S(1)} async-done(((bf16[16,16,2048]{2,1,0:T(8,128)(2,1)}), bf16[16,16,2048]{2,1,0:T(8,128)(2,1)S(1)}, u32[]{:S(2)}, u32[]{:S(2)}) %all-to-all-start.2) | async-done | bytes 1048608 | tf_op jit(solution)/shard_map/all_to_all | solution.py:34
  175.7 3.4 %fusion.22 = bf16[2,32,4,2048]{3,2,1,0:T(4,128)(2,1)S(1)} fusion(f32[4,2,32,2048]{3,0,2,1:T(4,128)} %get-tuple-element.9, f32[4,2,32,2048]{3,2,1,0:T(8,128)S(1)} %convert.9), kind=kLoop, calls=%fused_computation.46 | loop fusion | flops 1048576 | bytes 5242880 | tf_op jit(solution)/shard_map/transpose | solution.py:97
  (83 shorter events, 38.9 us)
Async XLA Ops:
  0.6 21.1 %copy-start = (bf16[1,2048,512]{2,1,0:T(8,128)(2,1)S(1)}, bf16[1,2048,512]{2,1,0:T(8,128)(2,1)}, u32[]{:S(2)}) copy-start(bf16[1,2048,512]{2,1,0:T(8,128)(2,1)} %param.9) | copy-start | bytes 6291460
  0.6 9.6 %collective-permute-start = (bf16[2,128,512]{2,1,0:T(8,128)(2,1)}, bf16[2,128,512]{2,1,0:T(8,128)(2,1)S(1)}, u32[]{:S(2)}, u32[]{:S(2)}) collective-permute-start(bf16[2,128,512]{2,1,0:T(8,128)(2,1)} %bitcast.105), channel_id=1, source_target_pairs={{0,64},{64,128},{128,192},{192,0},{1,65},{65,129},{129,193},{193,1... | collective-permute-start | bytes 786440 | tf_op jit(solution)/shard_map/ppermute | solution.py:61
  2.3 14.7 %collective-permute-start.1 = (bf16[2,128,512]{2,1,0:T(8,128)(2,1)}, bf16[2,128,512]{2,1,0:T(8,128)(2,1)S(1)}, u32[]{:S(2)}, u32[]{:S(2)}) collective-permute-start(bf16[2,128,512]{2,1,0:T(8,128)(2,1)} %bitcast.106), channel_id=1, source_target_pairs={{0,128},{64,192},{128,0},{192,64},{1,129},{65,193},{129,1},{193,65... | collective-permute-start | bytes 786440 | tf_op jit(solution)/shard_map/ppermute | solution.py:61
  5.2 11.9 %collective-permute-start.2 = (bf16[2,128,512]{2,1,0:T(8,128)(2,1)}, bf16[2,128,512]{2,1,0:T(8,128)(2,1)S(1)}, u32[]{:S(2)}, u32[]{:S(2)}) collective-permute-start(bf16[2,128,512]{2,1,0:T(8,128)(2,1)} %bitcast.107), channel_id=1, source_target_pairs={{0,192},{64,0},{128,64},{192,128},{1,193},{65,1},{129,65},{193,129... | collective-permute-start | bytes 786440 | tf_op jit(solution)/shard_map/ppermute | solution.py:61
  10.3 6.8 %copy-start.10 = (bf16[2,128,512]{2,1,0:T(8,128)(2,1)}, bf16[2,128,512]{2,1,0:T(8,128)(2,1)S(1)}, u32[]{:S(2)}) copy-start(bf16[2,128,512]{2,1,0:T(8,128)(2,1)S(1)} %collective-permute-done) | copy-start | bytes 786436
  27.6 12.0 %collective-permute-start.3 = (bf16[4,2,2,32,2048]{4,3,2,0,1:T(8,128)(2,1)}, bf16[4,2,2,32,2048]{4,3,2,0,1:T(8,128)(2,1)}, u32[]{:S(2)}, u32[]{:S(2)}) collective-permute-start(bf16[4,2,2,32,2048]{4,3,2,0,1:T(8,128)(2,1)} %bitcast.91), channel_id=1, source_target_pairs={{0,1},{1,0},{2,3},{3,2},{4,5},{5,4},{6,7},{7,6},{8,9},{9,8},{10,11... | collective-permute-start | bytes 6291464 | tf_op jit(solution)/shard_map/ppermute | solution.py:76
  31.9 7.7 %copy-start.5 = (bf16[4,2,1,2,32,2048]{5,4,2,1,0,3:T(8,128)(2,1)S(1)}, bf16[4,2,1,2,32,2048]{5,4,2,1,0,3:T(8,128)(2,1)}, u32[]{:S(2)}) copy-start(bf16[4,2,1,2,32,2048]{5,4,2,1,0,3:T(8,128)(2,1)} %get-tuple-element.6) | copy-start | bytes 6291460
  32.8 12.3 %collective-permute-start.5 = (bf16[2,32,2048]{2,1,0:T(8,128)(2,1)}, bf16[2,32,2048]{2,1,0:T(8,128)(2,1)S(1)}, u32[]{:S(2)}, u32[]{:S(2)}) collective-permute-start(bf16[2,32,2048]{2,1,0:T(8,128)(2,1)} %bitcast.94), channel_id=1, source_target_pairs={{0,64},{64,128},{128,192},{192,0},{1,65},{65,129},{129,193},{193,1... | collective-permute-start | bytes 786440 | tf_op jit(solution)/shard_map/ppermute | solution.py:108
  34.8 14.1 %collective-permute-start.6 = (bf16[2,32,2048]{2,1,0:T(8,128)(2,1)}, bf16[2,32,2048]{2,1,0:T(8,128)(2,1)}, u32[]{:S(2)}, u32[]{:S(2)}) collective-permute-start(bf16[2,32,2048]{2,1,0:T(8,128)(2,1)} %bitcast.93), channel_id=1, source_target_pairs={{0,128},{64,192},{128,0},{192,64},{1,129},{65,193},{129,1},{193,65... | collective-permute-start | bytes 786440 | tf_op jit(solution)/shard_map/ppermute | solution.py:108
  38.1 12.1 %collective-permute-start.7 = (bf16[2,32,2048]{2,1,0:T(8,128)(2,1)}, bf16[2,32,2048]{2,1,0:T(8,128)(2,1)}, u32[]{:S(2)}, u32[]{:S(2)}) collective-permute-start(bf16[2,32,2048]{2,1,0:T(8,128)(2,1)} %bitcast.92), channel_id=1, source_target_pairs={{0,192},{64,0},{128,64},{192,128},{1,193},{65,1},{129,65},{193,129... | collective-permute-start | bytes 786440 | tf_op jit(solution)/shard_map/ppermute | solution.py:108
  44.4 27.9 %collective-permute-start.4 = (bf16[4,2,32,2048]{3,2,1,0:T(8,128)(2,1)}, bf16[4,2,32,2048]{3,2,1,0:T(8,128)(2,1)}, u32[]{:S(2)}, u32[]{:S(2)}) collective-permute-start(bf16[4,2,32,2048]{3,2,1,0:T(8,128)(2,1)} %dynamic-slice_bitcast_fusion), channel_id=1, source_target_pairs={{0,2},{1,3},{2,0},{3,1},{4,6},{5,7},{6,4},{7,5},{8,10},{9,11},{10,... | collective-permute-start | bytes 3145736 | tf_op jit(solution)/shard_map/ppermute | solution.py:80
  52.7 2.2 %copy-start.16 = (bf16[1,8192]{1,0:T(2,128)(2,1)S(1)}, bf16[1,8192]{1,0:T(2,128)(2,1)}, u32[]{:S(2)}) copy-start(bf16[1,8192]{1,0:T(2,128)(2,1)} %param.10) | copy-start | bytes 49156
  52.7 40.7 %collective-permute-start.8 = (bf16[4,2,32,2048]{3,2,1,0:T(8,128)(2,1)}, bf16[4,2,32,2048]{3,2,1,0:T(8,128)(2,1)}, u32[]{:S(2)}, u32[]{:S(2)}) collective-permute-start(bf16[4,2,32,2048]{3,2,1,0:T(8,128)(2,1)} %get-tuple-element.11), channel_id=1, source_target_pairs={{0,2},{1,3},{2,0},{3,1},{4,6},{5,7},{6,4},{7,5},{8,10},{9,11},{10,... | collective-permute-start | bytes 3145736 | tf_op jit(solution)/shard_map/ppermute | solution.py:111
  75.1 22.0 %all-to-all-start = ((bf16[4,2,32,2048]{3,2,1,0:T(8,128)(2,1)}), bf16[4,2,32,2048]{3,2,1,0:T(8,128)(2,1)S(1)}, u32[]{:S(2)}, u32[]{:S(2)}) async-start(bf16[4,2,32,2048]{3,2,1,0:T(8,128)(2,1)} %fusion.15), calls=%async_computation | async-start | bytes 2097152 | tf_op jit(solution)/shard_map/all_to_all | solution.py:82
  95.1 2.0 %copy-start.2 = (bf16[2,4,2,32,2048]{4,3,2,1,0:T(8,128)(2,1)}, bf16[2,4,2,32,2048]{4,3,2,1,0:T(8,128)(2,1)S(1)}, u32[]{:S(2)}) copy-start(bf16[2,4,2,32,2048]{4,3,2,1,0:T(8,128)(2,1)S(1)} %pad_maximum_fusion) | copy-start | bytes 6291460
  97.1 20.1 %collective-permute-start.9 = (bf16[2,4,2,32,2048]{4,3,2,1,0:T(8,128)(2,1)}, bf16[2,4,2,32,2048]{4,3,2,1,0:T(8,128)(2,1)}, u32[]{:S(2)}, u32[]{:S(2)}) collective-permute-start(bf16[2,4,2,32,2048]{4,3,2,1,0:T(8,128)(2,1)} %reverse_select_fusion), channel_id=1, source_target_pairs={{0,1},{1,0},{2,3},{3,2},{4,5},{5,4},{6,7},{7,6},{8,9},{9,8},{10,11... | collective-permute-start | bytes 6291464 | tf_op jit(solution)/shard_map/ppermute | solution.py:114
  103.7 38.7 %all-to-all-start.1 = ((bf16[16,16,2048]{2,1,0:T(8,128)(2,1)}), bf16[16,16,2048]{2,1,0:T(8,128)(2,1)S(1)}, u32[]{:S(2)}, u32[]{:S(2)}) async-start(bf16[16,16,2048]{2,1,0:T(8,128)(2,1)} %bitcast.19), calls=%async_computation.1 | async-start | bytes 2097152 | tf_op jit(solution)/shard_map/all_to_all | solution.py:31
  114.2 2.5 %copy-start.3 = (bf16[2,4,2,32,2048]{4,3,2,1,0:T(8,128)(2,1)S(1)}, bf16[2,4,2,32,2048]{4,3,2,1,0:T(8,128)(2,1)}, u32[]{:S(2)}) copy-start(bf16[2,4,2,32,2048]{4,3,2,1,0:T(8,128)(2,1)} %copy-done.2) | copy-start | bytes 6291460
  142.5 5.4 %copy-start.9 = (bf16[1,2,128,512]{3,2,1,0:T(8,128)(2,1)S(1)}, bf16[1,2,128,512]{3,2,1,0:T(8,128)(2,1)}, u32[]{:S(2)}) copy-start(bf16[1,2,128,512]{3,2,1,0:T(8,128)(2,1)} %param.8) | copy-start | bytes 786436
  142.5 5.4 %copy-start.11 = (bf16[2,128,512]{2,1,0:T(8,128)(2,1)S(1)}, bf16[2,128,512]{2,1,0:T(8,128)(2,1)}, u32[]{:S(2)}) copy-start(bf16[2,128,512]{2,1,0:T(8,128)(2,1)} %copy-done.10) | copy-start | bytes 786436
  142.5 5.4 %copy-start.13 = (bf16[2,128,512]{2,1,0:T(8,128)(2,1)S(1)}, bf16[2,128,512]{2,1,0:T(8,128)(2,1)}, u32[]{:S(2)}) copy-start(bf16[2,128,512]{2,1,0:T(8,128)(2,1)} %copy-done.12) | copy-start | bytes 786436
  142.5 5.4 %copy-start.15 = (bf16[2,128,512]{2,1,0:T(8,128)(2,1)S(1)}, bf16[2,128,512]{2,1,0:T(8,128)(2,1)}, u32[]{:S(2)}) copy-start(bf16[2,128,512]{2,1,0:T(8,128)(2,1)} %copy-done.14) | copy-start | bytes 786436
  144.0 31.4 %all-to-all-start.2 = ((bf16[16,16,2048]{2,1,0:T(8,128)(2,1)}), bf16[16,16,2048]{2,1,0:T(8,128)(2,1)S(1)}, u32[]{:S(2)}, u32[]{:S(2)}) async-start(bf16[16,16,2048]{2,1,0:T(8,128)(2,1)} %reduce-window_convert_fusion), calls=%async_computation.2 | async-start | bytes 2097152 | tf_op jit(solution)/shard_map/all_to_all | solution.py:34
  175.7 5.0 %copy-start.1 = (bf16[1,2048,512]{2,1,0:T(8,128)(2,1)S(1)}, bf16[1,2048,512]{2,1,0:T(8,128)(2,1)}, u32[]{:S(2)}) copy-start(bf16[1,2048,512]{2,1,0:T(8,128)(2,1)} %param.9) | copy-start | bytes 6291460
  (6 other events, 7.6 us)

commit v8 on v7

--- a/solution.py
+++ b/solution.py
@@ -64,15 +64,16 @@
     kv_rev = jnp.concatenate([kv_sel[::-1], kv_sel[::-1]], axis=0)
     cotan_all = lax.dynamic_slice_in_dim(kv_rev, n_dp - 1 - my_p, n_dp, axis=0)
     cotan_all = cotan_all.transpose(1, 0, 2, 3).reshape(mb, n_dp * cotan.shape[1], width_t)
-    part = jnp.einsum(
-        "mjik,dk->jmid",
-        cotan_all.reshape(mb, n_dp * n_t, tok_dev, width_t),
-        weight,
-        preferred_element_type=jnp.float32,
-    ).astype(jnp.bfloat16)
-    part = part.reshape(n_dp, n_t // 2, 2, mb, tok_dev, rows_p)
-    keep = lax.dynamic_index_in_dim(part, my_core, 2, False)
-    send = lax.dynamic_index_in_dim(part, 1 - my_core, 2, False)
+    cot_blocks = cotan_all.reshape(mb, n_dp, n_t // 2, 2, tok_dev, width_t)
+
+    def part_for(core):
+        cot_c = lax.dynamic_index_in_dim(cot_blocks, core, 3, False)
+        return jnp.einsum(
+            "mpxik,dk->pxmid", cot_c, weight, preferred_element_type=jnp.float32
+        ).astype(jnp.bfloat16)
+
+    keep = part_for(my_core)
+    send = part_for(1 - my_core)
     recv = lax.ppermute(send, "tensor", [(q, q ^ 1) for q in range(n_t)])
     pair = (keep.astype(jnp.float32) + recv.astype(jnp.float32)).astype(jnp.bfloat16)
     keep = lax.dynamic_index_in_dim(pair, my_hi, 1, False)

time: 181 us -> 184 us (1.017)
  matrix products: 16.1 us -> 19.4 us
  other arithmetic: 36.1 us -> 33.6 us
    convert_element_type x2 -> x1, other arithmetic: 5.27 us -> 1.93 us  [body(): (keep.astype(jnp.float32) + recv.astype(jnp.float32)).astype(jnp.bfloat16)]
    dot_general x1 -> x2, matrix products: 2.39 us -> 5.71 us  [part_for(): jnp.einsum('mpxik,dk->pxmid', cot_c, weight, preferred_element_type=jnp.f...]
    dynamic_slice x2 -> x1, local copies, waits for them, and re-layouts: 3.45 us -> 0.89 us  [part_for(): cot_c = lax.dynamic_index_in_dim(cot_blocks, core, 3, False)]
    dynamic_slice x1, local copies, waits for them, and re-layouts: 3.15 us -> 5.6 us  [body(): pieces = [lax.dynamic_index_in_dim(nrm_blocks, my_p, 2, False)]]
    reshape x1, local copies, waits for them, and re-layouts: 0.8 us -> 2.65 us  [body(): nrm_blocks = own_normed.reshape(mb, tok_dev, n_dp, rows_p)]
    unnamed x38 -> x36, local copies, waits for them, and re-layouts: 5.28 us -> 3.92 us
  transfers between devices with their start and end apart: 13 -> 13, of which waited for: 8 -> 8; matrix products, arithmetic and copies ran while one was open for 33% -> 36% of each run, Pallas kernels for 0% -> 0%
where the time goes in v8:
time: 184 us; the launch traced here: 183 us
  waiting for transfers between devices  71.6 us (39%)
  other arithmetic  33.6 us (18%)
  starting transfers between devices  28.6 us (16%)
  local copies, waits for them, and re-layouts  27.4 us (15%)
  matrix products  19.4 us (11%)
  between operations  2.26 us (1%)
    all_to_all x1, waiting for transfers between devices, later_sum(): got = lax.all_to_all(chunks, 'section', 0, 0, tiled=True)  20.1 us
    ppermute x1, waiting for transfers between devices, body(): far = lax.ppermute(mine, 'tensor', [(q, q ^ 2) for q in range(n_t)])  14.7 us
    dot_general x1, matrix products, body(): jnp.einsum('tkmid,mktic->kdc', nrm, cot_sel, preferred_element_type=jnp.f...  13.7 us
    ppermute x1, waiting for transfers between devices, body(): recv = lax.ppermute(send, 'tensor', [(q, q ^ 2) for q in range(n_t)])  12.6 us
    all_to_all x1, waiting for transfers between devices, later_sum(): lax.all_to_all(suffix.astype(jnp.bfloat16), 'section', 0, 0, tiled=True)  10.5 us
    all_to_all x1, starting transfers between devices, later_sum(): got = lax.all_to_all(chunks, 'section', 0, 0, tiled=True)  9.2 us
    ppermute x3, waiting for transfers between devices, body(): lax.ppermute(cotan, 'dp', [(q, (q + k) % n_dp) for q in range(n_dp)])  8.08 us
    ppermute x3, starting transfers between devices, body(): lax.ppermute(cotan, 'dp', [(q, (q + k) % n_dp) for q in range(n_dp)])  5.9 us
  transfers between devices with their start and end apart: 13, of which 8 were waited for; matrix products, arithmetic and copies ran while one was open for 36% of the time, Pallas kernels for 0%

profile of v8, /device:TPU:4, one launch (start us, length us, event | category | flops | bytes accessed | tf_op | source)
XLA Modules:
  0.0 182.9 jit_solution(4237499734433818691)
XLA Ops:
  2.3 2.9 %collective-permute-start.1 = (bf16[2,128,512]{2,1,0:T(8,128)(2,1)}, bf16[2,128,512]{2,1,0:T(8,128)(2,1)S(1)}, u32[]{:S(2)}, u32[]{:S(2)}) collective-permute-start(bf16[2,128,512]{2,1,0:T(8,128)(2,1)} %bitcast.107), channel_id=1, source_target_pairs={{0,128},{64,192},{128,0},{192,64},{1,129},{65,193},{129,1},{193,65... | collective-permute-start | bytes 786440 | tf_op jit(solution)/shard_map/ppermute | solution.py:61
  10.3 6.8 %collective-permute-done.1 = bf16[2,128,512]{2,1,0:T(8,128)(2,1)S(1)} collective-permute-done((bf16[2,128,512]{2,1,0:T(8,128)(2,1)}, bf16[2,128,512]{2,1,0:T(8,128)(2,1)S(1)}, u32[]{:S(2)}, u32[]{:S(2)}) %collective-permute-start.1) | collective-permute-done | bytes 262176 | tf_op jit(solution)/shard_map/ppermute | solution.py:61
  22.5 2.7 %fusion.12 = bf16[4,2,2,32,2048]{4,3,1,0,2:T(8,128)(2,1)} fusion(bf16[1,2048,512]{2,1,0:T(8,128)(2,1)S(1)} %copy-done, bf16[2,4,2,1,32,512]{5,4,3,2,0,1:T(8,128)(2,1)S(1)} %get-tuple-element.15), kind=kOutput, calls=%fused_computation.22 | convolution fusion | flops 1074790400 | bytes 4718592 | tf_op jit(solution)/shard_map/mpxik,dk->pxmid/dot_general | solution.py:71
  26.5 2.6 %reshape.119 = bf16[2,32,4,2048]{3,2,1,0:T(4,128)(2,1)} reshape(bf16[2,32,8192]{2,1,0:T(8,128)(2,1)} %fusion.15) | data formatting | bytes 2097152 | tf_op jit(solution)/shard_map/reshape | solution.py:104
  29.1 5.6 %constant_dynamic-slice_fusion.3 = (bf16[2,32,1,2048]{3,2,1,0:T(2,128)(2,1)}, bf16[2,32,1,2048]{3,2,1,0:T(2,128)(2,1)S(1)}, bf16[2,32,1,2048]{3,2,1,0:T(2,128)(2,1)S(1)}, bf16[2,32,1,2048]{3,2,1,0:T(2,128)(2,1)S(1)}) fusion(bf16[2,32,4,2048]{3,2,1,0:T(4,128)(2,1)} %reshape.119, s32[]{:T(128)S(6)} %select_n.88, s32[]{:T(128)S(6)} %select_n.94, ...), kind=kLoop, calls=%fused_computation.68 | loop fusion | bytes 2097168 | tf_op jit(solution)/shard_map/jit(dynamic_index_in_dim)/dynamic_slice | solution.py:105
  37.6 2.4 %collective-permute-start.6 = (bf16[2,32,2048]{2,1,0:T(8,128)(2,1)}, bf16[2,32,2048]{2,1,0:T(8,128)(2,1)}, u32[]{:S(2)}, u32[]{:S(2)}) collective-permute-start(bf16[2,32,2048]{2,1,0:T(8,128)(2,1)} %bitcast.95), channel_id=1, source_target_pairs={{0,128},{64,192},{128,0},{192,64},{1,129},{65,193},{129,1},{193,65... | collective-permute-start | bytes 786440 | tf_op jit(solution)/shard_map/ppermute | solution.py:109
  42.4 3.1 %fusion.11 = bf16[4,2,2,32,2048]{4,3,1,0,2:T(8,128)(2,1)S(1)} fusion(bf16[4,2,2,32,2048]{4,3,1,0,2:T(8,128)(2,1)} %collective-permute-done.3, bf16[1,2048,512]{2,1,0:T(8,128)(2,1)S(1)} %copy-done, bf16[2,4,2,1,32,512]{5,4,3,2,0,1:T(8,128)(2,1)} %get-tuple-element.14), kind=kOutput, calls=%fused_computation.17 | convolution fusion | flops 1078984704 | bytes 6815744 | tf_op jit(solution)/shard_map/mpxik,dk->pxmid/dot_general | solution.py:71
  47.3 4.5 %collective-permute-done.6 = bf16[2,32,2048]{2,1,0:T(8,128)(2,1)} collective-permute-done((bf16[2,32,2048]{2,1,0:T(8,128)(2,1)}, bf16[2,32,2048]{2,1,0:T(8,128)(2,1)}, u32[]{:S(2)}, u32[]{:S(2)}) %collective-permute-start.6) | collective-permute-done | bytes 262176 | tf_op jit(solution)/shard_map/ppermute | solution.py:109
  52.9 2.5 %fusion.33 = (bf16[1,4,2,32,2048]{4,3,2,1,0:T(8,128)(2,1)}, bf16[4,2,32,2048]{3,2,1,0:T(8,128)(2,1)}) fusion(bf16[1,2,32,2048]{3,2,1,0:T(8,128)(2,1)} %bitcast.26, bf16[1,2,32,2048]{3,2,1,0:T(8,128)(2,1)} %bitcast.25, bf16[1,2,32,2048]{3,2,1,0:T(8,128)(2,1)S(1)} %bitcast.105, bf16[1,2,32,2048]{3,2,1,0:T(8,128)(2,1)S(1)} %bitcast.104), kind=kLoop, calls=%fused_computation.80 | loop fusion | flops 1572864 | bytes 3145728 | tf_op jit(solution)/shard_map/stack | solution.py:113
  57.8 3.7 %reshape.125 = f32[2,32,4,2048]{3,2,1,0:T(4,128)} reshape(bf16[2,32,8192]{2,1,0:T(8,128)(2,1)} %param.11) | data formatting | bytes 3145728 | tf_op jit(solution)/shard_map/convert_element_type | solution.py:95
  61.8 12.6 %collective-permute-done.4 = bf16[4,2,32,2048]{3,2,0,1:T(8,128)(2,1)} collective-permute-done((bf16[4,2,32,2048]{3,2,0,1:T(8,128)(2,1)}, bf16[4,2,32,2048]{3,2,0,1:T(8,128)(2,1)}, u32[]{:S(2)}, u32[]{:S(2)}) %collective-permute-start.4) | collective-permute-done | bytes 1048608 | tf_op jit(solution)/shard_map/ppermute | solution.py:81
  77.4 3.5 %all-to-all-start = ((bf16[4,2,32,2048]{3,2,1,0:T(8,128)(2,1)}), bf16[4,2,32,2048]{3,2,1,0:T(8,128)(2,1)S(1)}, u32[]{:S(2)}, u32[]{:S(2)}) async-start(bf16[4,2,32,2048]{3,2,1,0:T(8,128)(2,1)} %copy.37), calls=%async_computation | async-start | bytes 2097152 | tf_op jit(solution)/shard_map/all_to_all | solution.py:83
  80.9 14.7 %collective-permute-done.8 = bf16[4,2,32,2048]{3,2,1,0:T(8,128)(2,1)} collective-permute-done((bf16[4,2,32,2048]{3,2,1,0:T(8,128)(2,1)}, bf16[4,2,32,2048]{3,2,1,0:T(8,128)(2,1)}, u32[]{:S(2)}, u32[]{:S(2)}) %collective-permute-start.8) | collective-permute-done | bytes 1048608 | tf_op jit(solution)/shard_map/ppermute | solution.py:112
  100.9 3.4 %fusion.29 = (bf16[4,2,32,2048]{3,0,2,1:T(4,128)(2,1)S(1)}, f32[4,2,32,2048]{3,0,2,1:T(4,128)}) fusion(f32[2,32]{1,0:T(2,128)S(1)} %broadcast_multiply_fusion, f32[2,32,4,2048]{3,2,1,0:T(4,128)S(1)} %reshape.123, f32[2,32]{1,0:T(2,128)S(1)} %add_rsqrt_fusion.1, f32[4,2048]{1,0:T(4,128)S(1)} %reshape.122, bf16[4,2,32,2048]{3,2,1,0:T(8,128)(2,1)S(1)} %all-to-all-done, ...), kind=kLoop, calls=%fused_computation.62 | loop fusion | flops 4194304 | bytes 8421888 | tf_op jit(solution)/shard_map/convert_element_type | solution.py:30
  105.9 9.2 %all-to-all-start.1 = ((bf16[16,16,2048]{2,1,0:T(8,128)(2,1)}), bf16[16,16,2048]{2,1,0:T(8,128)(2,1)S(1)}, u32[]{:S(2)}, u32[]{:S(2)}) async-start(bf16[16,16,2048]{2,1,0:T(8,128)(2,1)} %bitcast.21), calls=%async_computation.1 | async-start | bytes 2097152 | tf_op jit(solution)/shard_map/all_to_all | solution.py:31
  116.5 2.5 %add_add_fusion = s32[2048,512]{1,0:T(8,128)} fusion(s32[]{:T(128)S(6)} %mul.161, s32[]{:T(128)} %bitcast.41, s32[]{:T(128)} %bitcast.40, s32[2048]{0:T(1024)S(1)} %multiply_add_fusion), kind=kLoop, calls=%fused_computation.18 | loop fusion | flops 5242880 | bytes 4202508 | tf_op jit(solution)/shard_map/add | solution.py:13
  119.4 2.8 %fusion.10 = bf16[2,2,4,2,32,2048]{5,4,3,2,0,1:T(8,128)(2,1)S(1)} fusion(bf16[1,2,4,2,32,2048]{5,4,3,2,1,0:T(8,128)(2,1)} %bitcast.30, bf16[1,2,4,2,32,2048]{5,4,3,2,1,0:T(8,128)(2,1)S(1)} %fusion.35, pred[]{:T(512)S(6)} %eq.13), kind=kLoop, calls=%fused_computation.15 | loop fusion | flops 6291456 | bytes 8388609 | tf_op jit(solution)/shard_map/transpose | solution.py:117
  122.2 2.3 %copy.41 = bf16[2,2,4,2,32,2048]{5,4,3,2,1,0:T(8,128)(2,1)} copy(bf16[2,2,4,2,32,2048]{5,4,3,2,0,1:T(8,128)(2,1)S(1)} %fusion.10) | data formatting | bytes 8388608 | tf_op jit(solution)/shard_map/transpose | solution.py:117
  124.5 20.1 %all-to-all-done.1 = bf16[16,16,2048]{2,1,0:T(8,128)(2,1)S(1)} async-done(((bf16[16,16,2048]{2,1,0:T(8,128)(2,1)}), bf16[16,16,2048]{2,1,0:T(8,128)(2,1)S(1)}, u32[]{:S(2)}, u32[]{:S(2)}) %all-to-all-start.1) | async-done | bytes 1048608 | tf_op jit(solution)/shard_map/all_to_all | solution.py:31
  146.2 3.9 %all-to-all-start.2 = ((bf16[16,16,2048]{2,1,0:T(8,128)(2,1)}), bf16[16,16,2048]{2,1,0:T(8,128)(2,1)S(1)}, u32[]{:S(2)}, u32[]{:S(2)}) async-start(bf16[16,16,2048]{2,1,0:T(8,128)(2,1)} %reduce-window_convert_fusion), calls=%async_computation.2 | async-start | bytes 2097152 | tf_op jit(solution)/shard_map/all_to_all | solution.py:34
  150.1 13.7 %fusion.9 = bf16[4,2048,512]{2,1,0:T(8,128)(2,1)S(1)} fusion(s32[4]{0:T(128)S(1)} %fusion.30, s32[2048,512]{1,0:T(8,128)} %add_add_fusion, bf16[4,4,2,32,2048]{4,3,2,1,0:T(8,128)(2,1)} %bitcast.102, bf16[1,2,4,32,512]{4,3,2,1,0:T(8,128)(2,1)S(1)} %bitcast.115, bf16[1,2,4,32,512]{4,3,2,1,0:T(8,128)(2,1)S(1)} %bitcast.113, ...), kind=kOutput, calls=%fused_computation.13 | convolution fusion | flops 2220359680 | bytes 17825808 | tf_op jit(solution)/shard_map/tkmid,mktic->kdc/dot_general | solution.py:127
  163.8 3.3 %convert_reduce_fusion = f32[2048,512]{1,0:T(8,128)} fusion(bf16[4,2048,512]{2,1,0:T(8,128)(2,1)S(1)} %fusion.9), kind=kLoop, calls=%fused_computation.12 | loop fusion | flops 7340032 | bytes 12582912 | tf_op jit(solution)/shard_map/reduce_sum | solution.py:129
  167.2 10.5 %all-to-all-done.2 = bf16[16,16,2048]{2,1,0:T(8,128)(2,1)S(1)} async-done(((bf16[16,16,2048]{2,1,0:T(8,128)(2,1)}), bf16[16,16,2048]{2,1,0:T(8,128)(2,1)S(1)}, u32[]{:S(2)}, u32[]{:S(2)}) %all-to-all-start.2) | async-done | bytes 1048608 | tf_op jit(solution)/shard_map/all_to_all | solution.py:34
  177.9 3.4 %fusion.24 = bf16[2,32,4,2048]{3,2,1,0:T(4,128)(2,1)S(1)} fusion(f32[4,2,32,2048]{3,0,2,1:T(4,128)} %get-tuple-element.7, f32[4,2,32,2048]{3,2,1,0:T(8,128)S(1)} %convert.8), kind=kLoop, calls=%fused_computation.47 | loop fusion | flops 1048576 | bytes 5242880 | tf_op jit(solution)/shard_map/transpose | solution.py:98
  (80 shorter events, 38.1 us)
Async XLA Ops:
  0.6 21.9 %copy-start = (bf16[1,2048,512]{2,1,0:T(8,128)(2,1)S(1)}, bf16[1,2048,512]{2,1,0:T(8,128)(2,1)}, u32[]{:S(2)}) copy-start(bf16[1,2048,512]{2,1,0:T(8,128)(2,1)} %param.9) | copy-start | bytes 6291460
  0.6 9.6 %collective-permute-start = (bf16[2,128,512]{2,1,0:T(8,128)(2,1)}, bf16[2,128,512]{2,1,0:T(8,128)(2,1)S(1)}, u32[]{:S(2)}, u32[]{:S(2)}) collective-permute-start(bf16[2,128,512]{2,1,0:T(8,128)(2,1)} %bitcast.106), channel_id=1, source_target_pairs={{0,64},{64,128},{128,192},{192,0},{1,65},{65,129},{129,193},{193,1... | collective-permute-start | bytes 786440 | tf_op jit(solution)/shard_map/ppermute | solution.py:61
  2.3 14.7 %collective-permute-start.1 = (bf16[2,128,512]{2,1,0:T(8,128)(2,1)}, bf16[2,128,512]{2,1,0:T(8,128)(2,1)S(1)}, u32[]{:S(2)}, u32[]{:S(2)}) collective-permute-start(bf16[2,128,512]{2,1,0:T(8,128)(2,1)} %bitcast.107), channel_id=1, source_target_pairs={{0,128},{64,192},{128,0},{192,64},{1,129},{65,193},{129,1},{193,65... | collective-permute-start | bytes 786440 | tf_op jit(solution)/shard_map/ppermute | solution.py:61
  5.2 11.9 %collective-permute-start.2 = (bf16[2,128,512]{2,1,0:T(8,128)(2,1)}, bf16[2,128,512]{2,1,0:T(8,128)(2,1)S(1)}, u32[]{:S(2)}, u32[]{:S(2)}) collective-permute-start(bf16[2,128,512]{2,1,0:T(8,128)(2,1)} %bitcast.108), channel_id=1, source_target_pairs={{0,192},{64,0},{128,64},{192,128},{1,193},{65,1},{129,65},{193,129... | collective-permute-start | bytes 786440 | tf_op jit(solution)/shard_map/ppermute | solution.py:61
  10.3 6.8 %copy-start.9 = (bf16[2,128,512]{2,1,0:T(8,128)(2,1)}, bf16[2,128,512]{2,1,0:T(8,128)(2,1)S(1)}, u32[]{:S(2)}) copy-start(bf16[2,128,512]{2,1,0:T(8,128)(2,1)S(1)} %collective-permute-done) | copy-start | bytes 786436
  22.5 2.7 %copy-start.4 = (bf16[1,2,32,8192]{3,2,1,0:T(8,128)(2,1)S(1)}, bf16[1,2,32,8192]{3,2,1,0:T(8,128)(2,1)}, u32[]{:S(2)}) copy-start(bf16[1,2,32,8192]{3,2,1,0:T(8,128)(2,1)} %param.7) | copy-start | bytes 3145732
  25.2 17.2 %collective-permute-start.3 = (bf16[4,2,2,32,2048]{4,3,1,0,2:T(8,128)(2,1)}, bf16[4,2,2,32,2048]{4,3,1,0,2:T(8,128)(2,1)}, u32[]{:S(2)}, u32[]{:S(2)}) collective-permute-start(bf16[4,2,2,32,2048]{4,3,1,0,2:T(8,128)(2,1)} %fusion.12), channel_id=1, source_target_pairs={{0,1},{1,0},{2,3},{3,2},{4,5},{5,4},{6,7},{7,6},{8,9},{9,8},{10,11... | collective-permute-start | bytes 6291464 | tf_op jit(solution)/shard_map/ppermute | solution.py:77
  35.6 11.7 %collective-permute-start.5 = (bf16[2,32,2048]{2,1,0:T(8,128)(2,1)}, bf16[2,32,2048]{2,1,0:T(8,128)(2,1)S(1)}, u32[]{:S(2)}, u32[]{:S(2)}) collective-permute-start(bf16[2,32,2048]{2,1,0:T(8,128)(2,1)} %bitcast.96), channel_id=1, source_target_pairs={{0,64},{64,128},{128,192},{192,0},{1,65},{65,129},{129,193},{193,1... | collective-permute-start | bytes 786440 | tf_op jit(solution)/shard_map/ppermute | solution.py:109
  37.6 14.2 %collective-permute-start.6 = (bf16[2,32,2048]{2,1,0:T(8,128)(2,1)}, bf16[2,32,2048]{2,1,0:T(8,128)(2,1)}, u32[]{:S(2)}, u32[]{:S(2)}) collective-permute-start(bf16[2,32,2048]{2,1,0:T(8,128)(2,1)} %bitcast.95), channel_id=1, source_target_pairs={{0,128},{64,192},{128,0},{192,64},{1,129},{65,193},{129,1},{193,65... | collective-permute-start | bytes 786440 | tf_op jit(solution)/shard_map/ppermute | solution.py:109
  40.8 12.1 %collective-permute-start.7 = (bf16[2,32,2048]{2,1,0:T(8,128)(2,1)}, bf16[2,32,2048]{2,1,0:T(8,128)(2,1)}, u32[]{:S(2)}, u32[]{:S(2)}) collective-permute-start(bf16[2,32,2048]{2,1,0:T(8,128)(2,1)} %bitcast.94), channel_id=1, source_target_pairs={{0,192},{64,0},{128,64},{192,128},{1,193},{65,1},{129,65},{193,129... | collective-permute-start | bytes 786440 | tf_op jit(solution)/shard_map/ppermute | solution.py:109
  45.5 10.0 %copy-start.6 = (bf16[4,2,2,32,2048]{4,3,1,0,2:T(8,128)(2,1)}, bf16[4,2,2,32,2048]{4,3,1,0,2:T(8,128)(2,1)S(1)}, u32[]{:S(2)}) copy-start(bf16[4,2,2,32,2048]{4,3,1,0,2:T(8,128)(2,1)S(1)} %fusion.11) | copy-start | bytes 6291460
  46.6 27.9 %collective-permute-start.4 = (bf16[4,2,32,2048]{3,2,0,1:T(8,128)(2,1)}, bf16[4,2,32,2048]{3,2,0,1:T(8,128)(2,1)}, u32[]{:S(2)}, u32[]{:S(2)}) collective-permute-start(bf16[4,2,32,2048]{3,2,0,1:T(8,128)(2,1)} %dynamic-slice_bitcast_fusion), channel_id=1, source_target_pairs={{0,2},{1,3},{2,0},{3,1},{4,6},{5,7},{6,4},{7,5},{8,10},{9,11},{10,... | collective-permute-start | bytes 3145736 | tf_op jit(solution)/shard_map/ppermute | solution.py:81
  55.5 2.2 %copy-start.15 = (bf16[1,8192]{1,0:T(2,128)(2,1)S(1)}, bf16[1,8192]{1,0:T(2,128)(2,1)}, u32[]{:S(2)}) copy-start(bf16[1,8192]{1,0:T(2,128)(2,1)} %param.10) | copy-start | bytes 49156
  55.5 40.1 %collective-permute-start.8 = (bf16[4,2,32,2048]{3,2,1,0:T(8,128)(2,1)}, bf16[4,2,32,2048]{3,2,1,0:T(8,128)(2,1)}, u32[]{:S(2)}, u32[]{:S(2)}) collective-permute-start(bf16[4,2,32,2048]{3,2,1,0:T(8,128)(2,1)} %get-tuple-element.9), channel_id=1, source_target_pairs={{0,2},{1,3},{2,0},{3,1},{4,6},{5,7},{6,4},{7,5},{8,10},{9,11},{10,... | collective-permute-start | bytes 3145736 | tf_op jit(solution)/shard_map/ppermute | solution.py:112
  77.4 21.9 %all-to-all-start = ((bf16[4,2,32,2048]{3,2,1,0:T(8,128)(2,1)}), bf16[4,2,32,2048]{3,2,1,0:T(8,128)(2,1)S(1)}, u32[]{:S(2)}, u32[]{:S(2)}) async-start(bf16[4,2,32,2048]{3,2,1,0:T(8,128)(2,1)} %copy.37), calls=%async_computation | async-start | bytes 2097152 | tf_op jit(solution)/shard_map/all_to_all | solution.py:83
  99.3 20.1 %collective-permute-start.9 = (bf16[2,4,2,32,2048]{4,3,2,1,0:T(8,128)(2,1)}, bf16[2,4,2,32,2048]{4,3,2,1,0:T(8,128)(2,1)}, u32[]{:S(2)}, u32[]{:S(2)}) collective-permute-start(bf16[2,4,2,32,2048]{4,3,2,1,0:T(8,128)(2,1)} %reverse_select_fusion), channel_id=1, source_target_pairs={{0,1},{1,0},{2,3},{3,2},{4,5},{5,4},{6,7},{7,6},{8,9},{9,8},{10,11... | collective-permute-start | bytes 6291464 | tf_op jit(solution)/shard_map/ppermute | solution.py:115
  105.9 38.7 %all-to-all-start.1 = ((bf16[16,16,2048]{2,1,0:T(8,128)(2,1)}), bf16[16,16,2048]{2,1,0:T(8,128)(2,1)S(1)}, u32[]{:S(2)}, u32[]{:S(2)}) async-start(bf16[16,16,2048]{2,1,0:T(8,128)(2,1)} %bitcast.21), calls=%async_computation.1 | async-start | bytes 2097152 | tf_op jit(solution)/shard_map/all_to_all | solution.py:31
  116.5 2.5 %copy-start.3 = (bf16[2,4,2,32,2048]{4,3,2,1,0:T(8,128)(2,1)S(1)}, bf16[2,4,2,32,2048]{4,3,2,1,0:T(8,128)(2,1)}, u32[]{:S(2)}) copy-start(bf16[2,4,2,32,2048]{4,3,2,1,0:T(8,128)(2,1)} %copy-done.2) | copy-start | bytes 6291460
  144.6 5.4 %copy-start.8 = (bf16[1,2,128,512]{3,2,1,0:T(8,128)(2,1)S(1)}, bf16[1,2,128,512]{3,2,1,0:T(8,128)(2,1)}, u32[]{:S(2)}) copy-start(bf16[1,2,128,512]{3,2,1,0:T(8,128)(2,1)} %param.8) | copy-start | bytes 786436
  144.7 5.4 %copy-start.10 = (bf16[2,128,512]{2,1,0:T(8,128)(2,1)S(1)}, bf16[2,128,512]{2,1,0:T(8,128)(2,1)}, u32[]{:S(2)}) copy-start(bf16[2,128,512]{2,1,0:T(8,128)(2,1)} %copy-done.9) | copy-start | bytes 786436
  144.7 5.4 %copy-start.12 = (bf16[2,128,512]{2,1,0:T(8,128)(2,1)S(1)}, bf16[2,128,512]{2,1,0:T(8,128)(2,1)}, u32[]{:S(2)}) copy-start(bf16[2,128,512]{2,1,0:T(8,128)(2,1)} %copy-done.11) | copy-start | bytes 786436
  144.7 5.4 %copy-start.14 = (bf16[2,128,512]{2,1,0:T(8,128)(2,1)S(1)}, bf16[2,128,512]{2,1,0:T(8,128)(2,1)}, u32[]{:S(2)}) copy-start(bf16[2,128,512]{2,1,0:T(8,128)(2,1)} %copy-done.13) | copy-start | bytes 786436
  146.2 31.4 %all-to-all-start.2 = ((bf16[16,16,2048]{2,1,0:T(8,128)(2,1)}), bf16[16,16,2048]{2,1,0:T(8,128)(2,1)S(1)}, u32[]{:S(2)}, u32[]{:S(2)}) async-start(bf16[16,16,2048]{2,1,0:T(8,128)(2,1)} %reduce-window_convert_fusion), calls=%async_computation.2 | async-start | bytes 2097152 | tf_op jit(solution)/shard_map/all_to_all | solution.py:34
  177.9 5.0 %copy-start.1 = (bf16[1,2048,512]{2,1,0:T(8,128)(2,1)S(1)}, bf16[1,2048,512]{2,1,0:T(8,128)(2,1)}, u32[]{:S(2)}) copy-start(bf16[1,2048,512]{2,1,0:T(8,128)(2,1)} %param.9) | copy-start | bytes 6291460
  (5 other events, 6.7 us)

commit v9 on v8

--- a/solution.py
+++ b/solution.py
@@ -61,9 +61,13 @@
             lax.ppermute(cotan, "dp", [(q, (q + k) % n_dp) for q in range(n_dp)])
         )
     kv_sel = jnp.stack(kv_pieces)
-    kv_rev = jnp.concatenate([kv_sel[::-1], kv_sel[::-1]], axis=0)
-    cotan_all = lax.dynamic_slice_in_dim(kv_rev, n_dp - 1 - my_p, n_dp, axis=0)
-    cotan_all = cotan_all.transpose(1, 0, 2, 3).reshape(mb, n_dp * cotan.shape[1], width_t)
+    blocks = []
+    for j in range(n_dp):
+        pick = kv_pieces[0]
+        for k in range(1, n_dp):
+            pick = jnp.where((my_p - k) % n_dp == j, kv_pieces[k], pick)
+        blocks.append(pick)
+    cotan_all = jnp.concatenate(blocks, axis=1)
     cot_blocks = cotan_all.reshape(mb, n_dp, n_t // 2, 2, tok_dev, width_t)
 
     def part_for(core):

time: 184 us -> 180 us (0.978)
  local copies, waits for them, and re-layouts: 27.4 us -> 24.4 us
    another operation x1 -> x0, other arithmetic: 2.05 us -> none  [body(): kv_sel = jnp.stack(kv_pieces)]
    unnamed x36 -> x34, local copies, waits for them, and re-layouts: 3.92 us -> 3.12 us
where the time goes in v9:
time: 180 us; the launch traced here: 179 us
  waiting for transfers between devices  71.4 us (40%)
  other arithmetic  32.7 us (18%)
  starting transfers between devices  28.6 us (16%)
  local copies, waits for them, and re-layouts  24.4 us (14%)
  matrix products  19.4 us (11%)
  between operations  2.33 us (1%)
    all_to_all x1, waiting for transfers between devices, later_sum(): got = lax.all_to_all(chunks, 'section', 0, 0, tiled=True)  20.1 us
    ppermute x1, waiting for transfers between devices, body(): far = lax.ppermute(mine, 'tensor', [(q, q ^ 2) for q in range(n_t)])  14.7 us
    dot_general x1, matrix products, body(): jnp.einsum('tkmid,mktic->kdc', nrm, cot_sel, preferred_element_type=jnp.f...  13.7 us
    ppermute x1, waiting for transfers between devices, body(): recv = lax.ppermute(send, 'tensor', [(q, q ^ 2) for q in range(n_t)])  12.5 us
    all_to_all x1, waiting for transfers between devices, later_sum(): lax.all_to_all(suffix.astype(jnp.bfloat16), 'section', 0, 0, tiled=True)  10.5 us
    all_to_all x1, starting transfers between devices, later_sum(): got = lax.all_to_all(chunks, 'section', 0, 0, tiled=True)  9.2 us
    ppermute x3, waiting for transfers between devices, body(): lax.ppermute(cotan, 'dp', [(q, (q + k) % n_dp) for q in range(n_dp)])  8.03 us
    ppermute x3, starting transfers between devices, body(): lax.ppermute(cotan, 'dp', [(q, (q + k) % n_dp) for q in range(n_dp)])  5.9 us
  transfers between devices with their start and end apart: 13, of which 8 were waited for; matrix products, arithmetic and copies ran while one was open for 36% of the time, Pallas kernels for 0%

profile of v9, /device:TPU:4, one launch (start us, length us, event | category | flops | bytes accessed | tf_op | source)
XLA Modules:
  0.0 178.9 jit_solution(16206225668035943521)
XLA Ops:
  2.3 2.9 %collective-permute-start.1 = (bf16[2,128,512]{2,1,0:T(8,128)(2,1)}, bf16[2,128,512]{2,1,0:T(8,128)(2,1)S(1)}, u32[]{:S(2)}, u32[]{:S(2)}) collective-permute-start(bf16[2,128,512]{2,1,0:T(8,128)(2,1)} %bitcast.110), channel_id=1, source_target_pairs={{0,128},{64,192},{128,0},{192,64},{1,129},{65,193},{129,1},{193,65... | collective-permute-start | bytes 786440 | tf_op jit(solution)/shard_map/ppermute | solution.py:61
  10.3 6.8 %collective-permute-done.1 = bf16[2,128,512]{2,1,0:T(8,128)(2,1)S(1)} collective-permute-done((bf16[2,128,512]{2,1,0:T(8,128)(2,1)}, bf16[2,128,512]{2,1,0:T(8,128)(2,1)S(1)}, u32[]{:S(2)}, u32[]{:S(2)}) %collective-permute-start.1) | collective-permute-done | bytes 262176 | tf_op jit(solution)/shard_map/ppermute | solution.py:61
  18.5 2.7 %fusion.12 = bf16[4,2,2,32,2048]{4,3,1,0,2:T(8,128)(2,1)} fusion(bf16[1,2048,512]{2,1,0:T(8,128)(2,1)S(1)} %copy-done, bf16[2,4,2,2,32,512]{5,4,3,2,1,0:T(8,128)(2,1)S(1)} %bitcast.107, s32[]{:T(128)S(6)} %select_n.209), kind=kOutput, calls=%fused_computation.22 | convolution fusion | flops 1074790400 | bytes 4718596 | tf_op jit(solution)/shard_map/mpxik,dk->pxmid/dot_general | solution.py:75
  22.4 2.6 %reshape.123 = bf16[2,32,4,2048]{3,2,1,0:T(4,128)(2,1)} reshape(bf16[2,32,8192]{2,1,0:T(8,128)(2,1)} %fusion.15) | data formatting | bytes 2097152 | tf_op jit(solution)/shard_map/reshape | solution.py:108
  25.1 5.6 %constant_dynamic-slice_fusion.3 = (bf16[2,32,1,2048]{3,2,1,0:T(2,128)(2,1)}, bf16[2,32,1,2048]{3,2,1,0:T(2,128)(2,1)S(1)}, bf16[2,32,1,2048]{3,2,1,0:T(2,128)(2,1)S(1)}, bf16[2,32,1,2048]{3,2,1,0:T(2,128)(2,1)S(1)}) fusion(bf16[2,32,4,2048]{3,2,1,0:T(4,128)(2,1)} %reshape.123, s32[]{:T(128)S(6)} %select_n.215, s32[]{:T(128)S(6)} %select_n.221, ...), kind=kLoop, calls=%fused_computation.73 | loop fusion | bytes 2097168 | tf_op jit(solution)/shard_map/jit(dynamic_index_in_dim)/dynamic_slice | solution.py:109
  33.6 2.4 %collective-permute-start.6 = (bf16[2,32,2048]{2,1,0:T(8,128)(2,1)}, bf16[2,32,2048]{2,1,0:T(8,128)(2,1)}, u32[]{:S(2)}, u32[]{:S(2)}) collective-permute-start(bf16[2,32,2048]{2,1,0:T(8,128)(2,1)} %bitcast.98), channel_id=1, source_target_pairs={{0,128},{64,192},{128,0},{192,64},{1,129},{65,193},{129,1},{193,65... | collective-permute-start | bytes 786440 | tf_op jit(solution)/shard_map/ppermute | solution.py:113
  38.4 3.1 %fusion.11 = bf16[4,2,2,32,2048]{4,3,1,0,2:T(8,128)(2,1)S(1)} fusion(bf16[4,2,2,32,2048]{4,3,1,0,2:T(8,128)(2,1)} %collective-permute-done.3, bf16[1,2048,512]{2,1,0:T(8,128)(2,1)S(1)} %copy-done, bf16[2,4,2,2,32,512]{5,4,3,2,1,0:T(8,128)(2,1)} %bitcast.108, s32[]{:T(128)S(6)} %select_n.208), kind=kOutput, calls=%fused_computation.17 | convolution fusion | flops 1078984704 | bytes 6815748 | tf_op jit(solution)/shard_map/mpxik,dk->pxmid/dot_general | solution.py:75
  43.2 4.5 %collective-permute-done.6 = bf16[2,32,2048]{2,1,0:T(8,128)(2,1)} collective-permute-done((bf16[2,32,2048]{2,1,0:T(8,128)(2,1)}, bf16[2,32,2048]{2,1,0:T(8,128)(2,1)}, u32[]{:S(2)}, u32[]{:S(2)}) %collective-permute-start.6) | collective-permute-done | bytes 262176 | tf_op jit(solution)/shard_map/ppermute | solution.py:113
  48.9 2.6 %fusion.38 = (bf16[1,4,2,32,2048]{4,3,2,1,0:T(8,128)(2,1)}, bf16[4,2,32,2048]{3,2,1,0:T(8,128)(2,1)}) fusion(bf16[1,2,32,2048]{3,2,1,0:T(8,128)(2,1)} %bitcast.21, bf16[1,2,32,2048]{3,2,1,0:T(8,128)(2,1)} %bitcast.20, bf16[1,2,32,2048]{3,2,1,0:T(8,128)(2,1)} %bitcast.19, bf16[1,2,32,2048]{3,2,1,0:T(8,128)(2,1)S(1)} %bitcast.106), kind=kLoop, calls=%fused_computation.83 | loop fusion | flops 1572864 | bytes 3145728 | tf_op jit(solution)/shard_map/stack | solution.py:117
  53.8 3.7 %reshape.129 = f32[2,32,4,2048]{3,2,1,0:T(4,128)} reshape(bf16[2,32,8192]{2,1,0:T(8,128)(2,1)} %param.11) | data formatting | bytes 3145728 | tf_op jit(solution)/shard_map/convert_element_type | solution.py:99
  57.9 12.5 %collective-permute-done.4 = bf16[4,2,32,2048]{3,2,0,1:T(8,128)(2,1)} collective-permute-done((bf16[4,2,32,2048]{3,2,0,1:T(8,128)(2,1)}, bf16[4,2,32,2048]{3,2,0,1:T(8,128)(2,1)}, u32[]{:S(2)}, u32[]{:S(2)}) %collective-permute-start.4) | collective-permute-done | bytes 1048608 | tf_op jit(solution)/shard_map/ppermute | solution.py:85
  73.4 3.5 %all-to-all-start = ((bf16[4,2,32,2048]{3,2,1,0:T(8,128)(2,1)}), bf16[4,2,32,2048]{3,2,1,0:T(8,128)(2,1)S(1)}, u32[]{:S(2)}, u32[]{:S(2)}) async-start(bf16[4,2,32,2048]{3,2,1,0:T(8,128)(2,1)} %copy.37), calls=%async_computation | async-start | bytes 2097152 | tf_op jit(solution)/shard_map/all_to_all | solution.py:87
  76.9 14.7 %collective-permute-done.8 = bf16[4,2,32,2048]{3,2,1,0:T(8,128)(2,1)} collective-permute-done((bf16[4,2,32,2048]{3,2,1,0:T(8,128)(2,1)}, bf16[4,2,32,2048]{3,2,1,0:T(8,128)(2,1)}, u32[]{:S(2)}, u32[]{:S(2)}) %collective-permute-start.8) | collective-permute-done | bytes 1048608 | tf_op jit(solution)/shard_map/ppermute | solution.py:116
  96.9 3.4 %fusion.32 = (bf16[4,2,32,2048]{3,0,2,1:T(4,128)(2,1)S(1)}, f32[4,2,32,2048]{3,0,2,1:T(4,128)}) fusion(f32[2,32]{1,0:T(2,128)S(1)} %broadcast_multiply_fusion, f32[2,32,4,2048]{3,2,1,0:T(4,128)S(1)} %reshape.127, f32[2,32]{1,0:T(2,128)S(1)} %add_rsqrt_fusion.1, f32[4,2048]{1,0:T(4,128)S(1)} %reshape.126, bf16[4,2,32,2048]{3,2,1,0:T(8,128)(2,1)S(1)} %all-to-all-done, ...), kind=kLoop, calls=%fused_computation.65 | loop fusion | flops 4194304 | bytes 8421888 | tf_op jit(solution)/shard_map/convert_element_type | solution.py:30
  101.9 9.2 %all-to-all-start.1 = ((bf16[16,16,2048]{2,1,0:T(8,128)(2,1)}), bf16[16,16,2048]{2,1,0:T(8,128)(2,1)S(1)}, u32[]{:S(2)}, u32[]{:S(2)}) async-start(bf16[16,16,2048]{2,1,0:T(8,128)(2,1)} %bitcast.16), calls=%async_computation.1 | async-start | bytes 2097152 | tf_op jit(solution)/shard_map/all_to_all | solution.py:31
  112.4 2.5 %add_add_fusion = s32[2048,512]{1,0:T(8,128)} fusion(s32[]{:T(128)S(6)} %mul.161, s32[]{:T(128)} %bitcast.36, s32[]{:T(128)} %bitcast.35, s32[2048]{0:T(1024)S(1)} %multiply_add_fusion), kind=kLoop, calls=%fused_computation.18 | loop fusion | flops 5242880 | bytes 4202508 | tf_op jit(solution)/shard_map/add | solution.py:13
  115.4 2.8 %fusion.10 = bf16[2,2,4,2,32,2048]{5,4,3,2,0,1:T(8,128)(2,1)S(1)} fusion(bf16[1,2,4,2,32,2048]{5,4,3,2,1,0:T(8,128)(2,1)} %bitcast.25, bf16[1,2,4,2,32,2048]{5,4,3,2,1,0:T(8,128)(2,1)S(1)} %fusion.40, pred[]{:T(512)S(6)} %eq.73), kind=kLoop, calls=%fused_computation.15 | loop fusion | flops 6291456 | bytes 8388609 | tf_op jit(solution)/shard_map/transpose | solution.py:121
  118.2 2.3 %copy.41 = bf16[2,2,4,2,32,2048]{5,4,3,2,1,0:T(8,128)(2,1)} copy(bf16[2,2,4,2,32,2048]{5,4,3,2,0,1:T(8,128)(2,1)S(1)} %fusion.10) | data formatting | bytes 8388608 | tf_op jit(solution)/shard_map/transpose | solution.py:121
  120.5 20.1 %all-to-all-done.1 = bf16[16,16,2048]{2,1,0:T(8,128)(2,1)S(1)} async-done(((bf16[16,16,2048]{2,1,0:T(8,128)(2,1)}), bf16[16,16,2048]{2,1,0:T(8,128)(2,1)S(1)}, u32[]{:S(2)}, u32[]{:S(2)}) %all-to-all-start.1) | async-done | bytes 1048608 | tf_op jit(solution)/shard_map/all_to_all | solution.py:31
  142.2 3.9 %all-to-all-start.2 = ((bf16[16,16,2048]{2,1,0:T(8,128)(2,1)}), bf16[16,16,2048]{2,1,0:T(8,128)(2,1)S(1)}, u32[]{:S(2)}, u32[]{:S(2)}) async-start(bf16[16,16,2048]{2,1,0:T(8,128)(2,1)} %reduce-window_convert_fusion), calls=%async_computation.2 | async-start | bytes 2097152 | tf_op jit(solution)/shard_map/all_to_all | solution.py:34
  146.1 13.7 %fusion.9 = bf16[4,2048,512]{2,1,0:T(8,128)(2,1)S(1)} fusion(s32[4]{0:T(128)S(1)} %fusion.35, s32[2048,512]{1,0:T(8,128)} %add_add_fusion, bf16[4,4,2,32,2048]{4,3,2,1,0:T(8,128)(2,1)} %bitcast.105, bf16[1,2,4,32,512]{4,3,2,1,0:T(8,128)(2,1)S(1)} %bitcast.115, bf16[1,2,4,32,512]{4,3,2,1,0:T(8,128)(2,1)S(1)} %bitcast.114, ...), kind=kOutput, calls=%fused_computation.13 | convolution fusion | flops 2220359680 | bytes 17825808 | tf_op jit(solution)/shard_map/tkmid,mktic->kdc/dot_general | solution.py:131
  159.8 3.3 %convert_reduce_fusion = f32[2048,512]{1,0:T(8,128)} fusion(bf16[4,2048,512]{2,1,0:T(8,128)(2,1)S(1)} %fusion.9), kind=kLoop, calls=%fused_computation.12 | loop fusion | flops 7340032 | bytes 12582912 | tf_op jit(solution)/shard_map/reduce_sum | solution.py:133
  163.1 10.5 %all-to-all-done.2 = bf16[16,16,2048]{2,1,0:T(8,128)(2,1)S(1)} async-done(((bf16[16,16,2048]{2,1,0:T(8,128)(2,1)}), bf16[16,16,2048]{2,1,0:T(8,128)(2,1)S(1)}, u32[]{:S(2)}, u32[]{:S(2)}) %all-to-all-start.2) | async-done | bytes 1048608 | tf_op jit(solution)/shard_map/all_to_all | solution.py:34
  173.9 3.4 %fusion.24 = bf16[2,32,4,2048]{3,2,1,0:T(4,128)(2,1)S(1)} fusion(f32[4,2,32,2048]{3,0,2,1:T(4,128)} %get-tuple-element.7, f32[4,2,32,2048]{3,2,1,0:T(8,128)S(1)} %convert.8), kind=kLoop, calls=%fused_computation.45 | loop fusion | flops 1048576 | bytes 5242880 | tf_op jit(solution)/shard_map/transpose | solution.py:102
  (76 shorter events, 33.9 us)
Async XLA Ops:
  0.6 17.8 %copy-start = (bf16[1,2048,512]{2,1,0:T(8,128)(2,1)S(1)}, bf16[1,2048,512]{2,1,0:T(8,128)(2,1)}, u32[]{:S(2)}) copy-start(bf16[1,2048,512]{2,1,0:T(8,128)(2,1)} %param.9) | copy-start | bytes 6291460
  0.6 9.6 %collective-permute-start.2 = (bf16[2,128,512]{2,1,0:T(8,128)(2,1)}, bf16[2,128,512]{2,1,0:T(8,128)(2,1)S(1)}, u32[]{:S(2)}, u32[]{:S(2)}) collective-permute-start(bf16[2,128,512]{2,1,0:T(8,128)(2,1)} %bitcast.109), channel_id=1, source_target_pairs={{0,64},{64,128},{128,192},{192,0},{1,65},{65,129},{129,193},{193,1... | collective-permute-start | bytes 786440 | tf_op jit(solution)/shard_map/ppermute | solution.py:61
  2.3 14.7 %collective-permute-start.1 = (bf16[2,128,512]{2,1,0:T(8,128)(2,1)}, bf16[2,128,512]{2,1,0:T(8,128)(2,1)S(1)}, u32[]{:S(2)}, u32[]{:S(2)}) collective-permute-start(bf16[2,128,512]{2,1,0:T(8,128)(2,1)} %bitcast.110), channel_id=1, source_target_pairs={{0,128},{64,192},{128,0},{192,64},{1,129},{65,193},{129,1},{193,65... | collective-permute-start | bytes 786440 | tf_op jit(solution)/shard_map/ppermute | solution.py:61
  5.2 11.9 %collective-permute-start = (bf16[2,128,512]{2,1,0:T(8,128)(2,1)}, bf16[2,128,512]{2,1,0:T(8,128)(2,1)S(1)}, u32[]{:S(2)}, u32[]{:S(2)}) collective-permute-start(bf16[2,128,512]{2,1,0:T(8,128)(2,1)} %bitcast.111), channel_id=1, source_target_pairs={{0,192},{64,0},{128,64},{192,128},{1,193},{65,1},{129,65},{193,129... | collective-permute-start | bytes 786440 | tf_op jit(solution)/shard_map/ppermute | solution.py:61
  18.4 2.7 %copy-start.8 = (bf16[2,512,512]{2,1,0:T(8,128)(2,1)}, bf16[2,512,512]{2,1,0:T(8,128)(2,1)S(1)}, u32[]{:S(2)}) copy-start(bf16[2,512,512]{2,1,0:T(8,128)(2,1)S(1)} %pad_maximum_fusion.1) | copy-start | bytes 3145732
  18.4 2.7 %copy-start.4 = (bf16[1,2,32,8192]{3,2,1,0:T(8,128)(2,1)S(1)}, bf16[1,2,32,8192]{3,2,1,0:T(8,128)(2,1)}, u32[]{:S(2)}) copy-start(bf16[1,2,32,8192]{3,2,1,0:T(8,128)(2,1)} %param.7) | copy-start | bytes 3145732
  21.1 17.3 %collective-permute-start.3 = (bf16[4,2,2,32,2048]{4,3,1,0,2:T(8,128)(2,1)}, bf16[4,2,2,32,2048]{4,3,1,0,2:T(8,128)(2,1)}, u32[]{:S(2)}, u32[]{:S(2)}) collective-permute-start(bf16[4,2,2,32,2048]{4,3,1,0,2:T(8,128)(2,1)} %fusion.12), channel_id=1, source_target_pairs={{0,1},{1,0},{2,3},{3,2},{4,5},{5,4},{6,7},{7,6},{8,9},{9,8},{10,11... | collective-permute-start | bytes 6291464 | tf_op jit(solution)/shard_map/ppermute | solution.py:81
  31.6 11.7 %collective-permute-start.5 = (bf16[2,32,2048]{2,1,0:T(8,128)(2,1)}, bf16[2,32,2048]{2,1,0:T(8,128)(2,1)}, u32[]{:S(2)}, u32[]{:S(2)}) collective-permute-start(bf16[2,32,2048]{2,1,0:T(8,128)(2,1)} %bitcast.99), channel_id=1, source_target_pairs={{0,64},{64,128},{128,192},{192,0},{1,65},{65,129},{129,193},{193,1... | collective-permute-start | bytes 786440 | tf_op jit(solution)/shard_map/ppermute | solution.py:113
  33.6 14.2 %collective-permute-start.6 = (bf16[2,32,2048]{2,1,0:T(8,128)(2,1)}, bf16[2,32,2048]{2,1,0:T(8,128)(2,1)}, u32[]{:S(2)}, u32[]{:S(2)}) collective-permute-start(bf16[2,32,2048]{2,1,0:T(8,128)(2,1)} %bitcast.98), channel_id=1, source_target_pairs={{0,128},{64,192},{128,0},{192,64},{1,129},{65,193},{129,1},{193,65... | collective-permute-start | bytes 786440 | tf_op jit(solution)/shard_map/ppermute | solution.py:113
  36.8 12.1 %collective-permute-start.7 = (bf16[2,32,2048]{2,1,0:T(8,128)(2,1)}, bf16[2,32,2048]{2,1,0:T(8,128)(2,1)}, u32[]{:S(2)}, u32[]{:S(2)}) collective-permute-start(bf16[2,32,2048]{2,1,0:T(8,128)(2,1)} %bitcast.97), channel_id=1, source_target_pairs={{0,192},{64,0},{128,64},{192,128},{1,193},{65,1},{129,65},{193,129... | collective-permute-start | bytes 786440 | tf_op jit(solution)/shard_map/ppermute | solution.py:113
  41.5 10.1 %copy-start.6 = (bf16[4,2,2,32,2048]{4,3,1,0,2:T(8,128)(2,1)}, bf16[4,2,2,32,2048]{4,3,1,0,2:T(8,128)(2,1)S(1)}, u32[]{:S(2)}) copy-start(bf16[4,2,2,32,2048]{4,3,1,0,2:T(8,128)(2,1)S(1)} %fusion.11) | copy-start | bytes 6291460
  42.6 27.9 %collective-permute-start.4 = (bf16[4,2,32,2048]{3,2,0,1:T(8,128)(2,1)}, bf16[4,2,32,2048]{3,2,0,1:T(8,128)(2,1)}, u32[]{:S(2)}, u32[]{:S(2)}) collective-permute-start(bf16[4,2,32,2048]{3,2,0,1:T(8,128)(2,1)} %dynamic-slice_bitcast_fusion), channel_id=1, source_target_pairs={{0,2},{1,3},{2,0},{3,1},{4,6},{5,7},{6,4},{7,5},{8,10},{9,11},{10,... | collective-permute-start | bytes 3145736 | tf_op jit(solution)/shard_map/ppermute | solution.py:85
  51.5 2.2 %copy-start.14 = (bf16[1,8192]{1,0:T(2,128)(2,1)S(1)}, bf16[1,8192]{1,0:T(2,128)(2,1)}, u32[]{:S(2)}) copy-start(bf16[1,8192]{1,0:T(2,128)(2,1)} %param.10) | copy-start | bytes 49156
  51.5 40.1 %collective-permute-start.8 = (bf16[4,2,32,2048]{3,2,1,0:T(8,128)(2,1)}, bf16[4,2,32,2048]{3,2,1,0:T(8,128)(2,1)}, u32[]{:S(2)}, u32[]{:S(2)}) collective-permute-start(bf16[4,2,32,2048]{3,2,1,0:T(8,128)(2,1)} %get-tuple-element.9), channel_id=1, source_target_pairs={{0,2},{1,3},{2,0},{3,1},{4,6},{5,7},{6,4},{7,5},{8,10},{9,11},{10,... | collective-permute-start | bytes 3145736 | tf_op jit(solution)/shard_map/ppermute | solution.py:116
  73.4 21.9 %all-to-all-start = ((bf16[4,2,32,2048]{3,2,1,0:T(8,128)(2,1)}), bf16[4,2,32,2048]{3,2,1,0:T(8,128)(2,1)S(1)}, u32[]{:S(2)}, u32[]{:S(2)}) async-start(bf16[4,2,32,2048]{3,2,1,0:T(8,128)(2,1)} %copy.37), calls=%async_computation | async-start | bytes 2097152 | tf_op jit(solution)/shard_map/all_to_all | solution.py:87
  93.3 2.0 %copy-start.2 = (bf16[2,4,2,32,2048]{4,3,2,1,0:T(8,128)(2,1)}, bf16[2,4,2,32,2048]{4,3,2,1,0:T(8,128)(2,1)S(1)}, u32[]{:S(2)}) copy-start(bf16[2,4,2,32,2048]{4,3,2,1,0:T(8,128)(2,1)S(1)} %pad_maximum_fusion) | copy-start | bytes 6291460
  95.3 20.1 %collective-permute-start.9 = (bf16[2,4,2,32,2048]{4,3,2,1,0:T(8,128)(2,1)}, bf16[2,4,2,32,2048]{4,3,2,1,0:T(8,128)(2,1)}, u32[]{:S(2)}, u32[]{:S(2)}) collective-permute-start(bf16[2,4,2,32,2048]{4,3,2,1,0:T(8,128)(2,1)} %reverse_select_fusion), channel_id=1, source_target_pairs={{0,1},{1,0},{2,3},{3,2},{4,5},{5,4},{6,7},{7,6},{8,9},{9,8},{10,11... | collective-permute-start | bytes 6291464 | tf_op jit(solution)/shard_map/ppermute | solution.py:119
  101.9 38.7 %all-to-all-start.1 = ((bf16[16,16,2048]{2,1,0:T(8,128)(2,1)}), bf16[16,16,2048]{2,1,0:T(8,128)(2,1)S(1)}, u32[]{:S(2)}, u32[]{:S(2)}) async-start(bf16[16,16,2048]{2,1,0:T(8,128)(2,1)} %bitcast.16), calls=%async_computation.1 | async-start | bytes 2097152 | tf_op jit(solution)/shard_map/all_to_all | solution.py:31
  112.4 2.5 %copy-start.3 = (bf16[2,4,2,32,2048]{4,3,2,1,0:T(8,128)(2,1)S(1)}, bf16[2,4,2,32,2048]{4,3,2,1,0:T(8,128)(2,1)}, u32[]{:S(2)}) copy-start(bf16[2,4,2,32,2048]{4,3,2,1,0:T(8,128)(2,1)} %copy-done.2) | copy-start | bytes 6291460
  140.6 5.4 %copy-start.9 = (bf16[1,2,128,512]{3,2,1,0:T(8,128)(2,1)S(1)}, bf16[1,2,128,512]{3,2,1,0:T(8,128)(2,1)}, u32[]{:S(2)}) copy-start(bf16[1,2,128,512]{3,2,1,0:T(8,128)(2,1)} %param.8) | copy-start | bytes 786436
  140.6 5.4 %copy-start.11 = (bf16[2,128,512]{2,1,0:T(8,128)(2,1)S(1)}, bf16[2,128,512]{2,1,0:T(8,128)(2,1)}, u32[]{:S(2)}) copy-start(bf16[2,128,512]{2,1,0:T(8,128)(2,1)} %copy-done.10) | copy-start | bytes 786436
  140.6 5.4 %copy-start.13 = (bf16[2,128,512]{2,1,0:T(8,128)(2,1)S(1)}, bf16[2,128,512]{2,1,0:T(8,128)(2,1)}, u32[]{:S(2)}) copy-start(bf16[2,128,512]{2,1,0:T(8,128)(2,1)} %copy-done.12) | copy-start | bytes 786436
  142.2 31.4 %all-to-all-start.2 = ((bf16[16,16,2048]{2,1,0:T(8,128)(2,1)}), bf16[16,16,2048]{2,1,0:T(8,128)(2,1)S(1)}, u32[]{:S(2)}, u32[]{:S(2)}) async-start(bf16[16,16,2048]{2,1,0:T(8,128)(2,1)} %reduce-window_convert_fusion), calls=%async_computation.2 | async-start | bytes 2097152 | tf_op jit(solution)/shard_map/all_to_all | solution.py:34
  173.8 5.0 %copy-start.1 = (bf16[1,2048,512]{2,1,0:T(8,128)(2,1)S(1)}, bf16[1,2048,512]{2,1,0:T(8,128)(2,1)}, u32[]{:S(2)}) copy-start(bf16[1,2048,512]{2,1,0:T(8,128)(2,1)} %param.9) | copy-start | bytes 6291460
  (4 other events, 5.9 us)

commit v10 on v9

--- a/solution.py
+++ b/solution.py
@@ -95,11 +95,13 @@
         hidden_gradient
         - centered4 * jnp.mean(hidden_gradient * centered4, axis=(0, 3), keepdims=True)
     )
-    top4 = top_grad.reshape(mb, tok_dev, n_dp, rows_p).transpose(2, 0, 1, 3)
-    ahead = lax.optimization_barrier(top4.astype(jnp.float32) + branch4)
+
+    def out_layout(v):
+        return v.transpose(1, 2, 0, 3).reshape(mb, tok_dev, d_model)
+
+    ahead = lax.optimization_barrier(top_grad.astype(jnp.float32) + out_layout(branch4))
     later4 = later_sum(branch4)
-    grad4 = (ahead + later4).astype(jnp.bfloat16)
-    grad_in = grad4.transpose(1, 2, 0, 3).reshape(mb, tok_dev, d_model)
+    grad_in = (ahead + out_layout(later4)).astype(jnp.bfloat16)
 
     own_input, own_gain = lax.optimization_barrier((saved_input[0], norm_gain[0]))
     own_float = own_input.astype(jnp.float32)

time: 180 us -> 196 us (1.089)
  the two profiles are of different devices: /device:TPU:4 before, /device:TPU:1 now
where the time goes in v10:
time: 196 us; the launch traced here: 193 us
  waiting for transfers between devices  67.4 us (34%)
  starting transfers between devices  42.6 us (22%)
  other arithmetic  36.9 us (19%)
  matrix products  22 us (11%)
  local copies, waits for them, and re-layouts  21.9 us (11%)
  between operations  2.24 us (1%)
    ppermute x1, waiting for transfers between devices, body(): recv = lax.ppermute(send, 'tensor', [(q, q ^ 2) for q in range(n_t)])  20.5 us
    ppermute x1, waiting for transfers between devices, body(): far = lax.ppermute(mine, 'tensor', [(q, q ^ 2) for q in range(n_t)])  17.5 us
    dot_general x1, matrix products, body(): jnp.einsum('tkmid,mktic->kdc', nrm, cot_sel, preferred_element_type=jnp.f...  16.5 us
    all_to_all x1, waiting for transfers between devices, later_sum(): lax.all_to_all(suffix.astype(jnp.bfloat16), 'section', 0, 0, tiled=True)  12.5 us
    all_to_all x1, starting transfers between devices, later_sum(): got = lax.all_to_all(chunks, 'section', 0, 0, tiled=True)  9.45 us
    all_to_all x1, waiting for transfers between devices, body(): got = lax.all_to_all(total, 'dp', 0, 0, tiled=True)  8.29 us
    all_to_all x1, waiting for transfers between devices, later_sum(): got = lax.all_to_all(chunks, 'section', 0, 0, tiled=True)  7.96 us
    reduce_sum x1, other arithmetic, body(): wsum = jnp.sum(rounded, axis=0)  7.27 us
  transfers between devices with their start and end apart: 13, of which 6 were waited for; matrix products, arithmetic and copies ran while one was open for 36% of the time, Pallas kernels for 0%

profile of v10, /device:TPU:1, one launch (start us, length us, event | category | flops | bytes accessed | tf_op | source)
XLA Modules:
  0.0 193.1 jit_solution(12459329409553244916)
XLA Ops:
  2.8 2.6 %collective-permute-start.1 = (bf16[2,128,512]{2,1,0:T(8,128)(2,1)}, bf16[2,128,512]{2,1,0:T(8,128)(2,1)}, u32[]{:S(2)}, u32[]{:S(2)}) collective-permute-start(bf16[2,128,512]{2,1,0:T(8,128)(2,1)} %bitcast.115), channel_id=1, source_target_pairs={{0,128},{64,192},{128,0},{192,64},{1,129},{65,193},{129,1},{193,65... | collective-permute-start | bytes 786440 | tf_op jit(solution)/shard_map/ppermute | solution.py:61
  8.9 2.5 %fusion.15 = bf16[2,32,8192]{2,1,0:T(8,128)(2,1)} fusion(bf16[2,32,8192]{2,1,0:T(8,128)(2,1)} %bitcast.106, f32[8192]{0:T(1024)S(1)} %convert_element_type.118, f32[2,32]{1,0:T(2,128)S(1)} %add_rsqrt_fusion), kind=kLoop, calls=%fused_computation.28 | loop fusion | flops 2097152 | bytes 2130176 | tf_op jit(solution)/shard_map/convert_element_type | solution.py:109
  13.3 3.3 %constant_dynamic-slice_fusion.3 = (bf16[2,32,1,2048]{3,2,1,0:T(2,128)(2,1)}, bf16[2,32,1,2048]{3,2,1,0:T(2,128)(2,1)}, bf16[2,32,1,2048]{3,2,1,0:T(2,128)(2,1)S(1)}, bf16[2,32,1,2048]{3,2,1,0:T(2,128)(2,1)S(1)}) fusion(bf16[2,32,4,2048]{3,2,1,0:T(4,128)(2,1)S(1)} %reshape.132, s32[]{:T(128)S(6)} %select_n.215, s32[]{:T(128)S(6)} %select_n.221, ...), kind=kLoop, calls=%fused_computation.74 | loop fusion | bytes 2097168 | tf_op jit(solution)/shard_map/jit(dynamic_index_in_dim)/dynamic_slice | solution.py:111
  25.6 2.6 %fusion.12 = bf16[4,2,2,32,2048]{4,3,1,0,2:T(8,128)(2,1)} fusion(bf16[1,2048,512]{2,1,0:T(8,128)(2,1)S(1)} %copy-done, bf16[2,4,2,2,32,512]{5,4,3,2,1,0:T(8,128)(2,1)S(1)} %bitcast.112, s32[]{:T(128)S(6)} %select_n.209), kind=kOutput, calls=%fused_computation.22 | convolution fusion | flops 1074790400 | bytes 4718596 | tf_op jit(solution)/shard_map/mpxik,dk->pxmid/dot_general | solution.py:75
  28.2 3.4 %collective-permute-start.3 = (bf16[4,2,2,32,2048]{4,3,1,0,2:T(8,128)(2,1)}, bf16[4,2,2,32,2048]{4,3,1,0,2:T(8,128)(2,1)}, u32[]{:S(2)}, u32[]{:S(2)}) collective-permute-start(bf16[4,2,2,32,2048]{4,3,1,0,2:T(8,128)(2,1)} %fusion.12), channel_id=1, source_target_pairs={{0,1},{1,0},{2,3},{3,2},{4,5},{5,4},{6,7},{7,6},{8,9},{9,8},{10,11... | collective-permute-start | bytes 6291464 | tf_op jit(solution)/shard_map/ppermute | solution.py:81
  32.3 2.5 %fusion.38 = (bf16[1,4,2,32,2048]{4,3,2,1,0:T(8,128)(2,1)}, bf16[4,2,32,2048]{3,2,1,0:T(8,128)(2,1)}) fusion(bf16[1,2,32,2048]{3,2,1,0:T(8,128)(2,1)S(1)} %bitcast.118, bf16[1,2,32,2048]{3,2,1,0:T(8,128)(2,1)} %bitcast.21, bf16[1,2,32,2048]{3,2,1,0:T(8,128)(2,1)} %bitcast.20, bf16[1,2,32,2048]{3,2,1,0:T(8,128)(2,1)S(1)} %bitcast.111), kind=kLoop, calls=%fused_computation.84 | loop fusion | flops 1572864 | bytes 3145728 | tf_op jit(solution)/shard_map/stack | solution.py:119
  34.8 3.4 %collective-permute-start.8 = (bf16[4,2,32,2048]{3,2,1,0:T(8,128)(2,1)}, bf16[4,2,32,2048]{3,2,1,0:T(8,128)(2,1)}, u32[]{:S(2)}, u32[]{:S(2)}) collective-permute-start(bf16[4,2,32,2048]{3,2,1,0:T(8,128)(2,1)} %get-tuple-element.9), channel_id=1, source_target_pairs={{0,2},{1,3},{2,0},{3,1},{4,6},{5,7},{6,4},{7,5},{8,10},{9,11},{10,... | collective-permute-start | bytes 3145736 | tf_op jit(solution)/shard_map/ppermute | solution.py:118
  38.2 2.7 %reshape.136 = f32[2,32,4,2048]{3,2,1,0:T(4,128)} reshape(bf16[1,2,32,8192]{3,2,1,0:T(8,128)(2,1)S(1)} %copy-done.5) | data formatting | bytes 3145728 | tf_op jit(solution)/shard_map/convert_element_type | solution.py:91
  42.3 17.5 %collective-permute-done.8 = bf16[4,2,32,2048]{3,2,1,0:T(8,128)(2,1)} collective-permute-done((bf16[4,2,32,2048]{3,2,1,0:T(8,128)(2,1)}, bf16[4,2,32,2048]{3,2,1,0:T(8,128)(2,1)}, u32[]{:S(2)}, u32[]{:S(2)}) %collective-permute-start.8) | collective-permute-done | bytes 1048608 | tf_op jit(solution)/shard_map/ppermute | solution.py:118
  63.6 2.8 %collective-permute-start.9 = (bf16[2,4,2,32,2048]{4,3,2,1,0:T(8,128)(2,1)}, bf16[2,4,2,32,2048]{4,3,2,1,0:T(8,128)(2,1)}, u32[]{:S(2)}, u32[]{:S(2)}) collective-permute-start(bf16[2,4,2,32,2048]{4,3,2,1,0:T(8,128)(2,1)} %reverse_select_fusion), channel_id=1, source_target_pairs={{0,1},{1,0},{2,3},{3,2},{4,5},{5,4},{6,7},{7,6},{8,9},{9,8},{10,11... | collective-permute-start | bytes 6291464 | tf_op jit(solution)/shard_map/ppermute | solution.py:121
  66.4 2.9 %fusion.11 = bf16[4,2,2,32,2048]{4,3,1,0,2:T(8,128)(2,1)S(1)} fusion(bf16[4,2,2,32,2048]{4,3,1,0,2:T(8,128)(2,1)} %collective-permute-done.3, bf16[1,2048,512]{2,1,0:T(8,128)(2,1)S(1)} %copy-done, bf16[2,4,2,2,32,512]{5,4,3,2,1,0:T(8,128)(2,1)S(1)} %bitcast.113, s32[]{:T(128)S(6)} %select_n.208), kind=kOutput, calls=%fused_computation.17 | convolution fusion | flops 1078984704 | bytes 6815748 | tf_op jit(solution)/shard_map/mpxik,dk->pxmid/dot_general | solution.py:75
  69.4 3.1 %collective-permute-start.4 = (bf16[4,2,32,2048]{3,2,0,1:T(8,128)(2,1)S(1)}, bf16[4,2,32,2048]{3,2,0,1:T(8,128)(2,1)S(1)}, u32[]{:S(2)}, u32[]{:S(2)}) collective-permute-start(bf16[4,2,32,2048]{3,2,0,1:T(8,128)(2,1)S(1)} %dynamic-slice_bitcast_fusion), channel_id=1, source_target_pairs={{0,2},{1,3},{2,0},{3,1},{4,6},{5,7},{6,4},{7,5},{8,10},{9,11},{10,... | collective-permute-start | bytes 3145736 | tf_op jit(solution)/shard_map/ppermute | solution.py:85
  75.3 20.5 %collective-permute-done.4 = bf16[4,2,32,2048]{3,2,0,1:T(8,128)(2,1)S(1)} collective-permute-done((bf16[4,2,32,2048]{3,2,0,1:T(8,128)(2,1)S(1)}, bf16[4,2,32,2048]{3,2,0,1:T(8,128)(2,1)S(1)}, u32[]{:S(2)}, u32[]{:S(2)}) %collective-permute-start.4) | collective-permute-done | bytes 1048608 | tf_op jit(solution)/shard_map/ppermute | solution.py:85
  97.2 4.6 %all-to-all-start = ((bf16[4,2,32,2048]{3,2,1,0:T(8,128)(2,1)}), bf16[4,2,32,2048]{3,2,1,0:T(8,128)(2,1)S(1)}, u32[]{:S(2)}, u32[]{:S(2)}) async-start(bf16[4,2,32,2048]{3,2,1,0:T(8,128)(2,1)} %copy.36), calls=%async_computation | async-start | bytes 2097152 | tf_op jit(solution)/shard_map/all_to_all | solution.py:87
  102.4 2.9 %fusion.10 = bf16[2,2,4,2,32,2048]{5,4,3,2,0,1:T(8,128)(2,1)S(1)} fusion(bf16[1,2,4,2,32,2048]{5,4,3,2,1,0:T(8,128)(2,1)} %bitcast.26, bf16[1,2,4,2,32,2048]{5,4,3,2,1,0:T(8,128)(2,1)S(1)} %fusion.40, pred[]{:T(512)S(6)} %eq.73), kind=kLoop, calls=%fused_computation.15 | loop fusion | flops 6291456 | bytes 8388609 | tf_op jit(solution)/shard_map/transpose | solution.py:123
  107.5 8.3 %all-to-all-done = bf16[4,2,32,2048]{3,2,1,0:T(8,128)(2,1)S(1)} async-done(((bf16[4,2,32,2048]{3,2,1,0:T(8,128)(2,1)}), bf16[4,2,32,2048]{3,2,1,0:T(8,128)(2,1)S(1)}, u32[]{:S(2)}, u32[]{:S(2)}) %all-to-all-start) | async-done | bytes 1048608 | tf_op jit(solution)/shard_map/all_to_all | solution.py:87
  117.1 3.1 %fusion.31 = (bf16[4,2,32,2048]{3,0,2,1:T(4,128)(2,1)S(1)}, f32[2,32,4,2048]{3,2,1,0:T(4,128)}) fusion(f32[2,32]{1,0:T(2,128)S(1)} %broadcast_multiply_fusion, f32[2,32,4,2048]{3,2,1,0:T(4,128)S(1)} %copy-done.2, f32[2,32]{1,0:T(2,128)S(1)} %add_rsqrt_fusion.1, f32[4,2048]{1,0:T(4,128)S(1)} %reshape.135, bf16[4,2,32,2048]{3,2,1,0:T(8,128)(2,1)S(1)} %all-to-all-done), kind=kLoop, calls=%fused_computation.65 | loop fusion | flops 3670016 | bytes 6324736 | tf_op jit(solution)/shard_map/convert_element_type | solution.py:30
  121.7 9.4 %all-to-all-start.1 = ((bf16[16,16,2048]{2,1,0:T(8,128)(2,1)}), bf16[16,16,2048]{2,1,0:T(8,128)(2,1)S(1)}, u32[]{:S(2)}, u32[]{:S(2)}) async-start(bf16[16,16,2048]{2,1,0:T(8,128)(2,1)} %bitcast.16), calls=%async_computation.1 | async-start | bytes 2097152 | tf_op jit(solution)/shard_map/all_to_all | solution.py:31
  131.2 16.5 %fusion.9 = bf16[4,2048,512]{2,1,0:T(8,128)(2,1)} fusion(s32[4]{0:T(128)S(1)} %fusion.35, s32[2048,512]{1,0:T(8,128)} %add_add_fusion, bf16[4,4,2,32,2048]{4,3,2,1,0:T(8,128)(2,1)} %bitcast.110, bf16[1,2,4,32,512]{4,3,2,1,0:T(8,128)(2,1)} %bitcast.32, bf16[1,2,4,32,512]{4,3,2,1,0:T(8,128)(2,1)} %bitcast.31, bf16[1,2,4,32,512]{4,3,2,1,0:T(8,128)(2,1)} %bitcast.30, ...), kind=kOutput, calls=%fused_computation.13 | convolution fusion | flops 2220359680 | bytes 17825808 | tf_op jit(solution)/shard_map/tkmid,mktic->kdc/dot_general | solution.py:133
  147.7 8.0 %all-to-all-done.1 = bf16[16,16,2048]{2,1,0:T(8,128)(2,1)S(1)} async-done(((bf16[16,16,2048]{2,1,0:T(8,128)(2,1)}), bf16[16,16,2048]{2,1,0:T(8,128)(2,1)S(1)}, u32[]{:S(2)}, u32[]{:S(2)}) %all-to-all-start.1) | async-done | bytes 1048608 | tf_op jit(solution)/shard_map/all_to_all | solution.py:31
  157.3 7.2 %all-to-all-start.2 = ((bf16[16,16,2048]{2,1,0:T(8,128)(2,1)}), bf16[16,16,2048]{2,1,0:T(8,128)(2,1)S(1)}, u32[]{:S(2)}, u32[]{:S(2)}) async-start(bf16[16,16,2048]{2,1,0:T(8,128)(2,1)} %reduce-window_convert_fusion), calls=%async_computation.2 | async-start | bytes 2097152 | tf_op jit(solution)/shard_map/all_to_all | solution.py:34
  164.5 7.3 %convert_reduce_fusion = f32[2048,512]{1,0:T(8,128)} fusion(bf16[4,2048,512]{2,1,0:T(8,128)(2,1)} %fusion.9), kind=kLoop, calls=%fused_computation.12 | loop fusion | flops 7340032 | bytes 12582912 | tf_op jit(solution)/shard_map/reduce_sum | solution.py:135
  174.2 3.4 %convert_add_fusion.1 = f32[2,32,8192]{2,1,0:T(8,128)} fusion(f32[2,32,8192]{2,1,0:T(8,128)} %reshape.128, bf16[2,32,8192]{2,1,0:T(8,128)(2,1)} %param.11), kind=kLoop, calls=%fused_computation.44 | loop fusion | flops 1048576 | bytes 5242880 | tf_op jit(solution)/shard_map/add | solution.py:102
  177.6 12.5 %all-to-all-done.2 = bf16[16,16,2048]{2,1,0:T(8,128)(2,1)S(1)} async-done(((bf16[16,16,2048]{2,1,0:T(8,128)(2,1)}), bf16[16,16,2048]{2,1,0:T(8,128)(2,1)S(1)}, u32[]{:S(2)}, u32[]{:S(2)}) %all-to-all-start.2) | async-done | bytes 1048608 | tf_op jit(solution)/shard_map/all_to_all | solution.py:34
  (75 shorter events, 38.0 us)
Async XLA Ops:
  0.6 25.0 %copy-start = (bf16[1,2048,512]{2,1,0:T(8,128)(2,1)S(1)}, bf16[1,2048,512]{2,1,0:T(8,128)(2,1)}, u32[]{:S(2)}) copy-start(bf16[1,2048,512]{2,1,0:T(8,128)(2,1)} %param.9) | copy-start | bytes 6291460
  0.6 21.0 %collective-permute-start.2 = (bf16[2,128,512]{2,1,0:T(8,128)(2,1)}, bf16[2,128,512]{2,1,0:T(8,128)(2,1)}, u32[]{:S(2)}, u32[]{:S(2)}) collective-permute-start(bf16[2,128,512]{2,1,0:T(8,128)(2,1)} %bitcast.114), channel_id=1, source_target_pairs={{0,64},{64,128},{128,192},{192,0},{1,65},{65,129},{129,193},{193,1... | collective-permute-start | bytes 786440 | tf_op jit(solution)/shard_map/ppermute | solution.py:61
  2.8 20.5 %collective-permute-start.1 = (bf16[2,128,512]{2,1,0:T(8,128)(2,1)}, bf16[2,128,512]{2,1,0:T(8,128)(2,1)}, u32[]{:S(2)}, u32[]{:S(2)}) collective-permute-start(bf16[2,128,512]{2,1,0:T(8,128)(2,1)} %bitcast.115), channel_id=1, source_target_pairs={{0,128},{64,192},{128,0},{192,64},{1,129},{65,193},{129,1},{193,65... | collective-permute-start | bytes 786440 | tf_op jit(solution)/shard_map/ppermute | solution.py:61
  5.5 17.9 %collective-permute-start = (bf16[2,128,512]{2,1,0:T(8,128)(2,1)}, bf16[2,128,512]{2,1,0:T(8,128)(2,1)}, u32[]{:S(2)}, u32[]{:S(2)}) collective-permute-start(bf16[2,128,512]{2,1,0:T(8,128)(2,1)} %bitcast.116), channel_id=1, source_target_pairs={{0,192},{64,0},{128,64},{192,128},{1,193},{65,1},{129,65},{193,129... | collective-permute-start | bytes 786440 | tf_op jit(solution)/shard_map/ppermute | solution.py:61
  16.6 4.8 %copy-start.8 = (bf16[2,32,1,2048]{3,2,1,0:T(2,128)(2,1)S(1)}, bf16[2,32,1,2048]{3,2,1,0:T(2,128)(2,1)}, u32[]{:S(2)}) copy-start(bf16[2,32,1,2048]{3,2,1,0:T(2,128)(2,1)} %get-tuple-element.10) | copy-start | bytes 786436
  16.6 6.7 %copy-start.11 = (bf16[1,2,128,512]{3,2,1,0:T(8,128)(2,1)S(1)}, bf16[1,2,128,512]{3,2,1,0:T(8,128)(2,1)}, u32[]{:S(2)}) copy-start(bf16[1,2,128,512]{3,2,1,0:T(8,128)(2,1)} %param.8) | copy-start | bytes 786436
  17.5 14.1 %collective-permute-start.5 = (bf16[2,32,2048]{2,1,0:T(8,128)(2,1)}, bf16[2,32,2048]{2,1,0:T(8,128)(2,1)}, u32[]{:S(2)}, u32[]{:S(2)}) collective-permute-start(bf16[2,32,2048]{2,1,0:T(8,128)(2,1)} %bitcast.103), channel_id=1, source_target_pairs={{0,64},{64,128},{128,192},{192,0},{1,65},{65,129},{129,193},{193,1... | collective-permute-start | bytes 786440 | tf_op jit(solution)/shard_map/ppermute | solution.py:115
  18.8 12.9 %collective-permute-start.6 = (bf16[2,32,2048]{2,1,0:T(8,128)(2,1)}, bf16[2,32,2048]{2,1,0:T(8,128)(2,1)}, u32[]{:S(2)}, u32[]{:S(2)}) collective-permute-start(bf16[2,32,2048]{2,1,0:T(8,128)(2,1)} %bitcast.102), channel_id=1, source_target_pairs={{0,128},{64,192},{128,0},{192,64},{1,129},{65,193},{129,1},{193,65... | collective-permute-start | bytes 786440 | tf_op jit(solution)/shard_map/ppermute | solution.py:115
  21.6 10.7 %collective-permute-start.7 = (bf16[2,32,2048]{2,1,0:T(8,128)(2,1)}, bf16[2,32,2048]{2,1,0:T(8,128)(2,1)S(1)}, u32[]{:S(2)}, u32[]{:S(2)}) collective-permute-start(bf16[2,32,2048]{2,1,0:T(8,128)(2,1)} %bitcast.101), channel_id=1, source_target_pairs={{0,192},{64,0},{128,64},{192,128},{1,193},{65,1},{129,65},{193,129... | collective-permute-start | bytes 786440 | tf_op jit(solution)/shard_map/ppermute | solution.py:115
  28.2 10.0 %copy-start.5 = (bf16[1,2,32,8192]{3,2,1,0:T(8,128)(2,1)S(1)}, bf16[1,2,32,8192]{3,2,1,0:T(8,128)(2,1)}, u32[]{:S(2)}) copy-start(bf16[1,2,32,8192]{3,2,1,0:T(8,128)(2,1)} %param.7) | copy-start | bytes 3145732
  28.2 38.2 %collective-permute-start.3 = (bf16[4,2,2,32,2048]{4,3,1,0,2:T(8,128)(2,1)}, bf16[4,2,2,32,2048]{4,3,1,0,2:T(8,128)(2,1)}, u32[]{:S(2)}, u32[]{:S(2)}) collective-permute-start(bf16[4,2,2,32,2048]{4,3,1,0,2:T(8,128)(2,1)} %fusion.12), channel_id=1, source_target_pairs={{0,1},{1,0},{2,3},{3,2},{4,5},{5,4},{6,7},{7,6},{8,9},{9,8},{10,11... | collective-permute-start | bytes 6291464 | tf_op jit(solution)/shard_map/ppermute | solution.py:81
  34.8 7.4 %copy-start.13 = (bf16[1,8192]{1,0:T(2,128)(2,1)S(1)}, bf16[1,8192]{1,0:T(2,128)(2,1)}, u32[]{:S(2)}) copy-start(bf16[1,8192]{1,0:T(2,128)(2,1)} %param.10) | copy-start | bytes 49156
  34.8 25.0 %collective-permute-start.8 = (bf16[4,2,32,2048]{3,2,1,0:T(8,128)(2,1)}, bf16[4,2,32,2048]{3,2,1,0:T(8,128)(2,1)}, u32[]{:S(2)}, u32[]{:S(2)}) collective-permute-start(bf16[4,2,32,2048]{3,2,1,0:T(8,128)(2,1)} %get-tuple-element.9), channel_id=1, source_target_pairs={{0,2},{1,3},{2,0},{3,1},{4,6},{5,7},{6,4},{7,5},{8,10},{9,11},{10,... | collective-permute-start | bytes 3145736 | tf_op jit(solution)/shard_map/ppermute | solution.py:118
  61.6 4.9 %copy-start.10 = (bf16[2,512,512]{2,1,0:T(8,128)(2,1)S(1)}, bf16[2,512,512]{2,1,0:T(8,128)(2,1)}, u32[]{:S(2)}) copy-start(bf16[2,512,512]{2,1,0:T(8,128)(2,1)} %copy-done.9) | copy-start | bytes 3145732
  63.6 38.8 %collective-permute-start.9 = (bf16[2,4,2,32,2048]{4,3,2,1,0:T(8,128)(2,1)}, bf16[2,4,2,32,2048]{4,3,2,1,0:T(8,128)(2,1)}, u32[]{:S(2)}, u32[]{:S(2)}) collective-permute-start(bf16[2,4,2,32,2048]{4,3,2,1,0:T(8,128)(2,1)} %reverse_select_fusion), channel_id=1, source_target_pairs={{0,1},{1,0},{2,3},{3,2},{4,5},{5,4},{6,7},{7,6},{8,9},{9,8},{10,11... | collective-permute-start | bytes 6291464 | tf_op jit(solution)/shard_map/ppermute | solution.py:121
  69.4 26.3 %collective-permute-start.4 = (bf16[4,2,32,2048]{3,2,0,1:T(8,128)(2,1)S(1)}, bf16[4,2,32,2048]{3,2,0,1:T(8,128)(2,1)S(1)}, u32[]{:S(2)}, u32[]{:S(2)}) collective-permute-start(bf16[4,2,32,2048]{3,2,0,1:T(8,128)(2,1)S(1)} %dynamic-slice_bitcast_fusion), channel_id=1, source_target_pairs={{0,2},{1,3},{2,0},{3,1},{4,6},{5,7},{6,4},{7,5},{8,10},{9,11},{10,... | collective-permute-start | bytes 3145736 | tf_op jit(solution)/shard_map/ppermute | solution.py:85
  96.2 5.6 %copy-start.4 = (bf16[2,4,2,32,2048]{4,3,2,1,0:T(8,128)(2,1)S(1)}, bf16[2,4,2,32,2048]{4,3,2,1,0:T(8,128)(2,1)}, u32[]{:S(2)}) copy-start(bf16[2,4,2,32,2048]{4,3,2,1,0:T(8,128)(2,1)} %copy-done.3) | copy-start | bytes 6291460
  97.2 18.6 %all-to-all-start = ((bf16[4,2,32,2048]{3,2,1,0:T(8,128)(2,1)}), bf16[4,2,32,2048]{3,2,1,0:T(8,128)(2,1)S(1)}, u32[]{:S(2)}, u32[]{:S(2)}) async-start(bf16[4,2,32,2048]{3,2,1,0:T(8,128)(2,1)} %copy.36), calls=%async_computation | async-start | bytes 2097152 | tf_op jit(solution)/shard_map/all_to_all | solution.py:87
  105.2 10.6 %copy-start.2 = (f32[2,32,4,2048]{3,2,1,0:T(4,128)S(1)}, f32[2,32,4,2048]{3,2,1,0:T(4,128)}, u32[]{:S(2)}) copy-start(f32[2,32,4,2048]{3,2,1,0:T(4,128)} %reshape.136) | copy-start | bytes 6291460
  120.2 11.0 %copy-start.12 = (bf16[1,2,128,512]{3,2,1,0:T(8,128)(2,1)S(1)}, bf16[1,2,128,512]{3,2,1,0:T(8,128)(2,1)}, u32[]{:S(2)}) copy-start(bf16[1,2,128,512]{3,2,1,0:T(8,128)(2,1)} %param.8) | copy-start | bytes 786436
  121.7 33.9 %all-to-all-start.1 = ((bf16[16,16,2048]{2,1,0:T(8,128)(2,1)}), bf16[16,16,2048]{2,1,0:T(8,128)(2,1)S(1)}, u32[]{:S(2)}, u32[]{:S(2)}) async-start(bf16[16,16,2048]{2,1,0:T(8,128)(2,1)} %bitcast.16), calls=%async_computation.1 | async-start | bytes 2097152 | tf_op jit(solution)/shard_map/all_to_all | solution.py:31
  157.3 32.8 %all-to-all-start.2 = ((bf16[16,16,2048]{2,1,0:T(8,128)(2,1)}), bf16[16,16,2048]{2,1,0:T(8,128)(2,1)S(1)}, u32[]{:S(2)}, u32[]{:S(2)}) async-start(bf16[16,16,2048]{2,1,0:T(8,128)(2,1)} %reduce-window_convert_fusion), calls=%async_computation.2 | async-start | bytes 2097152 | tf_op jit(solution)/shard_map/all_to_all | solution.py:34
  164.5 7.3 %copy-start.6 = (f32[2,32,4,2048]{3,2,1,0:T(4,128)S(1)}, f32[2,32,4,2048]{3,2,1,0:T(4,128)}, u32[]{:S(2)}) copy-start(f32[2,32,4,2048]{3,2,1,0:T(4,128)} %get-tuple-element.7) | copy-start | bytes 6291460
  190.5 2.5 %copy-start.1 = (bf16[1,2048,512]{2,1,0:T(8,128)(2,1)S(1)}, bf16[1,2048,512]{2,1,0:T(8,128)(2,1)}, u32[]{:S(2)}) copy-start(bf16[1,2048,512]{2,1,0:T(8,128)(2,1)} %param.9) | copy-start | bytes 6291460
  (3 other events, 4.6 us)

commit v11 on v10

--- a/solution.py
+++ b/solution.py
@@ -79,9 +79,13 @@
     keep = part_for(my_core)
     send = part_for(1 - my_core)
     recv = lax.ppermute(send, "tensor", [(q, q ^ 1) for q in range(n_t)])
-    pair = (keep.astype(jnp.float32) + recv.astype(jnp.float32)).astype(jnp.bfloat16)
-    keep = lax.dynamic_index_in_dim(pair, my_hi, 1, False)
-    send = lax.dynamic_index_in_dim(pair, 1 - my_hi, 1, False)
+
+    def pair_half(hi):
+        a = lax.dynamic_index_in_dim(keep, hi, 1, False).astype(jnp.float32)
+        b = lax.dynamic_index_in_dim(recv, hi, 1, False).astype(jnp.float32)
+        return (a + b).astype(jnp.bfloat16)
+
+    keep, send = pair_half(my_hi), pair_half(1 - my_hi)
     recv = lax.ppermute(send, "tensor", [(q, q ^ 2) for q in range(n_t)])
     total = (keep.astype(jnp.float32) + recv.astype(jnp.float32)).astype(jnp.bfloat16)
     got = lax.all_to_all(total, "dp", 0, 0, tiled=True)

time: 196 us -> 196 us (level)
  other arithmetic: 36.9 us -> 39.5 us
    ppermute x1, waiting for transfers between devices: 17.5 us -> 15 us  [body(): far = lax.ppermute(mine, 'tensor', [(q, q ^ 2) for q in range(n_t)])]
    unnamed x32 -> x28, local copies, waits for them, and re-layouts: 6.38 us -> 5.27 us
  transfers between devices with their start and end apart: 13 -> 13, of which waited for: 6 -> 6; matrix products, arithmetic and copies ran while one was open for 36% -> 37% of each run, Pallas kernels for 0% -> 0%
where the time goes in v11:
time: 196 us; the launch traced here: 193 us
  waiting for transfers between devices  65.9 us (34%)
  starting transfers between devices  42.6 us (22%)
  other arithmetic  39.5 us (20%)
  matrix products  21.6 us (11%)
  local copies, waits for them, and re-layouts  20.7 us (11%)
  between operations  2.23 us (1%)
    ppermute x1, waiting for transfers between devices, body(): recv = lax.ppermute(send, 'tensor', [(q, q ^ 2) for q in range(n_t)])  20.5 us
    dot_general x1, matrix products, body(): jnp.einsum('tkmid,mktic->kdc', nrm, cot_sel, preferred_element_type=jnp.f...  16.5 us
    ppermute x1, waiting for transfers between devices, body(): far = lax.ppermute(mine, 'tensor', [(q, q ^ 2) for q in range(n_t)])  15 us
    all_to_all x1, waiting for transfers between devices, later_sum(): lax.all_to_all(suffix.astype(jnp.bfloat16), 'section', 0, 0, tiled=True)  12.5 us
    all_to_all x1, starting transfers between devices, later_sum(): got = lax.all_to_all(chunks, 'section', 0, 0, tiled=True)  9.43 us
    all_to_all x1, waiting for transfers between devices, body(): got = lax.all_to_all(total, 'dp', 0, 0, tiled=True)  8.41 us
    all_to_all x1, waiting for transfers between devices, later_sum(): got = lax.all_to_all(chunks, 'section', 0, 0, tiled=True)  7.96 us
    reduce_sum x1, other arithmetic, body(): wsum = jnp.sum(rounded, axis=0)  7.27 us
  transfers between devices with their start and end apart: 13, of which 6 were waited for; matrix products, arithmetic and copies ran while one was open for 37% of the time, Pallas kernels for 0%

profile of v11, /device:TPU:1, one launch (start us, length us, event | category | flops | bytes accessed | tf_op | source)
XLA Modules:
  0.0 192.6 jit_solution(3126313614960471788)
XLA Ops:
  2.8 2.6 %collective-permute-start.1 = (bf16[2,128,512]{2,1,0:T(8,128)(2,1)}, bf16[2,128,512]{2,1,0:T(8,128)(2,1)}, u32[]{:S(2)}, u32[]{:S(2)}) collective-permute-start(bf16[2,128,512]{2,1,0:T(8,128)(2,1)} %bitcast.133), channel_id=1, source_target_pairs={{0,128},{64,192},{128,0},{192,64},{1,129},{65,193},{129,1},{193,65... | collective-permute-start | bytes 786440 | tf_op jit(solution)/shard_map/ppermute | solution.py:61
  8.9 2.5 %fusion.14 = bf16[2,32,8192]{2,1,0:T(8,128)(2,1)} fusion(bf16[2,32,8192]{2,1,0:T(8,128)(2,1)} %bitcast.124, f32[8192]{0:T(1024)S(1)} %convert_element_type.143, f32[2,32]{1,0:T(2,128)S(1)} %add_rsqrt_fusion), kind=kLoop, calls=%fused_computation.26 | loop fusion | flops 2097152 | bytes 2130176 | tf_op jit(solution)/shard_map/convert_element_type | solution.py:113
  13.3 3.3 %constant_dynamic-slice_fusion.2 = (bf16[2,32,1,2048]{3,2,1,0:T(2,128)(2,1)}, bf16[2,32,1,2048]{3,2,1,0:T(2,128)(2,1)}, bf16[2,32,1,2048]{3,2,1,0:T(2,128)(2,1)S(1)}, bf16[2,32,1,2048]{3,2,1,0:T(2,128)(2,1)S(1)}) fusion(bf16[2,32,4,2048]{3,2,1,0:T(4,128)(2,1)S(1)} %reshape.140, s32[]{:T(128)S(6)} %select_n.217, s32[]{:T(128)S(6)} %select_n.223, ...), kind=kLoop, calls=%fused_computation.74 | loop fusion | bytes 2097168 | tf_op jit(solution)/shard_map/jit(dynamic_index_in_dim)/dynamic_slice | solution.py:115
  24.7 2.7 %fusion.11 = bf16[4,2,2,32,2048]{4,3,0,2,1:T(8,128)(2,1)} fusion(bf16[1,2048,512]{2,1,0:T(8,128)(2,1)S(1)} %copy-done, bf16[2,4,2,2,32,512]{5,4,3,2,1,0:T(8,128)(2,1)S(1)} %bitcast.130, s32[]{:T(128)S(6)} %select_n.213), kind=kOutput, calls=%fused_computation.20 | convolution fusion | flops 1074790400 | bytes 4718596 | tf_op jit(solution)/shard_map/mpxik,dk->pxmid/dot_general | solution.py:75
  27.3 3.4 %collective-permute-start.3 = (bf16[4,2,2,32,2048]{4,3,0,2,1:T(8,128)(2,1)}, bf16[4,2,2,32,2048]{4,3,0,2,1:T(8,128)(2,1)}, u32[]{:S(2)}, u32[]{:S(2)}) collective-permute-start(bf16[4,2,2,32,2048]{4,3,0,2,1:T(8,128)(2,1)} %fusion.11), channel_id=1, source_target_pairs={{0,1},{1,0},{2,3},{3,2},{4,5},{5,4},{6,7},{7,6},{8,9},{9,8},{10,11... | collective-permute-start | bytes 6291464 | tf_op jit(solution)/shard_map/ppermute | solution.py:81
  32.3 2.5 %fusion.39 = (bf16[1,4,2,32,2048]{4,3,2,1,0:T(8,128)(2,1)}, bf16[4,2,32,2048]{3,2,1,0:T(8,128)(2,1)}) fusion(bf16[1,2,32,2048]{3,2,1,0:T(8,128)(2,1)S(1)} %bitcast.136, bf16[1,2,32,2048]{3,2,1,0:T(8,128)(2,1)} %bitcast.23, bf16[1,2,32,2048]{3,2,1,0:T(8,128)(2,1)} %bitcast.22, bf16[1,2,32,2048]{3,2,1,0:T(8,128)(2,1)S(1)} %bitcast.129), kind=kLoop, calls=%fused_computation.86 | loop fusion | flops 1572864 | bytes 3145728 | tf_op jit(solution)/shard_map/stack | solution.py:123
  34.8 3.4 %collective-permute-start.8 = (bf16[4,2,32,2048]{3,2,1,0:T(8,128)(2,1)}, bf16[4,2,32,2048]{3,2,1,0:T(8,128)(2,1)}, u32[]{:S(2)}, u32[]{:S(2)}) collective-permute-start(bf16[4,2,32,2048]{3,2,1,0:T(8,128)(2,1)} %get-tuple-element.9), channel_id=1, source_target_pairs={{0,2},{1,3},{2,0},{3,1},{4,6},{5,7},{6,4},{7,5},{8,10},{9,11},{10,... | collective-permute-start | bytes 3145736 | tf_op jit(solution)/shard_map/ppermute | solution.py:122
  38.2 2.7 %reshape.144 = f32[2,32,4,2048]{3,2,1,0:T(4,128)} reshape(bf16[1,2,32,8192]{3,2,1,0:T(8,128)(2,1)S(1)} %copy-done.3) | data formatting | bytes 3145728 | tf_op jit(solution)/shard_map/convert_element_type | solution.py:95
  44.8 15.0 %collective-permute-done.8 = bf16[4,2,32,2048]{3,2,1,0:T(8,128)(2,1)} collective-permute-done((bf16[4,2,32,2048]{3,2,1,0:T(8,128)(2,1)}, bf16[4,2,32,2048]{3,2,1,0:T(8,128)(2,1)}, u32[]{:S(2)}, u32[]{:S(2)}) %collective-permute-start.8) | collective-permute-done | bytes 1048608 | tf_op jit(solution)/shard_map/ppermute | solution.py:122
  63.1 2.8 %collective-permute-start.9 = (bf16[2,4,2,32,2048]{4,3,2,1,0:T(8,128)(2,1)}, bf16[2,4,2,32,2048]{4,3,2,1,0:T(8,128)(2,1)}, u32[]{:S(2)}, u32[]{:S(2)}) collective-permute-start(bf16[2,4,2,32,2048]{4,3,2,1,0:T(8,128)(2,1)} %reverse_select_fusion), channel_id=1, source_target_pairs={{0,1},{1,0},{2,3},{3,2},{4,5},{5,4},{6,7},{7,6},{8,9},{9,8},{10,11... | collective-permute-start | bytes 6291464 | tf_op jit(solution)/shard_map/ppermute | solution.py:125
  67.6 3.1 %collective-permute-start.4 = (bf16[4,2,32,2048]{3,2,0,1:T(8,128)(2,1)S(1)}, bf16[4,2,32,2048]{3,2,0,1:T(8,128)(2,1)S(1)}, u32[]{:S(2)}, u32[]{:S(2)}) collective-permute-start(bf16[4,2,32,2048]{3,2,0,1:T(8,128)(2,1)S(1)} %fusion.26), channel_id=1, source_target_pairs={{0,2},{1,3},{2,0},{3,1},{4,6},{5,7},{6,4},{7,5},{8,10},{9,11},{10,... | collective-permute-start | bytes 3145736 | tf_op jit(solution)/shard_map/ppermute | solution.py:89
  73.4 20.5 %collective-permute-done.4 = bf16[4,2,32,2048]{3,2,0,1:T(8,128)(2,1)S(1)} collective-permute-done((bf16[4,2,32,2048]{3,2,0,1:T(8,128)(2,1)S(1)}, bf16[4,2,32,2048]{3,2,0,1:T(8,128)(2,1)S(1)}, u32[]{:S(2)}, u32[]{:S(2)}) %collective-permute-start.4) | collective-permute-done | bytes 1048608 | tf_op jit(solution)/shard_map/ppermute | solution.py:89
  96.7 4.6 %all-to-all-start = ((bf16[4,2,32,2048]{3,2,1,0:T(8,128)(2,1)}), bf16[4,2,32,2048]{3,2,1,0:T(8,128)(2,1)S(1)}, u32[]{:S(2)}, u32[]{:S(2)}) async-start(bf16[4,2,32,2048]{3,2,1,0:T(8,128)(2,1)} %copy.51), calls=%async_computation | async-start | bytes 2097152 | tf_op jit(solution)/shard_map/all_to_all | solution.py:91
  101.8 2.9 %fusion.10 = bf16[2,2,4,2,32,2048]{5,4,3,2,0,1:T(8,128)(2,1)S(1)} fusion(bf16[1,2,4,2,32,2048]{5,4,3,2,1,0:T(8,128)(2,1)} %bitcast.28, bf16[1,2,4,2,32,2048]{5,4,3,2,1,0:T(8,128)(2,1)S(1)} %fusion.41, pred[]{:T(512)S(6)} %eq.73), kind=kLoop, calls=%fused_computation.15 | loop fusion | flops 6291456 | bytes 8388609 | tf_op jit(solution)/shard_map/transpose | solution.py:127
  106.9 8.4 %all-to-all-done = bf16[4,2,32,2048]{3,2,1,0:T(8,128)(2,1)S(1)} async-done(((bf16[4,2,32,2048]{3,2,1,0:T(8,128)(2,1)}), bf16[4,2,32,2048]{3,2,1,0:T(8,128)(2,1)S(1)}, u32[]{:S(2)}, u32[]{:S(2)}) %all-to-all-start) | async-done | bytes 1048608 | tf_op jit(solution)/shard_map/all_to_all | solution.py:91
  116.6 3.1 %fusion.33 = (bf16[4,2,32,2048]{3,0,2,1:T(4,128)(2,1)S(1)}, f32[2,32,4,2048]{3,2,1,0:T(4,128)}) fusion(f32[2,32]{1,0:T(2,128)S(1)} %broadcast_multiply_fusion, f32[2,32,4,2048]{3,2,1,0:T(4,128)S(1)} %copy-done.2, f32[2,32]{1,0:T(2,128)S(1)} %add_rsqrt_fusion.1, f32[4,2048]{1,0:T(4,128)S(1)} %reshape.143, bf16[4,2,32,2048]{3,2,1,0:T(8,128)(2,1)S(1)} %all-to-all-done), kind=kLoop, calls=%fused_computation.68 | loop fusion | flops 3670016 | bytes 6324736 | tf_op jit(solution)/shard_map/convert_element_type | solution.py:30
  121.2 9.4 %all-to-all-start.1 = ((bf16[16,16,2048]{2,1,0:T(8,128)(2,1)}), bf16[16,16,2048]{2,1,0:T(8,128)(2,1)S(1)}, u32[]{:S(2)}, u32[]{:S(2)}) async-start(bf16[16,16,2048]{2,1,0:T(8,128)(2,1)} %bitcast.18), calls=%async_computation.1 | async-start | bytes 2097152 | tf_op jit(solution)/shard_map/all_to_all | solution.py:31
  130.7 16.5 %fusion.9 = bf16[4,2048,512]{2,1,0:T(8,128)(2,1)} fusion(s32[4]{0:T(128)S(1)} %fusion.36, s32[2048,512]{1,0:T(8,128)} %add_add_fusion, bf16[4,4,2,32,2048]{4,3,2,1,0:T(8,128)(2,1)} %bitcast.128, bf16[1,2,4,32,512]{4,3,2,1,0:T(8,128)(2,1)} %bitcast.34, bf16[1,2,4,32,512]{4,3,2,1,0:T(8,128)(2,1)} %bitcast.33, bf16[1,2,4,32,512]{4,3,2,1,0:T(8,128)(2,1)} %bitcast.32, ...), kind=kOutput, calls=%fused_computation.13 | convolution fusion | flops 2220359680 | bytes 17825808 | tf_op jit(solution)/shard_map/tkmid,mktic->kdc/dot_general | solution.py:137
  147.2 8.0 %all-to-all-done.1 = bf16[16,16,2048]{2,1,0:T(8,128)(2,1)S(1)} async-done(((bf16[16,16,2048]{2,1,0:T(8,128)(2,1)}), bf16[16,16,2048]{2,1,0:T(8,128)(2,1)S(1)}, u32[]{:S(2)}, u32[]{:S(2)}) %all-to-all-start.1) | async-done | bytes 1048608 | tf_op jit(solution)/shard_map/all_to_all | solution.py:31
  156.8 7.2 %all-to-all-start.2 = ((bf16[16,16,2048]{2,1,0:T(8,128)(2,1)}), bf16[16,16,2048]{2,1,0:T(8,128)(2,1)S(1)}, u32[]{:S(2)}, u32[]{:S(2)}) async-start(bf16[16,16,2048]{2,1,0:T(8,128)(2,1)} %reduce-window_convert_fusion), calls=%async_computation.2 | async-start | bytes 2097152 | tf_op jit(solution)/shard_map/all_to_all | solution.py:34
  164.0 7.3 %convert_reduce_fusion = f32[2048,512]{1,0:T(8,128)} fusion(bf16[4,2048,512]{2,1,0:T(8,128)(2,1)} %fusion.9), kind=kLoop, calls=%fused_computation.12 | loop fusion | flops 7340032 | bytes 12582912 | tf_op jit(solution)/shard_map/reduce_sum | solution.py:139
  171.2 2.5 %reshape.136 = f32[2,32,8192]{2,1,0:T(8,128)} reshape(f32[2,32,4,2048]{3,2,1,0:T(4,128)S(1)} %copy-done.4) | data formatting | bytes 4194304 | tf_op jit(solution)/shard_map/reshape | solution.py:104
  173.7 3.4 %convert_add_fusion.2 = f32[2,32,8192]{2,1,0:T(8,128)} fusion(f32[2,32,8192]{2,1,0:T(8,128)} %reshape.136, bf16[2,32,8192]{2,1,0:T(8,128)(2,1)} %param.11), kind=kLoop, calls=%fused_computation.46 | loop fusion | flops 1048576 | bytes 5242880 | tf_op jit(solution)/shard_map/add | solution.py:106
  177.1 12.5 %all-to-all-done.2 = bf16[16,16,2048]{2,1,0:T(8,128)(2,1)S(1)} async-done(((bf16[16,16,2048]{2,1,0:T(8,128)(2,1)}), bf16[16,16,2048]{2,1,0:T(8,128)(2,1)S(1)}, u32[]{:S(2)}, u32[]{:S(2)}) %all-to-all-start.2) | async-done | bytes 1048608 | tf_op jit(solution)/shard_map/all_to_all | solution.py:34
  (71 shorter events, 40.3 us)
Async XLA Ops:
  0.6 24.0 %copy-start = (bf16[1,2048,512]{2,1,0:T(8,128)(2,1)S(1)}, bf16[1,2048,512]{2,1,0:T(8,128)(2,1)}, u32[]{:S(2)}) copy-start(bf16[1,2048,512]{2,1,0:T(8,128)(2,1)} %param.9) | copy-start | bytes 6291460
  0.6 21.0 %collective-permute-start.2 = (bf16[2,128,512]{2,1,0:T(8,128)(2,1)}, bf16[2,128,512]{2,1,0:T(8,128)(2,1)}, u32[]{:S(2)}, u32[]{:S(2)}) collective-permute-start(bf16[2,128,512]{2,1,0:T(8,128)(2,1)} %bitcast.132), channel_id=1, source_target_pairs={{0,64},{64,128},{128,192},{192,0},{1,65},{65,129},{129,193},{193,1... | collective-permute-start | bytes 786440 | tf_op jit(solution)/shard_map/ppermute | solution.py:61
  2.8 20.5 %collective-permute-start.1 = (bf16[2,128,512]{2,1,0:T(8,128)(2,1)}, bf16[2,128,512]{2,1,0:T(8,128)(2,1)}, u32[]{:S(2)}, u32[]{:S(2)}) collective-permute-start(bf16[2,128,512]{2,1,0:T(8,128)(2,1)} %bitcast.133), channel_id=1, source_target_pairs={{0,128},{64,192},{128,0},{192,64},{1,129},{65,193},{129,1},{193,65... | collective-permute-start | bytes 786440 | tf_op jit(solution)/shard_map/ppermute | solution.py:61
  5.5 17.9 %collective-permute-start = (bf16[2,128,512]{2,1,0:T(8,128)(2,1)}, bf16[2,128,512]{2,1,0:T(8,128)(2,1)}, u32[]{:S(2)}, u32[]{:S(2)}) collective-permute-start(bf16[2,128,512]{2,1,0:T(8,128)(2,1)} %bitcast.134), channel_id=1, source_target_pairs={{0,192},{64,0},{128,64},{192,128},{1,193},{65,1},{129,65},{193,129... | collective-permute-start | bytes 786440 | tf_op jit(solution)/shard_map/ppermute | solution.py:61
  16.6 4.8 %copy-start.7 = (bf16[2,32,1,2048]{3,2,1,0:T(2,128)(2,1)S(1)}, bf16[2,32,1,2048]{3,2,1,0:T(2,128)(2,1)}, u32[]{:S(2)}) copy-start(bf16[2,32,1,2048]{3,2,1,0:T(2,128)(2,1)} %get-tuple-element.10) | copy-start | bytes 786436
  16.6 6.7 %copy-start.9 = (bf16[1,2,128,512]{3,2,1,0:T(8,128)(2,1)S(1)}, bf16[1,2,128,512]{3,2,1,0:T(8,128)(2,1)}, u32[]{:S(2)}) copy-start(bf16[1,2,128,512]{3,2,1,0:T(8,128)(2,1)} %param.8) | copy-start | bytes 786436
  17.5 13.2 %collective-permute-start.5 = (bf16[2,32,2048]{2,1,0:T(8,128)(2,1)}, bf16[2,32,2048]{2,1,0:T(8,128)(2,1)}, u32[]{:S(2)}, u32[]{:S(2)}) collective-permute-start(bf16[2,32,2048]{2,1,0:T(8,128)(2,1)} %bitcast.121), channel_id=1, source_target_pairs={{0,64},{64,128},{128,192},{192,0},{1,65},{65,129},{129,193},{193,1... | collective-permute-start | bytes 786440 | tf_op jit(solution)/shard_map/ppermute | solution.py:119
  18.8 12.0 %collective-permute-start.6 = (bf16[2,32,2048]{2,1,0:T(8,128)(2,1)}, bf16[2,32,2048]{2,1,0:T(8,128)(2,1)}, u32[]{:S(2)}, u32[]{:S(2)}) collective-permute-start(bf16[2,32,2048]{2,1,0:T(8,128)(2,1)} %bitcast.120), channel_id=1, source_target_pairs={{0,128},{64,192},{128,0},{192,64},{1,129},{65,193},{129,1},{193,65... | collective-permute-start | bytes 786440 | tf_op jit(solution)/shard_map/ppermute | solution.py:119
  21.6 10.7 %collective-permute-start.7 = (bf16[2,32,2048]{2,1,0:T(8,128)(2,1)}, bf16[2,32,2048]{2,1,0:T(8,128)(2,1)S(1)}, u32[]{:S(2)}, u32[]{:S(2)}) collective-permute-start(bf16[2,32,2048]{2,1,0:T(8,128)(2,1)} %bitcast.119), channel_id=1, source_target_pairs={{0,192},{64,0},{128,64},{192,128},{1,193},{65,1},{129,65},{193,129... | collective-permute-start | bytes 786440 | tf_op jit(solution)/shard_map/ppermute | solution.py:119
  24.7 2.7 %copy-start.8 = (bf16[2,512,512]{2,1,0:T(8,128)(2,1)}, bf16[2,512,512]{2,1,0:T(8,128)(2,1)S(1)}, u32[]{:S(2)}) copy-start(bf16[2,512,512]{2,1,0:T(8,128)(2,1)S(1)} %pad_maximum_fusion.1) | copy-start | bytes 3145732
  27.3 10.9 %copy-start.3 = (bf16[1,2,32,8192]{3,2,1,0:T(8,128)(2,1)S(1)}, bf16[1,2,32,8192]{3,2,1,0:T(8,128)(2,1)}, u32[]{:S(2)}) copy-start(bf16[1,2,32,8192]{3,2,1,0:T(8,128)(2,1)} %param.7) | copy-start | bytes 3145732
  27.3 38.6 %collective-permute-start.3 = (bf16[4,2,2,32,2048]{4,3,0,2,1:T(8,128)(2,1)}, bf16[4,2,2,32,2048]{4,3,0,2,1:T(8,128)(2,1)}, u32[]{:S(2)}, u32[]{:S(2)}) collective-permute-start(bf16[4,2,2,32,2048]{4,3,0,2,1:T(8,128)(2,1)} %fusion.11), channel_id=1, source_target_pairs={{0,1},{1,0},{2,3},{3,2},{4,5},{5,4},{6,7},{7,6},{8,9},{9,8},{10,11... | collective-permute-start | bytes 6291464 | tf_op jit(solution)/shard_map/ppermute | solution.py:81
  34.8 7.4 %copy-start.11 = (bf16[1,8192]{1,0:T(2,128)(2,1)S(1)}, bf16[1,8192]{1,0:T(2,128)(2,1)}, u32[]{:S(2)}) copy-start(bf16[1,8192]{1,0:T(2,128)(2,1)} %param.10) | copy-start | bytes 49156
  34.8 25.0 %collective-permute-start.8 = (bf16[4,2,32,2048]{3,2,1,0:T(8,128)(2,1)}, bf16[4,2,32,2048]{3,2,1,0:T(8,128)(2,1)}, u32[]{:S(2)}, u32[]{:S(2)}) collective-permute-start(bf16[4,2,32,2048]{3,2,1,0:T(8,128)(2,1)} %get-tuple-element.9), channel_id=1, source_target_pairs={{0,2},{1,3},{2,0},{3,1},{4,6},{5,7},{6,4},{7,5},{8,10},{9,11},{10,... | collective-permute-start | bytes 3145736 | tf_op jit(solution)/shard_map/ppermute | solution.py:122
  42.3 17.5 %copy-start.6 = (bf16[1,4,2,32,2048]{4,3,2,1,0:T(8,128)(2,1)S(1)}, bf16[1,4,2,32,2048]{4,3,2,1,0:T(8,128)(2,1)}, u32[]{:S(2)}) copy-start(bf16[1,4,2,32,2048]{4,3,2,1,0:T(8,128)(2,1)} %get-tuple-element.8) | copy-start | bytes 3145732
  63.1 38.6 %collective-permute-start.9 = (bf16[2,4,2,32,2048]{4,3,2,1,0:T(8,128)(2,1)}, bf16[2,4,2,32,2048]{4,3,2,1,0:T(8,128)(2,1)}, u32[]{:S(2)}, u32[]{:S(2)}) collective-permute-start(bf16[2,4,2,32,2048]{4,3,2,1,0:T(8,128)(2,1)} %reverse_select_fusion), channel_id=1, source_target_pairs={{0,1},{1,0},{2,3},{3,2},{4,5},{5,4},{6,7},{7,6},{8,9},{9,8},{10,11... | collective-permute-start | bytes 6291464 | tf_op jit(solution)/shard_map/ppermute | solution.py:125
  67.6 26.3 %collective-permute-start.4 = (bf16[4,2,32,2048]{3,2,0,1:T(8,128)(2,1)S(1)}, bf16[4,2,32,2048]{3,2,0,1:T(8,128)(2,1)S(1)}, u32[]{:S(2)}, u32[]{:S(2)}) collective-permute-start(bf16[4,2,32,2048]{3,2,0,1:T(8,128)(2,1)S(1)} %fusion.26), channel_id=1, source_target_pairs={{0,2},{1,3},{2,0},{3,1},{4,6},{5,7},{6,4},{7,5},{8,10},{9,11},{10,... | collective-permute-start | bytes 3145736 | tf_op jit(solution)/shard_map/ppermute | solution.py:89
  96.7 18.6 %all-to-all-start = ((bf16[4,2,32,2048]{3,2,1,0:T(8,128)(2,1)}), bf16[4,2,32,2048]{3,2,1,0:T(8,128)(2,1)S(1)}, u32[]{:S(2)}, u32[]{:S(2)}) async-start(bf16[4,2,32,2048]{3,2,1,0:T(8,128)(2,1)} %copy.51), calls=%async_computation | async-start | bytes 2097152 | tf_op jit(solution)/shard_map/all_to_all | solution.py:91
  104.7 10.7 %copy-start.2 = (f32[2,32,4,2048]{3,2,1,0:T(4,128)S(1)}, f32[2,32,4,2048]{3,2,1,0:T(4,128)}, u32[]{:S(2)}) copy-start(f32[2,32,4,2048]{3,2,1,0:T(4,128)} %reshape.144) | copy-start | bytes 6291460
  119.7 11.0 %copy-start.10 = (bf16[1,2,128,512]{3,2,1,0:T(8,128)(2,1)S(1)}, bf16[1,2,128,512]{3,2,1,0:T(8,128)(2,1)}, u32[]{:S(2)}) copy-start(bf16[1,2,128,512]{3,2,1,0:T(8,128)(2,1)} %param.8) | copy-start | bytes 786436
  121.2 33.9 %all-to-all-start.1 = ((bf16[16,16,2048]{2,1,0:T(8,128)(2,1)}), bf16[16,16,2048]{2,1,0:T(8,128)(2,1)S(1)}, u32[]{:S(2)}, u32[]{:S(2)}) async-start(bf16[16,16,2048]{2,1,0:T(8,128)(2,1)} %bitcast.18), calls=%async_computation.1 | async-start | bytes 2097152 | tf_op jit(solution)/shard_map/all_to_all | solution.py:31
  156.8 32.8 %all-to-all-start.2 = ((bf16[16,16,2048]{2,1,0:T(8,128)(2,1)}), bf16[16,16,2048]{2,1,0:T(8,128)(2,1)S(1)}, u32[]{:S(2)}, u32[]{:S(2)}) async-start(bf16[16,16,2048]{2,1,0:T(8,128)(2,1)} %reduce-window_convert_fusion), calls=%async_computation.2 | async-start | bytes 2097152 | tf_op jit(solution)/shard_map/all_to_all | solution.py:34
  164.0 7.3 %copy-start.4 = (f32[2,32,4,2048]{3,2,1,0:T(4,128)S(1)}, f32[2,32,4,2048]{3,2,1,0:T(4,128)}, u32[]{:S(2)}) copy-start(f32[2,32,4,2048]{3,2,1,0:T(4,128)} %get-tuple-element.7) | copy-start | bytes 6291460
  190.0 2.6 %copy-start.1 = (bf16[1,2048,512]{2,1,0:T(8,128)(2,1)S(1)}, bf16[1,2048,512]{2,1,0:T(8,128)(2,1)}, u32[]{:S(2)}) copy-start(bf16[1,2048,512]{2,1,0:T(8,128)(2,1)} %param.9) | copy-start | bytes 6291460
  (1 other events, 1.6 us)
